TPU v7x, 128 devices: a whole 4x4x4 slice. The times are simulated.
128 devices in a mesh: dp: 16 (over z, y_lo, core), mp: 8 (over x, y_hi).
Axes of the slice: x: 4, y: 4 (y_hi: 2, y_lo: 2; y = y_hi * 2 + y_lo), z: 4, core: 2. Of those that a mesh axis runs over, the one named last changes fastest.
Arguments:
- hidden: bfloat16 [6144, 8192], P('dp', 'mp'), may hold values from -1000 to 1000
- norm_gain: bfloat16 [8192], replicated, may hold values from 0.099609375 to 1.8984375
- query_weight: bfloat16 [8192, 8192], P('dp', 'mp'), may hold values from -0.0625 to 0.0625
- key_weight: bfloat16 [8192, 1024], P('dp', 'mp'), may hold values from -0.0625 to 0.0625
- value_weight: bfloat16 [8192, 1024], P('dp', 'mp'), may hold values from -0.0625 to 0.0625
- query_bias: bfloat16 [8192], P('mp'), may hold values from -3 to 3
- key_bias: bfloat16 [1024], P('mp'), may hold values from -3 to 3
- value_bias: bfloat16 [1024], P('mp'), may hold values from -3 to 3
- request_lens: int32 [3], replicated, may hold values from 1 to 3072, 6144 in all
- request_group: int32 [3], replicated, may hold values from 0 to 3
- prompt_lens: int32 [4], replicated, may hold values from 1 to 512, 1280 in all
- prompt_table: int32 [4, 4], replicated, may hold values from 0 to 15, as said below
- pool_keys: bfloat16 [16, 128, 1024], P('dp', None, 'mp'), may hold values from -1000 to 1000
- pool_values: bfloat16 [16, 128, 1024], P('dp', None, 'mp'), may hold values from -6 to 6
- prev_cache: bfloat16 [256, 4, 2, 128, 1024], P('dp', None, None, None, 'mp'), may hold values from -6 to 6
- dest_device: int32 [256, 1], P('dp'), may hold values from 0 to 15, as said below
Outputs:
- context: bfloat16 [6144, 8192], P('dp', 'mp')
- decode_cache: bfloat16 [256, 4, 2, 128, 1024], P('dp', None, None, None, 'mp')
Inputs may be any that keep to these rules, and one draw needn't show every extreme that they name: `request_lens`: requests are packed back to back in this order and sum to 6144. `prompt_table`: every pool block is named exactly once. `dest_device`: of the 16 blocks of one index of dp at most 2 name the same device, and every device is named by exactly 16 blocks in all.
All inputs are finite; a program needn't handle non-finite values.
Results may differ from a plain program's by a relative error of at most 0.03.
Values may be sent and summed in bfloat16 or wider, within the bound.
No kernel may reach another device: no remote copies, remote signals or barrier semaphores. Data moves between devices by JAX's collectives and lax.ppermute only.
A program may use at most 192 MiB of HBM per device.

v0:
```python
import math

import jax
import jax.numpy as jnp
from jax import lax
from jax.sharding import PartitionSpec as P

HD = 128
CAP = 2


NEG_BIG = -1e30
EPSILON = 1e-06
THETA = 1000000.0


def rotary(values, positions):
    head_dim = values.shape[-1]
    half_dim = head_dim // 2
    frequency = jnp.exp(
        -jnp.arange(half_dim, dtype=jnp.float32) * (2.0 / head_dim) * math.log(THETA)
    )
    angles = positions[:, None] * frequency[None, :]
    cosine = jnp.concatenate([jnp.cos(angles), jnp.cos(angles)], axis=-1)[:, None, :]
    sine_part = jnp.concatenate([jnp.sin(angles), jnp.sin(angles)], axis=-1)[:, None, :]
    first_half = values[..., :half_dim]
    second_half = values[..., half_dim:]
    turned = jnp.concatenate([-second_half, first_half], axis=-1)
    return values * cosine + turned * sine_part


def request_index(rows_here, ends_at):
    return jnp.sum((rows_here[:, None] >= ends_at[None, :]).astype(jnp.int32), axis=1)


def token_table(global_rows, request_lens, request_group, prompt_lens):
    ends_at = jnp.cumsum(request_lens)
    starts_at = ends_at - request_lens
    request_of = request_index(global_rows, ends_at)
    one_hot = request_of[:, None] == jnp.arange(request_lens.shape[0], dtype=jnp.int32)[None, :]
    first_row = jnp.sum(jnp.where(one_hot, starts_at[None, :], 0), axis=1)
    group_of = jnp.sum(jnp.where(one_hot, request_group[None, :], 0), axis=1)
    group_hot = group_of[:, None] == jnp.arange(prompt_lens.shape[0], dtype=jnp.int32)[None, :]
    prefix_of = jnp.sum(jnp.where(group_hot, prompt_lens[None, :], 0), axis=1)
    positions = (prefix_of + global_rows - first_row).astype(jnp.float32)
    return (request_of, group_hot, positions, ends_at)


def prompt_mask(prompt_table, prompt_lens, block_count, block_size):
    blocks = jnp.arange(block_count, dtype=jnp.int32)
    matching = prompt_table[:, :, None] == blocks[None, None, :]
    present = jnp.any(matching, axis=1)
    slot_no = jnp.sum(
        jnp.where(matching, jnp.arange(prompt_table.shape[1], dtype=jnp.int32)[None, :, None], 0),
        axis=1,
    )
    within = (
        slot_no[:, :, None] * block_size + jnp.arange(block_size, dtype=jnp.int32)[None, None, :]
    )
    allowed = present[:, :, None] & (within < prompt_lens[:, None, None])
    return allowed.reshape(prompt_table.shape[0], block_count * block_size)


def attend(current, queries, keys_flat, values_flat, allowed, score_scale):
    best_score, total_sum, accumulated = current
    scores = (
        jnp.einsum("kgqd,skd->kgqs", queries, keys_flat, preferred_element_type=jnp.float32)
        * score_scale
    )
    masked = allowed[None, None, :, :]
    scores = jnp.where(masked, scores, NEG_BIG)
    new_best = jnp.maximum(best_score, jnp.max(scores, axis=-1))
    weights = jnp.where(masked, jnp.exp(scores - new_best[..., None]), 0.0)
    factor = jnp.exp(best_score - new_best)
    total_sum = total_sum * factor + jnp.sum(weights, axis=-1)
    accumulated = accumulated * factor[..., None] + jnp.einsum(
        "kgqs,skd->kgqd",
        weights.astype(jnp.bfloat16),
        values_flat,
        preferred_element_type=jnp.float32,
    )
    return (new_best, total_sum, accumulated)


def relayout(prev_cache, dest_device):
    blocks_here = prev_cache.shape[0]
    devices = lax.axis_size("dp")
    slot_count = devices * CAP
    target = dest_device[:, 0]
    same_target = target[:, None] == target[None, :]
    earlier = (
        jnp.arange(blocks_here, dtype=jnp.int32)[None, :]
        < jnp.arange(blocks_here, dtype=jnp.int32)[:, None]
    )
    block_rank = jnp.sum((same_target & earlier).astype(jnp.int32), axis=1)
    slot_device = jnp.arange(slot_count, dtype=jnp.int32) // CAP
    slot_rank = jnp.arange(slot_count, dtype=jnp.int32) % CAP
    matches = (target[None, :] == slot_device[:, None]) & (
        block_rank[None, :] == slot_rank[:, None]
    )
    filled = jnp.any(matches, axis=1)
    source = jnp.sum(
        jnp.where(matches, jnp.arange(blocks_here, dtype=jnp.int32)[None, :], 0), axis=1
    )
    packed = jnp.take(prev_cache, source, axis=0)
    packed = jnp.where(filled[:, None, None, None, None], packed, jnp.zeros_like(packed))
    slot_flags = filled.astype(jnp.bfloat16)
    arrived, arrived_flags = (
        lax.all_to_all(packed, "dp", split_axis=0, concat_axis=0, tiled=True),
        lax.all_to_all(slot_flags, "dp", split_axis=0, concat_axis=0, tiled=True),
    )
    arrived_live = arrived_flags > 0.5
    order_no = jnp.cumsum(arrived_live.astype(jnp.int32)) - 1
    picked = arrived_live[None, :] & (
        order_no[None, :] == jnp.arange(blocks_here, dtype=jnp.int32)[:, None]
    )
    chosen = jnp.sum(jnp.where(picked, jnp.arange(slot_count, dtype=jnp.int32)[None, :], 0), axis=1)
    return jnp.take(arrived, chosen, axis=0)


def per_device(
    hidden,
    norm_gain,
    query_weight,
    key_weight,
    value_weight,
    query_bias,
    key_bias,
    value_bias,
    request_lens,
    request_group,
    prompt_lens,
    prompt_table,
    pool_keys,
    pool_values,
    prev_cache,
    dest_device,
):
    decode_cache = relayout(prev_cache, dest_device)
    row_count = hidden.shape[0]
    global_rows = lax.axis_index("dp") * row_count + jnp.arange(row_count, dtype=jnp.int32)
    request_of, group_hot, positions, ends_at = token_table(
        global_rows, request_lens, request_group, prompt_lens
    )
    full_rows = lax.all_gather(hidden, "mp", axis=1, tiled=True)
    as_float = full_rows.astype(jnp.float32)
    inverse = lax.rsqrt(jnp.mean(as_float * as_float, axis=1, keepdims=True) + EPSILON)
    normed = (as_float * inverse * norm_gain.astype(jnp.float32)[None, :]).astype(jnp.bfloat16)
    query_full, key_full, value_full = (
        lax.all_gather(query_weight, "dp", axis=0, tiled=True),
        lax.all_gather(key_weight, "dp", axis=0, tiled=True),
        lax.all_gather(value_weight, "dp", axis=0, tiled=True),
    )
    query_proj = jnp.dot(normed, query_full, preferred_element_type=jnp.float32)
    key_proj = jnp.dot(normed, key_full, preferred_element_type=jnp.float32)
    value_proj = jnp.dot(normed, value_full, preferred_element_type=jnp.float32)
    query_proj = query_proj + query_bias.astype(jnp.float32)[None, :]
    key_proj = key_proj + key_bias.astype(jnp.float32)[None, :]
    value_proj = value_proj + value_bias.astype(jnp.float32)[None, :]
    local_heads = query_proj.shape[1] // HD
    local_kv = key_proj.shape[1] // HD
    group_size = local_heads // local_kv
    queries = rotary(query_proj.reshape(row_count, local_heads, HD), positions).astype(jnp.bfloat16)
    queries = queries.reshape(row_count, local_kv, group_size, HD).transpose(1, 2, 0, 3)
    keys_new = (
        rotary(key_proj.reshape(row_count, local_kv, HD), positions)
        .astype(jnp.bfloat16)
        .reshape(row_count, local_kv * HD)
    )
    values_new = value_proj.astype(jnp.bfloat16)
    score_scale = HD ** (-0.5)
    carried = (
        jnp.full((local_kv, group_size, row_count), NEG_BIG, jnp.float32),
        jnp.zeros((local_kv, group_size, row_count), jnp.float32),
        jnp.zeros((local_kv, group_size, row_count, HD), jnp.float32),
    )
    block_size = pool_keys.shape[1]

    def unchanged(previous):
        return previous

    keys_part = lax.all_gather(pool_keys, "dp", axis=0, tiled=True)
    values_part = lax.all_gather(pool_values, "dp", axis=0, tiled=True)
    blocks_here = keys_part.shape[0]
    allowed_group = prompt_mask(prompt_table, prompt_lens, blocks_here, block_size)
    allowed = jnp.any(group_hot[:, :, None] & allowed_group[None, :, :], axis=1)
    keys_flat = keys_part.reshape(blocks_here * block_size, local_kv, HD)
    values_flat = values_part.reshape(blocks_here * block_size, local_kv, HD)

    def prompt_update(previous):
        return attend(previous, queries, keys_flat, values_flat, allowed, score_scale)

    carried = lax.cond(jnp.any(allowed), prompt_update, unchanged, carried)
    keys_part = lax.all_gather(keys_new, "dp", axis=0, tiled=True)
    values_part = lax.all_gather(values_new, "dp", axis=0, tiled=True)
    key_count = keys_part.shape[0]
    key_rows = jnp.arange(key_count, dtype=jnp.int32)
    key_request = request_index(key_rows, ends_at)
    span_allowed = (request_of[:, None] == key_request[None, :]) & (
        key_rows[None, :] <= global_rows[:, None]
    )
    span_keys_flat = keys_part.reshape(key_count, local_kv, HD)
    span_values_flat = values_part.reshape(key_count, local_kv, HD)

    def span_update(previous):
        return attend(
            previous, queries, span_keys_flat, span_values_flat, span_allowed, score_scale
        )

    carried = lax.cond(jnp.any(span_allowed), span_update, unchanged, carried)
    best_score, total_sum, accumulated = carried
    output = accumulated / total_sum[..., None]
    context = output.transpose(2, 0, 1, 3).reshape(row_count, local_heads * HD).astype(jnp.bfloat16)
    return (context, decode_cache)


def solution(mesh):
    return jax.shard_map(
        per_device,
        mesh=mesh,
        in_specs=(
            P("dp", "mp"),
            P(),
            P("dp", "mp"),
            P("dp", "mp"),
            P("dp", "mp"),
            P("mp"),
            P("mp"),
            P("mp"),
            P(),
            P(),
            P(),
            P(),
            P("dp", None, "mp"),
            P("dp", None, "mp"),
            P("dp", None, None, None, "mp"),
            P("dp", None),
        ),
        out_specs=(P("dp", "mp"), P("dp", None, None, None, "mp")),
        check_vma=False,
    )
```

profile of v0, /device:TPU:1, one launch (start us, length us, event | category | flops | bytes accessed | tf_op | source)
XLA Modules:
  0.0 482.7 jit_solution(6875735980011285791)
XLA Ops:
  7.2 0.7 all-gather.7.cloned.1.call-update
  7.9 0.7 all-gather.11.cloned.1.call-update
  8.6 0.0 all-gather.15.cloned.1.call-start
  8.7 0.7 all-gather.15.cloned.1.call-update
  9.4 0.5 all-gather.9.cloned.1.call-update
  10.0 0.9 convert_reduce_fusion.1
  10.9 0.7 fusion.52
  11.6 0.7 reshape.453
  12.3 7.8 %all-to-all-start = ((bf16[16,2,1]{1,2,0:T(2,128)(2,1)}), bf16[16,2,1]{1,2,0:T(2,128)(2,1)S(1)}, u32[]{:S(2)}, u32[]{:S(2)}) async-start(bf16[16,2,1]{1,2,0:T(2,128)(2,1)} %reshape.453), calls=%async_computation | async-start | bytes 16384 | tf_op jit(solution)/shard_map/all_to_all | solution.py:110
  20.2 0.8 reduce-window.16
  21.0 0.7 select_reduce_fusion.1
  21.8 7.4 %gather_fusion = bf16[32,4,2,128,128]{4,3,2,1,0:T(8,128)(2,1)} fusion(bf16[16,4,2,128,128]{4,3,2,1,0:T(8,128)(2,1)} %param.34, s32[1024]{0:T(1024)S(1)} %pad_clamp_fusion.1), kind=kCustom, calls=%fused_computation | custom fusion | bytes 16777344 | tf_op jit(solution)/shard_map/jit(_take)/gather | solution.py:105
  29.2 0.1 convert_reduce_fusion.2
  29.3 0.1 convert_reduce_fusion
  29.4 7.6 %select_select_fusion = bf16[32,4,2,128,128]{4,3,2,1,0:T(8,128)(2,1)} fusion(bf16[32,4,2,128,128]{4,3,2,1,0:T(8,128)(2,1)} %gather_fusion, pred[32]{0:T(512)(128)(4,1)S(1)} %compare_and_fusion.1, pred[32]{0:T(512)(128)(4,1)S(1)} %fusion.52), kind=kLoop, calls=%fused_computation.46 | loop fusion | flops 8388608 | bytes 16777280 | tf_op jit(solution)/shard_map/jit(_where)/select_n | solution.py:106
  37.1 5.8 %all-to-all-start.1 = ((bf16[32,4,2,128,128]{4,3,2,1,0:T(8,128)(2,1)}), bf16[32,4,2,128,128]{4,3,2,1,0:T(8,128)(2,1)}, u32[]{:S(2)}, u32[]{:S(2)}) async-start(bf16[32,4,2,128,128]{4,3,2,1,0:T(8,128)(2,1)} %select_select_fusion), calls=%async_computation.1 | async-start | bytes 16777216 | tf_op jit(solution)/shard_map/all_to_all | solution.py:109
  42.9 5.0 %fusion.36 = (pred[384,6144]{1,0:T(8,128)(4,1)}, pred[]{:T(512)}) fusion(s32[384]{0:T(512)S(1)} %iota_add_fusion, s32[6144]{0:T(1024)S(1)} %convert_reduce_fusion, s32[384]{0:T(512)S(1)} %convert_reduce_fusion.2), kind=kLoop, calls=%fused_computation.45 | loop fusion | flops 9437183 | bytes 2386945 | tf_op jit(solution)/shard_map/and | solution.py:199
  48.7 0.1 select_reduce_fusion.3
  48.7 0.1 fusion.49
  48.9 0.1 select_reduce_fusion.4
  49.0 0.2 select_reduce_fusion
  49.2 0.1 broadcast_bitcast_fusion.1
  49.3 0.1 broadcast_bitcast_fusion
  49.4 0.1 iota_compare_fusion.1
  49.5 0.4 multiply_cosine_fusion
  49.9 0.1 fusion.47
  50.0 86.1 %all-gather.7.cloned.1.call-done = bf16[384,8192]{1,0:T(8,128)(2,1)} async-done(((bf16[384,1024]{1,0:T(8,128)(2,1)}), bf16[384,8192]{1,0:T(8,128)(2,1)}) %all-gather.7.cloned.1.call-update) | async-done | bytes 6291472 | tf_op jit(solution)/shard_map/all_gather | solution.py:145
  136.1 4.1 fusion.33
  140.2 42.0 %all-gather.11.cloned.1.call-done = bf16[8192,128]{1,0:T(8,128)(2,1)} async-done(((bf16[512,128]{1,0:T(8,128)(2,1)}), bf16[8192,128]{1,0:T(8,128)(2,1)}) %all-gather.11.cloned.1.call-update) | async-done | bytes 2097168 | tf_op jit(solution)/shard_map/all_gather | solution.py:151
  182.2 5.7 %convolution_add_fusion.1 = f32[384,128]{0,1:T(8,128)S(1)} fusion(bf16[8192,128]{1,0:T(8,128)(2,1)} %all-gather.11.cloned.1.call-done, f32[128]{0:T(128)S(1)} %convert_element_type.112, bf16[384,8192]{1,0:T(8,128)(2,1)} %all-gather.7.cloned.1.call-done, f32[8192]{0:T(1024)S(1)} %convert_element_type.107, f32[384]{0:T(512)S(1)} %add_rsqrt_fusion), kind=kOutput, calls=%fused_computation.59 | convolution fusion | flops 817938432 | bytes 8620032 | tf_op jit(solution)/shard_map/dot_general | solution.py:155
  188.0 0.8 fusion.44
  188.8 0.0 all-gather.17.cloned.1.call-start
  188.8 7.6 %fusion.60 = (pred[]{:T(512)}, pred[384,4,2048]{2,1,0:T(4,128)(4,1)S(1)}) fusion(pred[4,2048]{1,0:T(4,128)(4,1)S(1)} %fusion.47, pred[384,4]{1,0:T(8,128)(4,1)S(1)} %iota_compare_fusion.1), kind=kLoop, calls=%fused_computation.126 | loop fusion | flops 6291455 | bytes 3155457 | tf_op jit(solution)/shard_map/reduce_or | solution.py:193
  197.1 24.4 %all_gather.26 = bf16[16,128,128]{2,1,0:T(8,128)(2,1)} all-gather(bf16[1,128,128]{2,1,0:T(8,128)(2,1)S(1)} %copy-done.3), channel_id=1, replica_groups=mesh['dp'=16,'mp'=8] {'dp'}, dimensions={0}, use_global_device_ids=true | all-gather | bytes 557056 | tf_op jit(solution)/shard_map/all_gather | solution.py:182
  221.5 22.5 %all_gather.27 = bf16[16,128,128]{2,1,0:T(8,128)(2,1)} all-gather(bf16[1,128,128]{2,1,0:T(8,128)(2,1)S(1)} %copy-done.4), channel_id=1, replica_groups=mesh['dp'=16,'mp'=8] {'dp'}, dimensions={0}, use_global_device_ids=true | all-gather | bytes 557056 | tf_op jit(solution)/shard_map/all_gather | solution.py:183
  244.0 0.1 reshape.454
  244.1 0.1 reduce-window.17
  244.2 0.1 gt.25
  244.3 0.1 add_reduce_fusion
  244.4 0.1 select_reduce_fusion.2
  244.6 6.6 %gather_fusion.1 = bf16[16,4,2,128,128]{4,3,2,1,0:T(8,128)(2,1)} fusion(bf16[32,4,2,128,128]{4,3,2,1,0:T(8,128)(2,1)} %all-to-all-done.1, s32[1024]{0:T(1024)S(1)} %pad_clamp_fusion), kind=kCustom, calls=%fused_computation.1 | custom fusion | bytes 8388672 | tf_op jit(solution)/shard_map/jit(_take)/gather | solution.py:118
  251.2 6.1 %fusion.40 = bf16[384,128]{1,0:T(8,128)(2,1)} fusion(bf16[8192,128]{1,0:T(8,128)(2,1)} %all-gather.15.cloned.1.call-done, f32[128]{0:T(128)S(1)} %convert_element_type.114, bf16[384,8192]{1,0:T(8,128)(2,1)} %all-gather.7.cloned.1.call-done, f32[8192]{0:T(1024)S(1)} %convert_element_type.107, f32[384]{0:T(512)S(1)} %add_rsqrt_fusion), kind=kOutput, calls=%fused_computation.60 | convolution fusion | flops 817987584 | bytes 8521728 | tf_op jit(solution)/shard_map/dot_general | solution.py:156
  257.4 4.8 broadcast_select_fusion
  262.1 0.1 copy.47
  262.2 1.1 copy.43
  263.3 51.1 %all-gather.9.cloned.1.call-done = bf16[8192,1024]{1,0:T(8,128)(2,1)} async-done(((bf16[512,1024]{1,0:T(8,128)(2,1)}), bf16[8192,1024]{1,0:T(8,128)(2,1)}) %all-gather.9.cloned.1.call-update) | async-done | bytes 16777232 | tf_op jit(solution)/shard_map/all_gather | solution.py:150
  314.4 12.2 %add_bitcast_fusion.1 = f32[48,8,8,128]{3,1,2,0:T(8,128)S(1)} fusion(bf16[8192,1024]{1,0:T(8,128)(2,1)} %all-gather.9.cloned.1.call-done, f32[1024]{0:T(1024)S(1)} %convert_element_type.109, bf16[384,8192]{1,0:T(8,128)(2,1)} %all-gather.7.cloned.1.call-done, f32[8192]{0:T(1024)} %copy-done.5, f32[384]{0:T(512)S(1)} %add_rsqrt_fusion), kind=kOutput, calls=%fused_computation.57 | convolution fusion | flops 6455427072 | bytes 24679936 | tf_op jit(solution)/shard_map/dot_general | solution.py:154
  326.7 0.3 copy.58
  327.0 0.5 fusion.61
  327.5 0.7 copy_bitcast_fusion
  328.2 1.6 fusion.41
  329.8 50.4 %conditional.2 = (f32[1,8,384]{2,1,0:T(8,128)S(1)}, f32[1,8,384]{2,1,0:T(8,128)S(1)}, f32[1,8,384,128]{3,2,1,0:T(8,128)}) conditional(s32[]{:T(128)} %convert_element_type.105, () %tuple.23, (pred[384,4,2048]{2,1,0:T(4,128)(4,1)S(1)}, bf16[1,8,384,128]{3,2,1,0:T(8,128)(2,1)}, bf16[16,128,128]{2,1,0:T(8,128)(2,1)}, ...), branch_computations={%region_11.12_spmd, %region_12.16_spmd} | conditional | flops 3305782272 | bytes 90587216 | solution.py:193
  330.0 10.3 %reduce_or.41 = pred[384,2048]{1,0:T(8,128)(4,1)} reduce(pred[384,4,2048]{2,1,0:T(4,128)(4,1)S(1)} %get-tuple-element.32, pred[]{:T(512)} %constant.64.clone), dimensions={1}, to_apply=%region_13.13 | reduce | flops 2359296 | bytes 3932161 | tf_op jit(solution)/shard_map/reduce_or | solution.py:186
  340.2 14.9 %fusion = (f32[8,384]{1,0:T(8,128)S(1)}, f32[8,384,2048]{2,1,0:T(8,128)}) fusion(pred[384,2048]{1,0:T(8,128)(4,1)} %reduce_or.41, bf16[2048,128,1]{1,0,2:T(8,128)(2,1)} %bitcast.112, bf16[1,8,384,128]{3,2,1,0:T(8,128)(2,1)} %get-tuple-element.33), kind=kOutput, calls=%fused_computation.4 | convolution fusion | flops 1629484032 | bytes 27275264 | tf_op jit(solution)/shard_map/cond/branch_1_fun/kgqd,skd->kgqs/dot_general | solution.py:67
  355.2 12.1 %fusion.2 = f32[8,384]{1,0:T(8,128)S(1)} fusion(f32[8,384,2048]{2,1,0:T(8,128)} %get-tuple-element.96, f32[8,384]{1,0:T(8,128)S(1)} %get-tuple-element.94, pred[384,2048]{1,0:T(8,128)(4,1)S(1)} %copy-done), kind=kLoop, calls=%fused_computation.6 | loop fusion | flops 31454208 | bytes 25976832 | tf_op jit(solution)/shard_map/cond/branch_1_fun/reduce_sum | solution.py:75
  367.3 12.7 %add_bitcast_fusion = f32[1,8,384,128]{3,2,1,0:T(8,128)} fusion(bf16[2048,128,1]{1,0,2:T(8,128)(2,1)S(1)} %bitcast.115, f32[8,384,2048]{2,1,0:T(8,128)} %get-tuple-element.96, f32[8,384]{1,0:T(8,128)S(1)} %get-tuple-element.94, pred[384,2048]{1,0:T(8,128)(4,1)S(1)} %copy-done, f32[8,384]{1,0:T(8,128)S(1)} %get-tuple-element.93), kind=kOutput, calls=%fused_computation.9 | convolution fusion | flops 1642463232 | bytes 28073984 | tf_op jit(solution)/shard_map/cond/branch_1_fun/kgqs,skd->kgqd/dot_general | solution.py:76
  380.2 4.5 all-gather.17.cloned.1.call-done
  384.7 87.5 %conditional.3 = ((f32[1,8,384]{2,1,0:T(8,128)S(1)}, f32[1,8,384,128]{3,2,1,0:T(8,128)})) conditional(s32[]{:T(128)} %convert_element_type.104, (f32[1,8,384]{2,1,0:T(8,128)S(1)}, f32[1,8,384,128]{3,2,1,0:T(8,128)}) %tuple.25, (pred[384,6144]{1,0:T(8,128)(4,1)}, bf16[1,8,384,128]{3,2,1,0:T(8,128)(2,1)}, bf16[6144,128]{0,1:T(8,128)(2,1)}, ...), branch_computations={%region_16.17_spmd, %region_17.20_spmd} | conditional | flops 9909841920 | bytes 250257472 | solution.py:210
  384.7 30.4 %fusion.14 = (f32[8,384]{1,0:T(8,128)S(1)}, f32[8,384,6144]{2,1,0:T(8,128)}) fusion(pred[384,6144]{1,0:T(8,128)(4,1)} %get-tuple-element.38, bf16[6144,128]{0,1:T(8,128)(2,1)} %get-tuple-element.78, bf16[1,8,384,128]{3,2,1,0:T(8,128)(2,1)} %get-tuple-element.39), kind=kOutput, calls=%fused_computation.21 | convolution fusion | flops 4888458240 | bytes 80228352 | tf_op jit(solution)/shard_map/cond/branch_1_fun/kgqd,skd->kgqs/dot_general | solution.py:67
  415.2 27.0 %fusion.16 = f32[8,384]{1,0:T(8,128)S(1)} fusion(f32[8,384,6144]{2,1,0:T(8,128)} %get-tuple-element.92, f32[8,384]{1,0:T(8,128)S(1)} %get-tuple-element.90, pred[384,6144]{1,0:T(8,128)(4,1)S(1)} %copy-done.1), kind=kLoop, calls=%fused_computation.23 | loop fusion | flops 94368768 | bytes 77881344 | tf_op jit(solution)/shard_map/cond/branch_1_fun/reduce_sum | solution.py:75
  442.2 30.0 %bitcast_add_fusion.1 = f32[1,8,384,128]{3,2,1,0:T(8,128)} fusion(bf16[6144,128]{1,0:T(8,128)(2,1)} %get-tuple-element.42, f32[8,384,6144]{2,1,0:T(8,128)} %get-tuple-element.92, f32[8,384]{1,0:T(8,128)S(1)} %get-tuple-element.90, pred[384,6144]{1,0:T(8,128)(4,1)S(1)} %copy-done.1, f32[1,8,384,128]{3,2,1,0:T(8,128)} %get-tuple-element.41, ...), kind=kOutput, calls=%fused_computation.26 | convolution fusion | flops 4926996480 | bytes 82599936 | tf_op jit(solution)/shard_map/cond/branch_1_fun/kgqs,skd->kgqd/dot_general | solution.py:76
  472.2 1.9 fusion.42
  474.1 0.5 copy.49
  474.6 1.1 copy.75
  (64 shorter events, 0.5 us)
Async XLA Ops:
  7.2 128.9 %all-gather.7.cloned.1.call-start = ((), (), s32[]{:S(2)}) async-start(), calls=%async_computation.2 | async-start | bytes 7077888 | tf_op jit(solution)/shard_map/all_gather | solution.py:145
  7.9 174.3 %all-gather.11.cloned.1.call-start = ((), (), s32[]{:S(2)}) async-start(), calls=%async_computation.4 | async-start | bytes 2228224 | tf_op jit(solution)/shard_map/all_gather | solution.py:151
  8.6 242.6 %all-gather.15.cloned.1.call-start = ((), (), s32[]{:S(2)}) async-start(), calls=%async_computation.6 | async-start | bytes 2228224 | tf_op jit(solution)/shard_map/all_gather | solution.py:152
  9.4 305.0 %all-gather.9.cloned.1.call-start = ((), (), s32[]{:S(2)}) async-start(), calls=%async_computation.3 | async-start | bytes 17825792 | tf_op jit(solution)/shard_map/all_gather | solution.py:150
  12.3 24.7 %all-to-all-start = ((bf16[16,2,1]{1,2,0:T(2,128)(2,1)}), bf16[16,2,1]{1,2,0:T(2,128)(2,1)S(1)}, u32[]{:S(2)}, u32[]{:S(2)}) async-start(bf16[16,2,1]{1,2,0:T(2,128)(2,1)} %reshape.453), calls=%async_computation | async-start | bytes 16384 | tf_op jit(solution)/shard_map/all_to_all | solution.py:110
  37.0 11.5 %copy-start.6 = (bf16[8192]{0:T(1024)(128)(2,1)S(1)}, bf16[8192]{0:T(1024)(128)(2,1)}, u32[]{:S(2)}) copy-start(bf16[8192]{0:T(1024)(128)(2,1)} %param.21) | copy-start | bytes 49156
  37.0 11.6 %copy-start.11 = (bf16[128]{0:T(256)(128)(2,1)S(1)}, bf16[128]{0:T(256)(128)(2,1)}, u32[]{:S(2)}) copy-start(bf16[128]{0:T(256)(128)(2,1)} %param.26) | copy-start | bytes 772
  37.0 11.6 %copy-start.7 = (s32[4,4]{1,0:T(4,128)S(1)}, s32[4,4]{1,0:T(4,128)}, u32[]{:S(2)}) copy-start(s32[4,4]{1,0:T(4,128)} %param.31) | copy-start | bytes 196
  37.0 11.8 %copy-start.12 = (s32[3]{0:T(128)S(1)}, s32[3]{0:T(128)}, u32[]{:S(2)}) copy-start(s32[3]{0:T(128)} %param.28) | copy-start | bytes 40
  37.0 11.8 %copy-start.10 = (s32[3]{0:T(128)S(1)}, s32[3]{0:T(128)}, u32[]{:S(2)}) copy-start(s32[3]{0:T(128)} %param.29) | copy-start | bytes 40
  37.0 11.9 %copy-start.8 = (s32[4]{0:T(128)S(1)}, s32[4]{0:T(128)}, u32[]{:S(2)}) copy-start(s32[4]{0:T(128)} %param.30) | copy-start | bytes 52
  37.1 207.5 %all-to-all-start.1 = ((bf16[32,4,2,128,128]{4,3,2,1,0:T(8,128)(2,1)}), bf16[32,4,2,128,128]{4,3,2,1,0:T(8,128)(2,1)}, u32[]{:S(2)}, u32[]{:S(2)}) async-start(bf16[32,4,2,128,128]{4,3,2,1,0:T(8,128)(2,1)} %select_select_fusion), calls=%async_computation.1 | async-start | bytes 16777216 | tf_op jit(solution)/shard_map/all_to_all | solution.py:109
  42.9 337.3 %all-gather.13.cloned.1.call-start = ((), (), s32[]{:S(2)}) async-start(), calls=%async_computation.5 | async-start | bytes 1671168 | tf_op jit(solution)/shard_map/all_gather | solution.py:194
  48.6 202.6 %copy-start.5 = (f32[8192]{0:T(1024)}, f32[8192]{0:T(1024)S(1)}, u32[]{:S(2)}) copy-start(f32[8192]{0:T(1024)S(1)} %convert_element_type.107) | copy-start | bytes 98308
  140.2 56.9 %copy-start.9 = (bf16[1024]{0:T(1024)(128)(2,1)S(1)}, bf16[1024]{0:T(1024)(128)(2,1)}, u32[]{:S(2)}) copy-start(bf16[1024]{0:T(1024)(128)(2,1)} %param.25) | copy-start | bytes 6148
  140.2 56.9 %copy-start.13 = (bf16[128]{0:T(256)(128)(2,1)S(1)}, bf16[128]{0:T(256)(128)(2,1)}, u32[]{:S(2)}) copy-start(bf16[128]{0:T(256)(128)(2,1)} %param.27) | copy-start | bytes 772
  140.2 56.9 %copy-start.3 = (bf16[1,128,128]{2,1,0:T(8,128)(2,1)S(1)}, bf16[1,128,128]{2,1,0:T(8,128)(2,1)}, u32[]{:S(2)}) copy-start(bf16[1,128,128]{2,1,0:T(8,128)(2,1)} %param.32) | copy-start | bytes 98308
  140.2 81.3 %copy-start.4 = (bf16[1,128,128]{2,1,0:T(8,128)(2,1)S(1)}, bf16[1,128,128]{2,1,0:T(8,128)(2,1)}, u32[]{:S(2)}) copy-start(bf16[1,128,128]{2,1,0:T(8,128)(2,1)} %param.33) | copy-start | bytes 98308
  188.8 196.0 %all-gather.17.cloned.1.call-start = ((), (), s32[]{:S(2)}) async-start(), calls=%async_computation.7 | async-start | bytes 1671168 | tf_op jit(solution)/shard_map/all_gather | solution.py:195
  340.2 14.9 %copy-start = (pred[384,2048]{1,0:T(8,128)(4,1)S(1)}, pred[384,2048]{1,0:T(8,128)(4,1)}, u32[]{:S(2)}) copy-start(pred[384,2048]{1,0:T(8,128)(4,1)} %reduce_or.41) | copy-start | bytes 2359300 | tf_op jit(solution)/shard_map/cond
  355.2 12.1 %copy-start.2 = (bf16[16,128,128]{2,1,0:T(8,128)(2,1)S(1)}, bf16[16,128,128]{2,1,0:T(8,128)(2,1)}, u32[]{:S(2)}) copy-start(bf16[16,128,128]{2,1,0:T(8,128)(2,1)} %get-tuple-element.35) | copy-start | bytes 1572868 | tf_op jit(solution)/shard_map/cond
  384.7 30.4 %copy-start.1 = (pred[384,6144]{1,0:T(8,128)(4,1)S(1)}, pred[384,6144]{1,0:T(8,128)(4,1)}, u32[]{:S(2)}) copy-start(pred[384,6144]{1,0:T(8,128)(4,1)} %get-tuple-element.38) | copy-start | bytes 7077892 | tf_op jit(solution)/shard_map/cond
Sparse Core Ops, SparseCore 0:
  10.3 125.7 all-gather.6
  137.8 44.4 all-gather.10
  183.9 35.6 all-gather.14
  221.2 93.1 all-gather.8
  315.9 34.0 all-gather.12
  351.6 33.1 all-gather.16
where the time goes:
time: 491 us; the launch traced here: 483 us
  waiting for transfers between devices  186 us (38%)
  matrix products  112 us (23%)
  other arithmetic  88.4 us (18%)
  blocking collectives  46.9 us (10%)
  local copies, waits for them, and re-layouts  18.7 us (4%)
  between operations  16 us (3%)
  starting transfers between devices  13.9 us (3%)
    all_gather x1, waiting for transfers between devices, per_device(): full_rows = lax.all_gather(hidden, 'mp', axis=1, tiled=True)  86.1 us
    all_gather x1, waiting for transfers between devices, per_device(): lax.all_gather(query_weight, 'dp', axis=0, tiled=True)  51.1 us
    dot_general x2, matrix products, attend(): jnp.einsum('kgqd,skd->kgqs', queries, keys_flat, preferred_element_type=j...  45.3 us
    dot_general x2, matrix products, attend(): jnp.einsum('kgqs,skd->kgqd', weights.astype(jnp.bfloat16), values_flat, p...  42.7 us
    all_gather x1, waiting for transfers between devices, per_device(): lax.all_gather(key_weight, 'dp', axis=0, tiled=True)  42 us
    reduce_sum x2, other arithmetic, attend(): total_sum = total_sum * factor + jnp.sum(weights, axis=-1)  39.1 us
    all_gather x1, blocking collectives, per_device(): keys_part = lax.all_gather(pool_keys, 'dp', axis=0, tiled=True)  24.4 us
    all_gather x1, blocking collectives, per_device(): values_part = lax.all_gather(pool_values, 'dp', axis=0, tiled=True)  22.5 us
  transfers between devices with their start and end apart: 8, of which 4 were waited for; matrix products, arithmetic and copies ran while one was open for 27% of the time, Pallas kernels for 0%

commit v1 on v0

--- a/solution.py
+++ b/solution.py
@@ -3,10 +3,11 @@
 import jax
 import jax.numpy as jnp
 from jax import lax
-from jax.sharding import PartitionSpec as P
+from jax.sharding import Mesh, PartitionSpec as P
 
 HD = 128
 CAP = 2
+MAX_REQUEST = 3072
 
 
 NEG_BIG = -1e30
@@ -82,9 +83,13 @@
     return (new_best, total_sum, accumulated)
 
 
+def dp_index():
+    return lax.axis_index("dz") * lax.axis_size("dc") + lax.axis_index("dc")
+
+
 def relayout(prev_cache, dest_device):
     blocks_here = prev_cache.shape[0]
-    devices = lax.axis_size("dp")
+    devices = lax.axis_size("dz") * lax.axis_size("dc")
     slot_count = devices * CAP
     target = dest_device[:, 0]
     same_target = target[:, None] == target[None, :]
@@ -106,8 +111,8 @@
     packed = jnp.where(filled[:, None, None, None, None], packed, jnp.zeros_like(packed))
     slot_flags = filled.astype(jnp.bfloat16)
     arrived, arrived_flags = (
-        lax.all_to_all(packed, "dp", split_axis=0, concat_axis=0, tiled=True),
-        lax.all_to_all(slot_flags, "dp", split_axis=0, concat_axis=0, tiled=True),
+        lax.all_to_all(packed, ("dz", "dc"), split_axis=0, concat_axis=0, tiled=True),
+        lax.all_to_all(slot_flags, ("dz", "dc"), split_axis=0, concat_axis=0, tiled=True),
     )
     arrived_live = arrived_flags > 0.5
     order_no = jnp.cumsum(arrived_live.astype(jnp.int32)) - 1
@@ -138,25 +143,36 @@
 ):
     decode_cache = relayout(prev_cache, dest_device)
     row_count = hidden.shape[0]
-    global_rows = lax.axis_index("dp") * row_count + jnp.arange(row_count, dtype=jnp.int32)
+    me = dp_index()
+    side = lax.axis_index("dc")
+    sides = lax.axis_size("dc")
+    global_rows = me * row_count + jnp.arange(row_count, dtype=jnp.int32)
     request_of, group_hot, positions, ends_at = token_table(
         global_rows, request_lens, request_group, prompt_lens
     )
     full_rows = lax.all_gather(hidden, "mp", axis=1, tiled=True)
+    q_cols = query_weight.shape[1]
+    k_cols = key_weight.shape[1]
+    weights_here = jnp.concatenate([query_weight, key_weight, value_weight], axis=1)
+    weights_mine = lax.all_gather(weights_here, "dz", axis=0, tiled=True)
+    weights_other = lax.ppermute(weights_mine, "dc", perm=[(0, 1), (1, 0)])
+    pool_here = jnp.concatenate([pool_keys, pool_values], axis=2)
+    pool_all = lax.all_gather(pool_here, ("dz", "dc"), axis=0, tiled=True)
     as_float = full_rows.astype(jnp.float32)
     inverse = lax.rsqrt(jnp.mean(as_float * as_float, axis=1, keepdims=True) + EPSILON)
     normed = (as_float * inverse * norm_gain.astype(jnp.float32)[None, :]).astype(jnp.bfloat16)
-    query_full, key_full, value_full = (
-        lax.all_gather(query_weight, "dp", axis=0, tiled=True),
-        lax.all_gather(key_weight, "dp", axis=0, tiled=True),
-        lax.all_gather(value_weight, "dp", axis=0, tiled=True),
-    )
-    query_proj = jnp.dot(normed, query_full, preferred_element_type=jnp.float32)
-    key_proj = jnp.dot(normed, key_full, preferred_element_type=jnp.float32)
-    value_proj = jnp.dot(normed, value_full, preferred_element_type=jnp.float32)
-    query_proj = query_proj + query_bias.astype(jnp.float32)[None, :]
-    key_proj = key_proj + key_bias.astype(jnp.float32)[None, :]
-    value_proj = value_proj + value_bias.astype(jnp.float32)[None, :]
+    block_rows = weights_here.shape[0]
+    split = normed.reshape(row_count, -1, sides, block_rows)
+    normed_mine = lax.dynamic_index_in_dim(split, side, axis=2, keepdims=False)
+    normed_other = lax.dynamic_index_in_dim(split, sides - 1 - side, axis=2, keepdims=False)
+    proj = jnp.dot(
+        normed_mine.reshape(row_count, -1), weights_mine, preferred_element_type=jnp.float32
+    ) + jnp.dot(
+        normed_other.reshape(row_count, -1), weights_other, preferred_element_type=jnp.float32
+    )
+    query_proj = proj[:, :q_cols] + query_bias.astype(jnp.float32)[None, :]
+    key_proj = proj[:, q_cols:q_cols + k_cols] + key_bias.astype(jnp.float32)[None, :]
+    value_proj = proj[:, q_cols + k_cols:] + value_bias.astype(jnp.float32)[None, :]
     local_heads = query_proj.shape[1] // HD
     local_kv = key_proj.shape[1] // HD
     group_size = local_heads // local_kv
@@ -168,46 +184,37 @@
         .reshape(row_count, local_kv * HD)
     )
     values_new = value_proj.astype(jnp.bfloat16)
+    span_here = jnp.concatenate([keys_new, values_new], axis=1)
+    span_all = lax.all_gather(span_here, ("dz", "dc"), axis=0, tiled=True)
     score_scale = HD ** (-0.5)
     carried = (
         jnp.full((local_kv, group_size, row_count), NEG_BIG, jnp.float32),
         jnp.zeros((local_kv, group_size, row_count), jnp.float32),
         jnp.zeros((local_kv, group_size, row_count, HD), jnp.float32),
     )
-    block_size = pool_keys.shape[1]
-
-    def unchanged(previous):
-        return previous
-
-    keys_part = lax.all_gather(pool_keys, "dp", axis=0, tiled=True)
-    values_part = lax.all_gather(pool_values, "dp", axis=0, tiled=True)
-    blocks_here = keys_part.shape[0]
+    block_size = pool_all.shape[1]
+    blocks_here = pool_all.shape[0]
+    kv_width = local_kv * HD
     allowed_group = prompt_mask(prompt_table, prompt_lens, blocks_here, block_size)
     allowed = jnp.any(group_hot[:, :, None] & allowed_group[None, :, :], axis=1)
-    keys_flat = keys_part.reshape(blocks_here * block_size, local_kv, HD)
-    values_flat = values_part.reshape(blocks_here * block_size, local_kv, HD)
-
-    def prompt_update(previous):
-        return attend(previous, queries, keys_flat, values_flat, allowed, score_scale)
-
-    carried = lax.cond(jnp.any(allowed), prompt_update, unchanged, carried)
-    keys_part = lax.all_gather(keys_new, "dp", axis=0, tiled=True)
-    values_part = lax.all_gather(values_new, "dp", axis=0, tiled=True)
-    key_count = keys_part.shape[0]
-    key_rows = jnp.arange(key_count, dtype=jnp.int32)
+    keys_flat = pool_all[:, :, :kv_width].reshape(blocks_here * block_size, local_kv, HD)
+    values_flat = pool_all[:, :, kv_width:].reshape(blocks_here * block_size, local_kv, HD)
+    carried = attend(carried, queries, keys_flat, values_flat, allowed, score_scale)
+    key_count = span_all.shape[0]
+    window = min(key_count, MAX_REQUEST + row_count)
+    window = -(-window // row_count) * row_count
+    window_start = jnp.maximum((me + 1) * row_count - window, 0)
+    span_window = lax.dynamic_slice_in_dim(span_all, window_start, window, axis=0)
+    key_rows = window_start + jnp.arange(window, dtype=jnp.int32)
     key_request = request_index(key_rows, ends_at)
     span_allowed = (request_of[:, None] == key_request[None, :]) & (
         key_rows[None, :] <= global_rows[:, None]
     )
-    span_keys_flat = keys_part.reshape(key_count, local_kv, HD)
-    span_values_flat = values_part.reshape(key_count, local_kv, HD)
-
-    def span_update(previous):
-        return attend(
-            previous, queries, span_keys_flat, span_values_flat, span_allowed, score_scale
-        )
-
-    carried = lax.cond(jnp.any(span_allowed), span_update, unchanged, carried)
+    span_keys_flat = span_window[:, :kv_width].reshape(window, local_kv, HD)
+    span_values_flat = span_window[:, kv_width:].reshape(window, local_kv, HD)
+    carried = attend(
+        carried, queries, span_keys_flat, span_values_flat, span_allowed, score_scale
+    )
     best_score, total_sum, accumulated = carried
     output = accumulated / total_sum[..., None]
     context = output.transpose(2, 0, 1, 3).reshape(row_count, local_heads * HD).astype(jnp.bfloat16)
@@ -215,15 +222,18 @@
 
 
 def solution(mesh):
+    dp_size, mp_size = mesh.devices.shape
+    inner = Mesh(mesh.devices.reshape(dp_size // 2, 2, mp_size), ("dz", "dc", "mp"))
+    dp = ("dz", "dc")
     return jax.shard_map(
         per_device,
-        mesh=mesh,
+        mesh=inner,
         in_specs=(
-            P("dp", "mp"),
-            P(),
-            P("dp", "mp"),
-            P("dp", "mp"),
-            P("dp", "mp"),
+            P(dp, "mp"),
+            P(),
+            P(dp, "mp"),
+            P(dp, "mp"),
+            P(dp, "mp"),
             P("mp"),
             P("mp"),
             P("mp"),
@@ -231,11 +241,11 @@
             P(),
             P(),
             P(),
-            P("dp", None, "mp"),
-            P("dp", None, "mp"),
-            P("dp", None, None, None, "mp"),
-            P("dp", None),
+            P(dp, None, "mp"),
+            P(dp, None, "mp"),
+            P(dp, None, None, None, "mp"),
+            P(dp, None),
         ),
-        out_specs=(P("dp", "mp"), P("dp", None, None, None, "mp")),
+        out_specs=(P(dp, "mp"), P(dp, None, None, None, "mp")),
         check_vma=False,
     )

time: 491 us -> 551 us (1.12)
  the two profiles are of different devices: /device:TPU:1 before, /device:TPU:104 now
where the time goes in v1:
time: 551 us; the launch traced here: 546 us
  waiting for transfers between devices  357 us (65%)
  matrix products  69.4 us (13%)
  other arithmetic  68.4 us (12%)
  local copies, waits for them, and re-layouts  24 us (4%)
  between operations  14.3 us (3%)
  starting transfers between devices  13 us (2%)
    all_gather x1, waiting for transfers between devices, per_device(): weights_mine = lax.all_gather(weights_here, 'dz', axis=0, tiled=True)  205 us
    all_gather x1, waiting for transfers between devices, per_device(): full_rows = lax.all_gather(hidden, 'mp', axis=1, tiled=True)  68 us
    all_gather x1, waiting for transfers between devices, per_device(): pool_all = lax.all_gather(pool_here, ('dz', 'dc'), axis=0, tiled=True)  64.9 us
    reduce_sum x2, other arithmetic, attend(): total_sum = total_sum * factor + jnp.sum(weights, axis=-1)  33.2 us
    dot_general x2, matrix products, attend(): jnp.einsum('kgqs,skd->kgqd', weights.astype(jnp.bfloat16), values_flat, p...  29.2 us
    dot_general x2, matrix products, attend(): jnp.einsum('kgqd,skd->kgqs', queries, keys_flat, preferred_element_type=j...  28.4 us
    all_gather x1, waiting for transfers between devices, per_device(): span_all = lax.all_gather(span_here, ('dz', 'dc'), axis=0, tiled=True)  14.7 us
  transfers between devices with their start and end apart: 7, of which 5 were waited for; matrix products, arithmetic and copies ran while one was open for 14% of the time, Pallas kernels for 0%

profile of v1, /device:TPU:104, one launch (start us, length us, event | category | flops | bytes accessed | tf_op | source)
XLA Modules:
  0.0 546.2 jit_solution(2110852912330342658)
XLA Ops:
  7.2 0.0 all-gather.7.cloned.1.call-start
  7.3 2.5 pad_maximum_fusion
  9.8 0.0 all-gather.5.cloned.1.call-start
  9.9 2.3 copy.49
  12.2 205.5 %all-gather.7.cloned.1.call-done = bf16[4096,1280]{1,0:T(8,128)(2,1)} async-done(((bf16[512,1280]{1,0:T(8,128)(2,1)}), bf16[4096,1280]{1,0:T(8,128)(2,1)}) %all-gather.7.cloned.1.call-update) | async-done | bytes 10485776 | tf_op jit(solution)/shard_map/all_gather | solution.py:157
  217.7 0.2 convert_reduce_fusion.1
  217.9 0.1 fusion.34
  218.0 0.7 reshape.536
  218.7 6.9 %all-to-all-start = ((bf16[16,2,1]{1,2,0:T(2,128)(2,1)}), bf16[16,2,1]{1,2,0:T(2,128)(2,1)S(1)}, u32[]{:S(2)}, u32[]{:S(2)}) async-start(bf16[16,2,1]{1,2,0:T(2,128)(2,1)} %reshape.536), calls=%async_computation | async-start | bytes 16384 | tf_op jit(solution)/shard_map/all_to_all | solution.py:115
  225.6 0.0 all-gather.9.cloned.1.call-start
  225.7 0.6 pad_maximum_fusion.4
  226.3 0.0 all-gather.9.cloned.1.call-update
  226.4 0.2 reduce-window.16
  226.6 0.1 select_reduce_fusion
  226.8 7.3 %gather_fusion = bf16[32,4,2,128,128]{4,3,2,1,0:T(8,128)(2,1)} fusion(bf16[16,4,2,128,128]{4,3,2,1,0:T(8,128)(2,1)} %param.30, s32[1024]{0:T(1024)S(1)} %pad_clamp_fusion.1), kind=kCustom, calls=%fused_computation | custom fusion | bytes 16777344 | tf_op jit(solution)/shard_map/jit(_take)/gather | solution.py:110
  234.1 0.1 select_reduce_fusion.2
  234.2 0.1 fusion.31
  234.3 0.1 convert_reduce_fusion.2
  234.4 0.1 convert_reduce_fusion
  234.5 0.1 select_reduce_fusion.5
  234.6 0.1 select_reduce_fusion.4
  234.7 0.1 broadcast_bitcast_fusion.1
  234.8 0.8 multiply_cosine_fusion
  235.6 7.7 %select_select_fusion = bf16[32,4,2,128,128]{4,3,2,1,0:T(8,128)(2,1)} fusion(bf16[32,4,2,128,128]{4,3,2,1,0:T(8,128)(2,1)} %gather_fusion, pred[32]{0:T(512)(128)(4,1)S(1)} %compare_and_fusion.2, pred[32]{0:T(512)(128)(4,1)S(1)} %fusion.34), kind=kLoop, calls=%fused_computation.22 | loop fusion | flops 8388608 | bytes 16777280 | tf_op jit(solution)/shard_map/jit(_where)/select_n | solution.py:111
  243.3 68.0 %all-gather.5.cloned.1.call-done = bf16[384,8192]{0,1:T(8,128)(2,1)} async-done(((bf16[384,1024]{0,1:T(8,128)(2,1)}), bf16[384,8192]{0,1:T(8,128)(2,1)}) %all-gather.5.cloned.1.call-update) | async-done | bytes 6291472 | tf_op jit(solution)/shard_map/all_gather | solution.py:153
  311.3 4.2 fusion.9
  315.5 5.7 %all-to-all-start.1 = ((bf16[32,4,2,128,128]{4,3,2,1,0:T(8,128)(2,1)}), bf16[32,4,2,128,128]{4,3,2,1,0:T(8,128)(2,1)}, u32[]{:S(2)}, u32[]{:S(2)}) async-start(bf16[32,4,2,128,128]{4,3,2,1,0:T(8,128)(2,1)} %select_select_fusion), calls=%async_computation.1 | async-start | bytes 16777216 | tf_op jit(solution)/shard_map/all_to_all | solution.py:114
  321.2 0.2 all-gather.11.cloned.1.call-start
  321.5 6.4 %fusion.11 = bf16[384,8192]{0,1:T(8,128)(2,1)S(1)} fusion(bf16[384,8192]{0,1:T(8,128)(2,1)} %all-gather.5.cloned.1.call-done, f32[8192]{0:T(1024)S(1)} %convert_element_type.101, f32[384]{0:T(512)S(1)} %add_rsqrt_fusion), kind=kLoop, calls=%fused_computation.18 | loop fusion | flops 12582912 | bytes 12617216 | tf_op jit(solution)/shard_map/convert_element_type | solution.py:163
  327.9 0.9 constant_dynamic-slice_fusion
  328.8 0.7 slice-done.2
  329.4 4.3 fusion.47
  333.8 7.6 %convolution_add_fusion = f32[384,1280]{1,0:T(8,128)S(1)} fusion(f32[384,1280]{1,0:T(8,128)S(1)} %fusion.47, bf16[384,4096]{0,1:T(8,128)(2,1)S(1)} %bitcast.84, bf16[4096,1280]{1,0:T(8,128)(2,1)} %collective-permute-done), kind=kOutput, calls=%fused_computation.25 | convolution fusion | flops 4027023360 | bytes 17563648 | tf_op jit(solution)/shard_map/dot_general | solution.py:170
  341.4 0.1 fusion.24
  341.5 1.1 copy-done
  342.6 1.0 fusion.26
  343.6 0.7 pad_maximum_fusion.3
  344.3 0.1 broadcast_bitcast_fusion
  344.4 0.1 fusion.29
  344.5 2.0 and_reduce_fusion
  346.5 1.2 compare_and_fusion
  347.7 0.1 reshape.537
  347.8 0.1 reduce-window.17
  347.9 0.1 gt.25
  348.0 0.1 add_reduce_fusion
  348.1 0.1 select_reduce_fusion.1
  348.3 64.9 %all-gather.9.cloned.1.call-done = bf16[16,128,256]{2,1,0:T(8,128)(2,1)} async-done(((bf16[1,128,256]{2,1,0:T(8,128)(2,1)}), bf16[16,128,256]{2,1,0:T(8,128)(2,1)}) %all-gather.9.cloned.1.call-update) | async-done | bytes 1048592 | tf_op jit(solution)/shard_map/all_gather | solution.py:160
  413.1 2.1 fusion.46
  415.2 3.9 all-to-all-done.1
  419.1 6.5 %gather_fusion.1 = bf16[16,4,2,128,128]{4,3,2,1,0:T(8,128)(2,1)} fusion(bf16[32,4,2,128,128]{4,3,2,1,0:T(8,128)(2,1)} %all-to-all-done.1, s32[1024]{0:T(1024)S(1)} %pad_clamp_fusion), kind=kCustom, calls=%fused_computation.1 | custom fusion | bytes 8388672 | tf_op jit(solution)/shard_map/jit(_take)/gather | solution.py:123
  425.6 4.8 broadcast_select_fusion
  430.4 0.2 fusion.15
  430.6 0.3 copy.65
  431.0 0.5 fusion.45
  431.5 0.7 copy_bitcast_fusion
  432.2 0.7 fusion.22
  432.9 10.7 %fusion.3 = (f32[8,384]{1,0:T(8,128)S(1)}, f32[8,384,2048]{2,1,0:T(8,128)}) fusion(pred[384,2048]{1,0:T(8,128)(4,1)S(1)} %and_reduce_fusion, bf16[8,384,128]{2,1,0:T(8,128)(2,1)S(1)} %fusion.22, bf16[2048,128,1]{1,0,2:T(8,128)(2,1)S(1)} %bitcast.85), kind=kOutput, calls=%fused_computation.9 | convolution fusion | flops 1629484032 | bytes 27275264 | tf_op jit(solution)/shard_map/kgqd,skd->kgqs/dot_general | solution.py:68
  443.7 14.7 %all-gather.11.cloned.1.call-done = bf16[6144,256]{1,0:T(8,128)(2,1)} async-done(((bf16[384,256]{1,0:T(8,128)(2,1)}), bf16[6144,256]{1,0:T(8,128)(2,1)}) %all-gather.11.cloned.1.call-update) | async-done | bytes 3145744 | tf_op jit(solution)/shard_map/all_gather | solution.py:188
  458.4 17.6 %fusion = (f32[8,384]{1,0:T(8,128)S(1)}, f32[8,384,3456]{2,1,0:T(8,128)}) fusion(pred[384,3456]{1,0:T(8,128)(4,1)S(1)} %compare_and_fusion, bf16[8,384,128]{2,1,0:T(8,128)(2,1)S(1)} %fusion.22, bf16[6144,256]{1,0:T(8,128)(2,1)} %all-gather.11.cloned.1.call-done, s32[]{:T(128)S(6)} %max.20), kind=kOutput, calls=%fused_computation.4 | convolution fusion | flops 2749756416 | bytes 45477892 | tf_op jit(solution)/shard_map/kgqd,skd->kgqs/dot_general | solution.py:68
  476.1 12.0 %fusion.7 = f32[8,384]{1,0:T(8,128)S(1)} fusion(f32[8,384,2048]{2,1,0:T(8,128)} %get-tuple-element.36, f32[8,384]{1,0:T(8,128)S(1)} %get-tuple-element.32, pred[384,2048]{1,0:T(8,128)(4,1)S(1)} %and_reduce_fusion), kind=kLoop, calls=%fused_computation.12 | loop fusion | flops 31454208 | bytes 25976832 | tf_op jit(solution)/shard_map/reduce_sum | solution.py:76
  488.1 11.2 %fusion.12 = f32[8,384,128]{1,2,0:T(8,128)S(1)} fusion(bf16[2048,128,1]{1,0,2:T(8,128)(2,1)S(1)} %bitcast.87, f32[8,384,2048]{2,1,0:T(8,128)} %get-tuple-element.36, f32[8,384]{1,0:T(8,128)S(1)} %get-tuple-element.32, pred[384,2048]{1,0:T(8,128)(4,1)S(1)} %and_reduce_fusion), kind=kOutput, calls=%fused_computation.19 | convolution fusion | flops 1642070016 | bytes 28061696 | tf_op jit(solution)/shard_map/kgqs,skd->kgqd/dot_general | solution.py:77
  499.3 21.1 %fusion.1 = f32[8,384]{1,0:T(8,128)S(1)} fusion(f32[8,384,3456]{2,1,0:T(8,128)} %get-tuple-element.38, f32[8,384]{1,0:T(8,128)S(1)} %get-tuple-element.31, pred[384,3456]{1,0:T(8,128)(4,1)S(1)} %compare_and_fusion), kind=kLoop, calls=%fused_computation.5 | loop fusion | flops 53081088 | bytes 43819008 | tf_op jit(solution)/shard_map/reduce_sum | solution.py:76
  520.5 18.0 %divide_convert_fusion = bf16[8,384,128]{1,2,0:T(8,128)(2,1)S(1)} fusion(f32[8,384,128]{1,2,0:T(8,128)S(1)} %fusion.12, f32[8,384,3456]{2,1,0:T(8,128)} %get-tuple-element.38, f32[8,384]{1,0:T(8,128)S(1)} %get-tuple-element.31, pred[384,3456]{1,0:T(8,128)(4,1)S(1)} %compare_and_fusion, bf16[6144,256]{1,0:T(8,128)(2,1)} %all-gather.11.cloned.1.call-done, ...), kind=kOutput, calls=%fused_computation.35 | convolution fusion | flops 2772959232 | bytes 47087624 | tf_op jit(solution)/shard_map/kgqs,skd->kgqd/dot_general | solution.py:77
  538.5 1.2 copy.57
  (68 shorter events, 0.4 us)
Async XLA Ops:
  7.2 210.5 %copy-start.11 = (s32[16,1]{0,1:T(1,128)S(1)}, s32[16,1]{0,1:T(1,128)}, u32[]{:S(2)}) copy-start(s32[16,1]{0,1:T(1,128)} %param.31) | copy-start | bytes 196
  7.2 218.5 %copy-start.6 = (bf16[1,128,128]{2,1,0:T(8,128)(2,1)S(1)}, bf16[1,128,128]{2,1,0:T(8,128)(2,1)}, u32[]{:S(2)}) copy-start(bf16[1,128,128]{2,1,0:T(8,128)(2,1)} %param.28) | copy-start | bytes 98308
  7.2 218.5 %copy-start.5 = (bf16[1,128,128]{2,1,0:T(8,128)(2,1)S(1)}, bf16[1,128,128]{2,1,0:T(8,128)(2,1)}, u32[]{:S(2)}) copy-start(bf16[1,128,128]{2,1,0:T(8,128)(2,1)} %param.29) | copy-start | bytes 98308
  7.2 219.2 %copy-start.7 = (bf16[8192]{0:T(1024)(128)(2,1)S(1)}, bf16[8192]{0:T(1024)(128)(2,1)}, u32[]{:S(2)}) copy-start(bf16[8192]{0:T(1024)(128)(2,1)} %param.17) | copy-start | bytes 49156
  7.2 219.2 %copy-start.13 = (bf16[128]{0:T(256)(128)(2,1)S(1)}, bf16[128]{0:T(256)(128)(2,1)}, u32[]{:S(2)}) copy-start(bf16[128]{0:T(256)(128)(2,1)} %param.22) | copy-start | bytes 772
  7.2 219.2 %copy-start.15 = (s32[3]{0:T(128)S(1)}, s32[3]{0:T(128)}, u32[]{:S(2)}) copy-start(s32[3]{0:T(128)} %param.24) | copy-start | bytes 40
  7.2 219.4 %copy-start.14 = (bf16[128]{0:T(256)(128)(2,1)S(1)}, bf16[128]{0:T(256)(128)(2,1)}, u32[]{:S(2)}) copy-start(bf16[128]{0:T(256)(128)(2,1)} %param.23) | copy-start | bytes 772
  7.2 219.4 %copy-start.10 = (bf16[1024]{0:T(1024)(128)(2,1)S(1)}, bf16[1024]{0:T(1024)(128)(2,1)}, u32[]{:S(2)}) copy-start(bf16[1024]{0:T(1024)(128)(2,1)} %param.21) | copy-start | bytes 6148
  7.2 210.4 %all-gather.7.cloned.1.call-start = ((), (), s32[]{:S(2)}) async-start(), calls=%async_computation.3 | async-start | bytes 11796480 | tf_op jit(solution)/shard_map/all_gather | solution.py:157
  9.8 301.4 %all-gather.5.cloned.1.call-start = ((), (), s32[]{:S(2)}) async-start(), calls=%async_computation.2 | async-start | bytes 7077888 | tf_op jit(solution)/shard_map/all_gather | solution.py:153
  217.7 116.1 %collective-permute-start = (bf16[4096,1280]{1,0:T(8,128)(2,1)}, bf16[4096,1280]{1,0:T(8,128)(2,1)}, u32[]{:S(2)}, u32[]{:S(2)}) collective-permute-start(bf16[4096,1280]{1,0:T(8,128)(2,1)} %all-gather.7.cloned.1.call-done), channel_id=1, source_target_pairs={{0,8},{8,0},{1,9},{9,1},{2,10},{10,2},{3,11},{11,3},{4,12},{12,4},... | collective-permute-start | bytes 31457288 | tf_op jit(solution)/shard_map/ppermute | solution.py:158
  218.7 96.8 %all-to-all-start = ((bf16[16,2,1]{1,2,0:T(2,128)(2,1)}), bf16[16,2,1]{1,2,0:T(2,128)(2,1)S(1)}, u32[]{:S(2)}, u32[]{:S(2)}) async-start(bf16[16,2,1]{1,2,0:T(2,128)(2,1)} %reshape.536), calls=%async_computation | async-start | bytes 16384 | tf_op jit(solution)/shard_map/all_to_all | solution.py:115
  225.6 187.5 %all-gather.9.cloned.1.call-start = ((), (), s32[]{:S(2)}) async-start(), calls=%async_computation.4 | async-start | bytes 1114112 | tf_op jit(solution)/shard_map/all_gather | solution.py:160
  226.7 7.4 %copy-start.8 = (s32[4,4]{1,0:T(4,128)S(1)}, s32[4,4]{1,0:T(4,128)}, u32[]{:S(2)}) copy-start(s32[4,4]{1,0:T(4,128)} %param.27) | copy-start | bytes 196
  226.7 7.8 %copy-start.12 = (s32[3]{0:T(128)S(1)}, s32[3]{0:T(128)}, u32[]{:S(2)}) copy-start(s32[3]{0:T(128)} %param.25) | copy-start | bytes 40
  226.8 7.9 %copy-start.9 = (s32[4]{0:T(128)S(1)}, s32[4]{0:T(128)}, u32[]{:S(2)}) copy-start(s32[4]{0:T(128)} %param.26) | copy-start | bytes 52
  315.5 103.6 %all-to-all-start.1 = ((bf16[32,4,2,128,128]{4,3,2,1,0:T(8,128)(2,1)}), bf16[32,4,2,128,128]{4,3,2,1,0:T(8,128)(2,1)}, u32[]{:S(2)}, u32[]{:S(2)}) async-start(bf16[32,4,2,128,128]{4,3,2,1,0:T(8,128)(2,1)} %select_select_fusion), calls=%async_computation.1 | async-start | bytes 16777216 | tf_op jit(solution)/shard_map/all_to_all | solution.py:114
  321.2 137.2 %all-gather.11.cloned.1.call-start = ((), (), s32[]{:S(2)}) async-start(), calls=%async_computation.5 | async-start | bytes 3342336 | tf_op jit(solution)/shard_map/all_gather | solution.py:188
  321.5 7.3 %slice-start = ((s8[10485760]{0:T(1024)(128)(4,1)}), s8[4194304]{0:T(1024)(128)(4,1)S(1)}, s32[]{:S(2)}) async-start(s8[10485760]{0:T(1024)(128)(4,1)} %bitcast.81), calls=%async_computation.6 | async-start | bytes 8388608
  321.5 7.3 %slice-start.1 = ((s8[10485760]{0:T(1024)(128)(4,1)}), s8[4194304]{0:T(1024)(128)(4,1)S(1)}, s32[]{:S(2)}) async-start(s8[10485760]{0:T(1024)(128)(4,1)} %bitcast.81), calls=%async_computation.7 | async-start | bytes 8388608
  327.9 1.6 slice-start.2
  341.4 1.3 copy-start
  425.6 4.8 copy-start.1
  431.0 1.2 copy-start.2
  431.0 1.2 copy-start.3
  476.1 12.1 %copy-start.4 = (bf16[16,128,128]{2,1,0:T(8,128)(2,1)S(1)}, bf16[16,128,128]{2,1,0:T(8,128)(2,1)}, u32[]{:S(2)}) copy-start(bf16[16,128,128]{2,1,0:T(8,128)(2,1)} %get-tuple-element.25) | copy-start | bytes 1572868
Sparse Core Ops, SparseCore 0:
  10.3 207.3 all-gather.6
  220.6 90.6 all-gather.4
  313.6 99.5 all-gather.8
  414.7 43.6 all-gather.10

commit v2 on v1

--- a/solution.py
+++ b/solution.py
@@ -108,7 +108,6 @@
         jnp.where(matches, jnp.arange(blocks_here, dtype=jnp.int32)[None, :], 0), axis=1
     )
     packed = jnp.take(prev_cache, source, axis=0)
-    packed = jnp.where(filled[:, None, None, None, None], packed, jnp.zeros_like(packed))
     slot_flags = filled.astype(jnp.bfloat16)
     arrived, arrived_flags = (
         lax.all_to_all(packed, ("dz", "dc"), split_axis=0, concat_axis=0, tiled=True),
@@ -141,7 +140,6 @@
     prev_cache,
     dest_device,
 ):
-    decode_cache = relayout(prev_cache, dest_device)
     row_count = hidden.shape[0]
     me = dp_index()
     side = lax.axis_index("dc")
@@ -150,29 +148,35 @@
     request_of, group_hot, positions, ends_at = token_table(
         global_rows, request_lens, request_group, prompt_lens
     )
-    full_rows = lax.all_gather(hidden, "mp", axis=1, tiled=True)
+    mp_size = lax.axis_size("mp")
+    spread = jnp.broadcast_to(hidden[None], (mp_size,) + hidden.shape)
+    pieces = lax.all_to_all(spread, "mp", split_axis=0, concat_axis=0, tiled=True)
     q_cols = query_weight.shape[1]
     k_cols = key_weight.shape[1]
-    weights_here = jnp.concatenate([query_weight, key_weight, value_weight], axis=1)
-    weights_mine = lax.all_gather(weights_here, "dz", axis=0, tiled=True)
-    weights_other = lax.ppermute(weights_mine, "dc", perm=[(0, 1), (1, 0)])
-    pool_here = jnp.concatenate([pool_keys, pool_values], axis=2)
-    pool_all = lax.all_gather(pool_here, ("dz", "dc"), axis=0, tiled=True)
-    as_float = full_rows.astype(jnp.float32)
-    inverse = lax.rsqrt(jnp.mean(as_float * as_float, axis=1, keepdims=True) + EPSILON)
-    normed = (as_float * inverse * norm_gain.astype(jnp.float32)[None, :]).astype(jnp.bfloat16)
-    block_rows = weights_here.shape[0]
-    split = normed.reshape(row_count, -1, sides, block_rows)
-    normed_mine = lax.dynamic_index_in_dim(split, side, axis=2, keepdims=False)
-    normed_other = lax.dynamic_index_in_dim(split, sides - 1 - side, axis=2, keepdims=False)
-    proj = jnp.dot(
-        normed_mine.reshape(row_count, -1), weights_mine, preferred_element_type=jnp.float32
-    ) + jnp.dot(
-        normed_other.reshape(row_count, -1), weights_other, preferred_element_type=jnp.float32
+    block_rows = query_weight.shape[0]
+    pool_here = jnp.concatenate([pool_keys, pool_values], axis=2).reshape(block_rows, -1)
+    weights_here = jnp.concatenate([query_weight, key_weight, value_weight, pool_here], axis=1)
+    weights_all = lax.all_gather(weights_here, ("dz", "dc"), axis=0, tiled=True)
+    proj_cols = q_cols + 2 * k_cols
+    pool_all = weights_all[:, proj_cols:].reshape(
+        (-1,) + pool_keys.shape[1:2] + (2 * pool_keys.shape[2],)
+    )
+    as_float = pieces.astype(jnp.float32)
+    inverse = lax.rsqrt(
+        jnp.mean(jnp.sum(as_float * as_float, axis=2), axis=0)[None, :, None] / pieces.shape[2]
+        + EPSILON
+    )
+    gain = norm_gain.astype(jnp.float32).reshape(mp_size, 1, -1)
+    normed = (as_float * inverse * gain).astype(jnp.bfloat16)
+    proj = jnp.einsum(
+        "jtf,jfc->tc",
+        normed,
+        weights_all.reshape(mp_size, -1, weights_all.shape[1]),
+        preferred_element_type=jnp.float32,
     )
     query_proj = proj[:, :q_cols] + query_bias.astype(jnp.float32)[None, :]
     key_proj = proj[:, q_cols:q_cols + k_cols] + key_bias.astype(jnp.float32)[None, :]
-    value_proj = proj[:, q_cols + k_cols:] + value_bias.astype(jnp.float32)[None, :]
+    value_proj = proj[:, q_cols + k_cols:proj_cols] + value_bias.astype(jnp.float32)[None, :]
     local_heads = query_proj.shape[1] // HD
     local_kv = key_proj.shape[1] // HD
     group_size = local_heads // local_kv
@@ -186,6 +190,8 @@
     values_new = value_proj.astype(jnp.bfloat16)
     span_here = jnp.concatenate([keys_new, values_new], axis=1)
     span_all = lax.all_gather(span_here, ("dz", "dc"), axis=0, tiled=True)
+    prev_cache, span_all = lax.optimization_barrier((prev_cache, span_all))
+    decode_cache = relayout(prev_cache, dest_device)
     score_scale = HD ** (-0.5)
     carried = (
         jnp.full((local_kv, group_size, row_count), NEG_BIG, jnp.float32),

time: 551 us -> 392 us (0.71)
  waiting for transfers between devices: 357 us -> 177 us
  local copies, waits for them, and re-layouts: 24 us -> 36.1 us
  matrix products: 69.4 us -> 75.6 us
    all_gather x3 -> x1, waiting for transfers between devices: 338 us -> 79 us  [per_device(): weights_all = lax.all_gather(weights_here, ('dz', 'dc'), axis=0, tiled=True)]
    all_to_all x0 -> x1, waiting for transfers between devices: none -> 86.7 us  [per_device(): lax.all_to_all(spread, 'mp', split_axis=0, concat_axis=0, tiled=True)]
    all_gather x1, waiting for transfers between devices: 14.7 us -> 0.82 us  [per_device(): span_all = lax.all_gather(span_here, ('dz', 'dc'), axis=0, tiled=True)]
    select_n x1 -> x0, other arithmetic: 7.69 us -> none  [relayout(): jnp.where(filled[:, None, None, None, None], packed, jnp.zeros_like(packed))]
    select_n x1 -> x2, other arithmetic: 0.01 us -> 7.57 us  [relayout(): packed = jnp.take(prev_cache, source, axis=0)]
    all_to_all x1, waiting for transfers between devices: 3.91 us -> 10.4 us  [relayout(): lax.all_to_all(packed, ('dz', 'dc'), split_axis=0, concat_axis=0, tiled=T...]
    convert_element_type x2 -> x0, other arithmetic: 6.38 us -> none  [the longest x1 6.37 us: per_device(): (as_float * inverse * norm_gain.astype(jnp.float32)[None, :]).astype(jnp....]
    all_to_all x0 -> x1, starting transfers between devices: none -> 6.18 us  [per_device(): lax.all_to_all(spread, 'mp', split_axis=0, concat_axis=0, tiled=True)]
  transfers between devices with their start and end apart: 7 -> 5, of which waited for: 5 -> 4; matrix products, arithmetic and copies ran while one was open for 14% -> 38% of each run, Pallas kernels for 0% -> 0%
where the time goes in v2:
time: 392 us; the launch traced here: 386 us
  waiting for transfers between devices  177 us (45%)
  matrix products  75.6 us (19%)
  other arithmetic  64.3 us (16%)
  local copies, waits for them, and re-layouts  36.1 us (9%)
  starting transfers between devices  18.5 us (5%)
  between operations  14.5 us (4%)
    all_to_all x1, waiting for transfers between devices, per_device(): lax.all_to_all(spread, 'mp', split_axis=0, concat_axis=0, tiled=True)  86.7 us
    all_gather x1, waiting for transfers between devices, per_device(): weights_all = lax.all_gather(weights_here, ('dz', 'dc'), axis=0, tiled=True)  79 us
    reduce_sum x2, other arithmetic, attend(): total_sum = total_sum * factor + jnp.sum(weights, axis=-1)  33.1 us
    dot_general x2, matrix products, attend(): jnp.einsum('kgqs,skd->kgqd', weights.astype(jnp.bfloat16), values_flat, p...  29.6 us
    dot_general x2, matrix products, attend(): jnp.einsum('kgqd,skd->kgqs', queries, keys_flat, preferred_element_type=j...  28.7 us
    dot_general x1, matrix products, per_device(): jnp.einsum('jtf,jfc->tc', normed, weights_all.reshape(mp_size, -1, weight...  17.4 us
    all_to_all x1, waiting for transfers between devices, relayout(): lax.all_to_all(packed, ('dz', 'dc'), split_axis=0, concat_axis=0, tiled=T...  10.4 us
  transfers between devices with their start and end apart: 5, of which 4 were waited for; matrix products, arithmetic and copies ran while one was open for 38% of the time, Pallas kernels for 0%

profile of v2, /device:TPU:104, one launch (start us, length us, event | category | flops | bytes accessed | tf_op | source)
XLA Modules:
  0.0 386.0 jit_solution(9952316751931135327)
XLA Ops:
  7.2 0.0 all-gather.3.cloned.1.call-start
  7.2 0.8 pad_maximum_fusion.4
  8.0 0.1 reshape.504
  8.1 2.6 pad_maximum_fusion
  10.7 0.0 all-gather.3.cloned.1.call-update
  10.7 4.6 %broadcast_in_dim.193 = bf16[8,384,1024]{2,1,0:T(8,128)(2,1)} broadcast(bf16[384,1024]{1,0:T(8,128)(2,1)} %param.16), dimensions={1,2} | broadcast | bytes 7077888 | tf_op jit(solution)/shard_map/broadcast_in_dim | solution.py:152
  15.4 6.2 %all-to-all-start = ((bf16[8,384,1024]{2,1,0:T(8,128)(2,1)}), bf16[8,384,1024]{2,1,0:T(8,128)(2,1)}, u32[]{:S(2)}, u32[]{:S(2)}) async-start(bf16[8,384,1024]{2,1,0:T(8,128)(2,1)} %broadcast_in_dim.193), calls=%async_computation | async-start | bytes 12582912 | tf_op jit(solution)/shard_map/all_to_all | solution.py:153
  21.7 0.2 reduce-window.16
  21.9 0.2 convert_reduce_fusion.1
  22.0 0.1 fusion.39
  22.1 0.7 reshape.537
  22.8 0.1 select_reduce_fusion
  23.0 0.1 select_reduce_fusion.2
  23.1 0.1 fusion.36
  23.2 0.1 convert_reduce_fusion.2
  23.3 0.1 convert_reduce_fusion
  23.4 0.1 select_reduce_fusion.5
  23.5 0.1 select_reduce_fusion.4
  23.6 0.4 multiply_cosine_fusion
  24.0 86.7 %all-to-all-done = bf16[8,384,1024]{2,1,0:T(8,128)(2,1)} async-done(((bf16[8,384,1024]{2,1,0:T(8,128)(2,1)}), bf16[8,384,1024]{2,1,0:T(8,128)(2,1)}, u32[]{:S(2)}, u32[]{:S(2)}) %all-to-all-start) | async-done | bytes 6291488 | tf_op jit(solution)/shard_map/all_to_all | solution.py:153
  110.7 5.4 %all-to-all-start.1 = ((bf16[16,2,1]{1,2,0:T(2,128)(2,1)}), bf16[16,2,1]{1,2,0:T(2,128)(2,1)S(1)}, u32[]{:S(2)}, u32[]{:S(2)}) async-start(bf16[16,2,1]{1,2,0:T(2,128)(2,1)} %reshape.537), calls=%async_computation.1 | async-start | bytes 16384 | tf_op jit(solution)/shard_map/all_to_all | solution.py:114
  116.2 0.0 all-gather.5.cloned.1.call-start
  116.2 4.3 %fusion.9 = f32[384]{0:T(512)S(1)} fusion(bf16[8,384,1024]{2,1,0:T(8,128)(2,1)} %all-to-all-done), kind=kLoop, calls=%fused_computation.16 | loop fusion | flops 9436800 | bytes 6292992 | tf_op jit(solution)/shard_map/reduce_sum | solution.py:166
  120.5 79.0 %all-gather.3.cloned.1.call-done = bf16[8192,1344]{1,0:T(8,128)(2,1)} async-done(((bf16[512,1344]{1,0:T(8,128)(2,1)}), bf16[8192,1344]{1,0:T(8,128)(2,1)}) %all-gather.3.cloned.1.call-update) | async-done | bytes 22020112 | tf_op jit(solution)/shard_map/all_gather | solution.py:159
  199.6 17.4 %fusion.19 = f32[384,1344]{0,1:T(8,128)S(1)} fusion(bf16[8,1024,1344]{2,1,0:T(8,128)(2,1)} %bitcast.75, bf16[8,384,1024]{2,1,0:T(8,128)(2,1)} %all-to-all-done, f32[8,1024]{1,0:T(8,128)S(1)} %reshape.513, f32[384]{0:T(512)S(1)} %add_rsqrt_fusion), kind=kOutput, calls=%fused_computation.28 | convolution fusion | flops 8468299776 | bytes 30410240 | tf_op jit(solution)/shard_map/jtf,jfc->tc/dot_general | solution.py:171
  216.9 0.1 fusion.31
  217.0 0.1 fusion.30
  217.2 1.0 pad_maximum_fusion.3
  218.2 0.1 broadcast_bitcast_fusion.1
  218.3 0.1 broadcast_bitcast_fusion
  218.3 0.1 fusion.34
  218.4 2.1 and_reduce_fusion
  220.5 1.2 compare_and_fusion
  221.7 0.1 reshape.538
  221.8 0.1 reduce-window.17
  221.9 0.1 gt.25
  222.0 0.1 add_reduce_fusion
  222.1 0.1 select_reduce_fusion.1
  222.3 0.8 copy.52
  223.1 0.8 copy.56
  223.9 1.6 slice_add_fusion
  225.5 1.3 fusion.50
  226.8 2.7 copy.67
  229.6 2.7 copy.68
  232.3 1.7 copy.53
  234.0 1.7 slice.55
  235.8 2.2 reshape.509
  237.9 1.4 fusion.51
  239.4 1.7 negate_bitcast_fusion
  241.1 1.5 fusion.27
  242.6 10.9 %fusion.3 = (f32[8,384]{1,0:T(8,128)S(1)}, f32[8,384,2048]{2,1,0:T(8,128)}) fusion(pred[384,2048]{1,0:T(8,128)(4,1)S(1)} %copy-done, bf16[8,384,128]{2,1,0:T(8,128)(2,1)S(1)} %fusion.27, bf16[2048,128,1]{1,0,2:T(8,128)(2,1)S(1)} %bitcast.72), kind=kOutput, calls=%fused_computation.9 | convolution fusion | flops 1629484032 | bytes 27275264 | tf_op jit(solution)/shard_map/kgqd,skd->kgqs/dot_general | solution.py:68
  253.5 0.8 all-gather.5.cloned.1.call-done
  254.4 7.2 %gather_fusion = bf16[32,4,2,128,128]{4,3,2,1,0:T(8,128)(2,1)} fusion(bf16[16,4,2,128,128]{4,3,2,1,0:T(8,128)(2,1)} %param.30, s32[1024]{0:T(1024)S(1)} %pad_clamp_fusion.1), kind=kCustom, calls=%fused_computation | custom fusion | bytes 16777344 | tf_op jit(solution)/shard_map/jit(_take)/gather | solution.py:110
  261.6 7.6 %broadcast_select_fusion = bf16[32,4,2,128,128]{4,3,2,1,0:T(8,128)(2,1)} fusion(bf16[32,4,2,128,128]{4,3,2,1,0:T(8,128)(2,1)} %gather_fusion, pred[32]{0:T(512)(128)(4,1)S(1)} %compare_and_fusion.2), kind=kLoop, calls=%fused_computation.22 | loop fusion | flops 4194304 | bytes 16777248 | tf_op jit(solution)/shard_map/jit(_take)/select_n | solution.py:110
  269.1 6.9 %all-to-all-start.2 = ((bf16[32,4,2,128,128]{4,3,2,1,0:T(8,128)(2,1)}), bf16[32,4,2,128,128]{4,3,2,1,0:T(8,128)(2,1)}, u32[]{:S(2)}, u32[]{:S(2)}) async-start(bf16[32,4,2,128,128]{4,3,2,1,0:T(8,128)(2,1)} %broadcast_select_fusion), calls=%async_computation.2 | async-start | bytes 16777216 | tf_op jit(solution)/shard_map/all_to_all | solution.py:113
  276.0 17.8 %fusion = (f32[8,384]{1,0:T(8,128)S(1)}, f32[8,384,3456]{2,1,0:T(8,128)}) fusion(pred[384,3456]{1,0:T(8,128)(4,1)S(1)} %compare_and_fusion, bf16[8,384,128]{2,1,0:T(8,128)(2,1)S(1)} %fusion.27, bf16[6144,256]{0,1:T(8,128)(2,1)} %all-gather.5.cloned.1.call-done, s32[]{:T(128)S(6)} %max.20), kind=kOutput, calls=%fused_computation.4 | convolution fusion | flops 2749756416 | bytes 45477892 | tf_op jit(solution)/shard_map/kgqd,skd->kgqs/dot_general | solution.py:68
  293.7 21.1 %fusion.1 = f32[8,384]{1,0:T(8,128)S(1)} fusion(f32[8,384,3456]{2,1,0:T(8,128)} %get-tuple-element.38, f32[8,384]{1,0:T(8,128)S(1)} %get-tuple-element.31, pred[384,3456]{1,0:T(8,128)(4,1)S(1)} %compare_and_fusion), kind=kLoop, calls=%fused_computation.5 | loop fusion | flops 53081088 | bytes 43819008 | tf_op jit(solution)/shard_map/reduce_sum | solution.py:76
  314.9 12.0 %fusion.7 = f32[8,384]{1,0:T(8,128)S(1)} fusion(f32[8,384,2048]{2,1,0:T(8,128)} %get-tuple-element.36, f32[8,384]{1,0:T(8,128)S(1)} %get-tuple-element.32, pred[384,2048]{1,0:T(8,128)(4,1)S(1)} %copy-done), kind=kLoop, calls=%fused_computation.12 | loop fusion | flops 31454208 | bytes 25976832 | tf_op jit(solution)/shard_map/reduce_sum | solution.py:76
  326.9 11.2 %fusion.12 = f32[8,384,128]{1,2,0:T(8,128)S(1)} fusion(bf16[2048,128,1]{1,0,2:T(8,128)(2,1)S(1)} %bitcast.74, f32[8,384,2048]{2,1,0:T(8,128)} %get-tuple-element.36, f32[8,384]{1,0:T(8,128)S(1)} %get-tuple-element.32, pred[384,2048]{1,0:T(8,128)(4,1)S(1)} %copy-done), kind=kOutput, calls=%fused_computation.19 | convolution fusion | flops 1642070016 | bytes 28061696 | tf_op jit(solution)/shard_map/kgqs,skd->kgqd/dot_general | solution.py:77
  338.1 18.4 %divide_convert_fusion = bf16[8,384,128]{1,2,0:T(8,128)(2,1)S(1)} fusion(f32[8,384,128]{1,2,0:T(8,128)S(1)} %fusion.12, f32[8,384,3456]{2,1,0:T(8,128)} %get-tuple-element.38, f32[8,384]{1,0:T(8,128)S(1)} %get-tuple-element.31, pred[384,3456]{1,0:T(8,128)(4,1)S(1)} %compare_and_fusion, bf16[6144,256]{0,1:T(8,128)(2,1)} %all-gather.5.cloned.1.call-done, ...), kind=kOutput, calls=%fused_computation.33 | convolution fusion | flops 2772959232 | bytes 47087624 | tf_op jit(solution)/shard_map/kgqs,skd->kgqd/dot_general | solution.py:77
  356.5 1.2 copy.61
  357.7 10.4 %all-to-all-done.2 = bf16[32,4,2,128,128]{4,3,2,1,0:T(8,128)(2,1)} async-done(((bf16[32,4,2,128,128]{4,3,2,1,0:T(8,128)(2,1)}), bf16[32,4,2,128,128]{4,3,2,1,0:T(8,128)(2,1)}, u32[]{:S(2)}, u32[]{:S(2)}) %all-to-all-start.2) | async-done | bytes 8388640 | tf_op jit(solution)/shard_map/all_to_all | solution.py:113
  368.0 6.5 %gather_fusion.1 = bf16[16,4,2,128,128]{4,3,2,1,0:T(8,128)(2,1)} fusion(bf16[32,4,2,128,128]{4,3,2,1,0:T(8,128)(2,1)} %all-to-all-done.2, s32[1024]{0:T(1024)S(1)} %pad_clamp_fusion), kind=kCustom, calls=%fused_computation.1 | custom fusion | bytes 8388672 | tf_op jit(solution)/shard_map/jit(_take)/gather | solution.py:122
  374.5 4.7 %broadcast_select_fusion.1 = bf16[16,4,2,128,128]{4,3,2,1,0:T(8,128)(2,1)} fusion(bf16[16,4,2,128,128]{4,3,2,1,0:T(8,128)(2,1)} %gather_fusion.1, pred[16]{0:T(512)(128)(4,1)S(1)} %compare_and_fusion.3), kind=kLoop, calls=%fused_computation.27 | loop fusion | flops 2097152 | bytes 8388624 | tf_op jit(solution)/shard_map/jit(_take)/select_n | solution.py:122
  (53 shorter events, 0.3 us)
Async XLA Ops:
  7.2 192.4 %all-gather.3.cloned.1.call-start = ((), (), s32[]{:S(2)}) async-start(), calls=%async_computation.3 | async-start | bytes 24510464 | tf_op jit(solution)/shard_map/all_gather | solution.py:159
  15.3 6.2 %copy-start.4 = (bf16[8192]{0:T(1024)(128)(2,1)S(1)}, bf16[8192]{0:T(1024)(128)(2,1)}, u32[]{:S(2)}) copy-start(bf16[8192]{0:T(1024)(128)(2,1)} %param.17) | copy-start | bytes 49156
  15.3 6.3 %copy-start.10 = (bf16[128]{0:T(256)(128)(2,1)S(1)}, bf16[128]{0:T(256)(128)(2,1)}, u32[]{:S(2)}) copy-start(bf16[128]{0:T(256)(128)(2,1)} %param.22) | copy-start | bytes 772
  15.3 6.3 %copy-start.11 = (bf16[128]{0:T(256)(128)(2,1)S(1)}, bf16[128]{0:T(256)(128)(2,1)}, u32[]{:S(2)}) copy-start(bf16[128]{0:T(256)(128)(2,1)} %param.23) | copy-start | bytes 772
  15.3 6.3 %copy-start.7 = (bf16[1024]{0:T(1024)(128)(2,1)S(1)}, bf16[1024]{0:T(1024)(128)(2,1)}, u32[]{:S(2)}) copy-start(bf16[1024]{0:T(1024)(128)(2,1)} %param.21) | copy-start | bytes 6148
  15.3 6.3 %copy-start.12 = (s32[3]{0:T(128)S(1)}, s32[3]{0:T(128)}, u32[]{:S(2)}) copy-start(s32[3]{0:T(128)} %param.24) | copy-start | bytes 40
  15.3 6.5 %copy-start.8 = (s32[16,1]{0,1:T(1,128)S(1)}, s32[16,1]{0,1:T(1,128)}, u32[]{:S(2)}) copy-start(s32[16,1]{0,1:T(1,128)} %param.31) | copy-start | bytes 196
  15.3 7.6 %copy-start.5 = (s32[4,4]{1,0:T(4,128)S(1)}, s32[4,4]{1,0:T(4,128)}, u32[]{:S(2)}) copy-start(s32[4,4]{1,0:T(4,128)} %param.27) | copy-start | bytes 196
  15.4 8.0 %copy-start.9 = (s32[3]{0:T(128)S(1)}, s32[3]{0:T(128)}, u32[]{:S(2)}) copy-start(s32[3]{0:T(128)} %param.25) | copy-start | bytes 40
  15.4 8.1 %copy-start.6 = (s32[4]{0:T(128)S(1)}, s32[4]{0:T(128)}, u32[]{:S(2)}) copy-start(s32[4]{0:T(128)} %param.26) | copy-start | bytes 52
  15.4 95.4 %all-to-all-start = ((bf16[8,384,1024]{2,1,0:T(8,128)(2,1)}), bf16[8,384,1024]{2,1,0:T(8,128)(2,1)}, u32[]{:S(2)}, u32[]{:S(2)}) async-start(bf16[8,384,1024]{2,1,0:T(8,128)(2,1)} %broadcast_in_dim.193), calls=%async_computation | async-start | bytes 12582912 | tf_op jit(solution)/shard_map/all_to_all | solution.py:153
  110.7 110.9 %all-to-all-start.1 = ((bf16[16,2,1]{1,2,0:T(2,128)(2,1)}), bf16[16,2,1]{1,2,0:T(2,128)(2,1)S(1)}, u32[]{:S(2)}, u32[]{:S(2)}) async-start(bf16[16,2,1]{1,2,0:T(2,128)(2,1)} %reshape.537), calls=%async_computation.1 | async-start | bytes 16384 | tf_op jit(solution)/shard_map/all_to_all | solution.py:114
  116.2 138.2 %all-gather.5.cloned.1.call-start = ((), (), s32[]{:S(2)}) async-start(), calls=%async_computation.4 | async-start | bytes 3342336 | tf_op jit(solution)/shard_map/all_gather | solution.py:192
  216.9 1.5 copy-start.3
  237.9 3.1 copy-start.1
  237.9 3.1 copy-start.2
  237.9 4.7 %copy-start = (pred[384,2048]{1,0:T(8,128)(4,1)S(1)}, pred[384,2048]{1,0:T(8,128)(4,1)}, u32[]{:S(2)}) copy-start(pred[384,2048]{1,0:T(8,128)(4,1)} %and_reduce_fusion) | copy-start | bytes 2359300
  269.1 98.9 %all-to-all-start.2 = ((bf16[32,4,2,128,128]{4,3,2,1,0:T(8,128)(2,1)}), bf16[32,4,2,128,128]{4,3,2,1,0:T(8,128)(2,1)}, u32[]{:S(2)}, u32[]{:S(2)}) async-start(bf16[32,4,2,128,128]{4,3,2,1,0:T(8,128)(2,1)} %broadcast_select_fusion), calls=%async_computation.2 | async-start | bytes 16777216 | tf_op jit(solution)/shard_map/all_to_all | solution.py:113
Sparse Core Ops, SparseCore 0:
  10.8 188.6 all-gather.2
  218.3 36.0 all-gather.4

commit v3 on v2

--- a/solution.py
+++ b/solution.py
@@ -4,6 +4,7 @@
 import jax.numpy as jnp
 from jax import lax
 from jax.sharding import Mesh, PartitionSpec as P
+
 
 HD = 128
 CAP = 2
@@ -47,8 +48,8 @@
     return (request_of, group_hot, positions, ends_at)
 
 
-def prompt_mask(prompt_table, prompt_lens, block_count, block_size):
-    blocks = jnp.arange(block_count, dtype=jnp.int32)
+def prompt_mask(prompt_table, prompt_lens, blocks, block_size):
+    block_count = blocks.shape[0]
     matching = prompt_table[:, :, None] == blocks[None, None, :]
     present = jnp.any(matching, axis=1)
     slot_no = jnp.sum(
@@ -122,7 +123,7 @@
     return jnp.take(arrived, chosen, axis=0)
 
 
-def per_device(
+def layer(
     hidden,
     norm_gain,
     query_weight,
@@ -142,8 +143,6 @@
 ):
     row_count = hidden.shape[0]
     me = dp_index()
-    side = lax.axis_index("dc")
-    sides = lax.axis_size("dc")
     global_rows = me * row_count + jnp.arange(row_count, dtype=jnp.int32)
     request_of, group_hot, positions, ends_at = token_table(
         global_rows, request_lens, request_group, prompt_lens
@@ -156,11 +155,35 @@
     block_rows = query_weight.shape[0]
     pool_here = jnp.concatenate([pool_keys, pool_values], axis=2).reshape(block_rows, -1)
     weights_here = jnp.concatenate([query_weight, key_weight, value_weight, pool_here], axis=1)
-    weights_all = lax.all_gather(weights_here, ("dz", "dc"), axis=0, tiled=True)
     proj_cols = q_cols + 2 * k_cols
-    pool_all = weights_all[:, proj_cols:].reshape(
-        (-1,) + pool_keys.shape[1:2] + (2 * pool_keys.shape[2],)
-    )
+    me16 = me
+    nd = lax.axis_size("dz") * lax.axis_size("dc")
+    dp_axes = ("dz", "dc")
+
+    def shift(x, pairs):
+        return lax.ppermute(x, dp_axes, perm=pairs)
+
+    y_swap = [(p, p ^ 2) for p in range(nd)]
+    z_up = [(p, (p + 4) % nd) for p in range(nd)]
+    z_down = [(p, (p - 4) % nd) for p in range(nd)]
+    half_rows = block_rows // 2
+    wave_a = weights_here
+    wave_b = shift(wave_a, y_swap)
+    held = []
+    for wave in (wave_a, wave_b):
+        from_below = shift(wave, z_up)
+        from_above = shift(wave, z_down)
+        far_low = shift(from_below[:half_rows], z_up)
+        far_high = shift(from_above[half_rows:], z_down)
+        held.extend([wave, from_below, from_above, jnp.concatenate([far_low, far_high], axis=0)])
+    ids_a = [me16, (me16 - 4) % nd, (me16 + 4) % nd, (me16 + 8) % nd]
+    ids = jnp.stack(ids_a + [i ^ 2 for i in ids_a])
+    weights_mine = jnp.concatenate(held[0:4] + held[4:8], axis=0)
+    weights_other = shift(weights_mine, [(p, p ^ 1) for p in range(nd)])
+    ids_other = ids ^ 1
+    block_ids = jnp.concatenate([ids, ids_other])
+    pool_rows = jnp.concatenate([weights_mine[:, proj_cols:], weights_other[:, proj_cols:]], axis=0)
+    pool_all = pool_rows.reshape((-1,) + pool_keys.shape[1:2] + (2 * pool_keys.shape[2],))
     as_float = pieces.astype(jnp.float32)
     inverse = lax.rsqrt(
         jnp.mean(jnp.sum(as_float * as_float, axis=2), axis=0)[None, :, None] / pieces.shape[2]
@@ -168,11 +191,16 @@
     )
     gain = norm_gain.astype(jnp.float32).reshape(mp_size, 1, -1)
     normed = (as_float * inverse * gain).astype(jnp.bfloat16)
-    proj = jnp.einsum(
-        "jtf,jfc->tc",
-        normed,
-        weights_all.reshape(mp_size, -1, weights_all.shape[1]),
-        preferred_element_type=jnp.float32,
+    per_piece = pieces.shape[2] // block_rows
+    normed_blocks = normed.reshape(mp_size, row_count, per_piece, block_rows)
+    normed_blocks = normed_blocks.transpose(0, 2, 1, 3).reshape(-1, row_count, block_rows)
+
+    def pick(which):
+        chosen = jnp.take(normed_blocks, which, axis=0)
+        return chosen.transpose(1, 0, 2).reshape(row_count, -1)
+
+    proj = jnp.dot(pick(ids), weights_mine, preferred_element_type=jnp.float32) + jnp.dot(
+        pick(ids_other), weights_other, preferred_element_type=jnp.float32
     )
     query_proj = proj[:, :q_cols] + query_bias.astype(jnp.float32)[None, :]
     key_proj = proj[:, q_cols:q_cols + k_cols] + key_bias.astype(jnp.float32)[None, :]
@@ -201,7 +229,7 @@
     block_size = pool_all.shape[1]
     blocks_here = pool_all.shape[0]
     kv_width = local_kv * HD
-    allowed_group = prompt_mask(prompt_table, prompt_lens, blocks_here, block_size)
+    allowed_group = prompt_mask(prompt_table, prompt_lens, block_ids, block_size)
     allowed = jnp.any(group_hot[:, :, None] & allowed_group[None, :, :], axis=1)
     keys_flat = pool_all[:, :, :kv_width].reshape(blocks_here * block_size, local_kv, HD)
     values_flat = pool_all[:, :, kv_width:].reshape(blocks_here * block_size, local_kv, HD)
@@ -221,7 +249,7 @@
     carried = attend(
         carried, queries, span_keys_flat, span_values_flat, span_allowed, score_scale
     )
-    best_score, total_sum, accumulated = carried
+    _, total_sum, accumulated = carried
     output = accumulated / total_sum[..., None]
     context = output.transpose(2, 0, 1, 3).reshape(row_count, local_heads * HD).astype(jnp.bfloat16)
     return (context, decode_cache)
@@ -232,7 +260,7 @@
     inner = Mesh(mesh.devices.reshape(dp_size // 2, 2, mp_size), ("dz", "dc", "mp"))
     dp = ("dz", "dc")
     return jax.shard_map(
-        per_device,
+        layer,
         mesh=inner,
         in_specs=(
             P(dp, "mp"),

time: 392 us -> 454 us (1.16)
  the two profiles are of different devices: /device:TPU:104 before, /device:TPU:1 now
where the time goes in v3:
time: 454 us; the launch traced here: 447 us
  waiting for transfers between devices  173 us (38%)
  other arithmetic  76.8 us (17%)
  matrix products  76.5 us (17%)
  local copies, waits for them, and re-layouts  69.7 us (15%)
  starting transfers between devices  35.9 us (8%)
  between operations  14.8 us (3%)
    all_to_all x1, waiting for transfers between devices, layer(): lax.all_to_all(spread, 'mp', split_axis=0, concat_axis=0, tiled=True)  84.7 us
    ppermute x10, waiting for transfers between devices, shift(): return lax.ppermute(x, dp_axes, perm=pairs)  76 us
    reduce_sum x2, other arithmetic, attend(): total_sum = total_sum * factor + jnp.sum(weights, axis=-1)  33.1 us
    dot_general x2, matrix products, attend(): jnp.einsum('kgqs,skd->kgqd', weights.astype(jnp.bfloat16), values_flat, p...  29.6 us
    dot_general x2, matrix products, attend(): jnp.einsum('kgqd,skd->kgqs', queries, keys_flat, preferred_element_type=j...  28.5 us
    unnamed x48, local copies, waits for them, and re-layouts  20.5 us
    ppermute x10, starting transfers between devices, shift(): return lax.ppermute(x, dp_axes, perm=pairs)  17.4 us
    all_to_all x1, waiting for transfers between devices, relayout(): lax.all_to_all(packed, ('dz', 'dc'), split_axis=0, concat_axis=0, tiled=T...  12.8 us
  transfers between devices with their start and end apart: 14, of which 7 were waited for; matrix products, arithmetic and copies ran while one was open for 42% of the time, Pallas kernels for 0%

profile of v3, /device:TPU:1, one launch (start us, length us, event | category | flops | bytes accessed | tf_op | source)
XLA Modules:
  0.0 447.2 jit_solution(8612869591227943510)
XLA Ops:
  7.2 1.5 copy.65
  9.7 1.0 copy.66
  10.7 1.0 copy.67
  11.7 1.3 pad_maximum_fusion.1
  13.1 2.1 collective-permute-start.4
  15.2 1.6 collective-permute-start
  16.8 2.1 collective-permute-start.1
  18.9 25.8 %collective-permute-done.4 = bf16[512,1344]{0,1:T(8,128)(2,1)S(1)} collective-permute-done((bf16[512,1344]{0,1:T(8,128)(2,1)S(1)}, bf16[512,1344]{0,1:T(8,128)(2,1)S(1)}, u32[]{:S(2)}, u32[]{:S(2)}) %collective-permute-start.4) | collective-permute-done | bytes 1376288 | tf_op jit(solution)/shard_map/ppermute | solution.py:164
  44.7 1.9 collective-permute-start.5
  46.6 2.0 collective-permute-done
  48.7 2.7 collective-permute-start.6
  51.5 1.2 constant_dynamic-update-slice_fusion.8
  52.7 1.2 constant_dynamic-update-slice_fusion.7
  53.9 38.6 %collective-permute-done.2 = bf16[256,1344]{0,1:T(8,128)(2,1)S(1)} collective-permute-done((bf16[256,1344]{0,1:T(8,128)(2,1)S(1)}, bf16[256,1344]{0,1:T(8,128)(2,1)S(1)}, u32[]{:S(2)}, u32[]{:S(2)}) %collective-permute-start.2) | collective-permute-done | bytes 688160 | tf_op jit(solution)/shard_map/ppermute | solution.py:164
  95.1 1.2 constant_dynamic-update-slice_fusion.4
  96.4 3.2 collective-permute-start.8
  99.6 1.3 constant_dynamic-update-slice_fusion.3
  100.9 1.3 constant_dynamic-update-slice_fusion.2
  102.1 9.3 %collective-permute-done.7 = bf16[256,1344]{0,1:T(8,128)(2,1)S(1)} collective-permute-done((bf16[256,1344]{0,1:T(8,128)(2,1)S(1)}, bf16[256,1344]{0,1:T(8,128)(2,1)S(1)}, u32[]{:S(2)}, u32[]{:S(2)}) %collective-permute-start.7) | collective-permute-done | bytes 688160 | tf_op jit(solution)/shard_map/ppermute | solution.py:164
  112.4 1.0 constant_dynamic-update-slice_fusion
  113.3 3.2 collective-permute-start.9
  116.6 3.4 broadcast_in_dim.202
  120.1 6.5 %all-to-all-start = ((bf16[8,384,1024]{2,1,0:T(8,128)(2,1)}), bf16[8,384,1024]{2,1,0:T(8,128)(2,1)}, u32[]{:S(2)}, u32[]{:S(2)}) async-start(bf16[8,384,1024]{2,1,0:T(8,128)(2,1)} %broadcast_in_dim.202), calls=%async_computation | async-start | bytes 12582912 | tf_op jit(solution)/shard_map/all_to_all | solution.py:152
  129.4 84.7 %all-to-all-done = bf16[8,384,1024]{2,1,0:T(8,128)(2,1)} async-done(((bf16[8,384,1024]{2,1,0:T(8,128)(2,1)}), bf16[8,384,1024]{2,1,0:T(8,128)(2,1)}, u32[]{:S(2)}, u32[]{:S(2)}) %all-to-all-start) | async-done | bytes 6291488 | tf_op jit(solution)/shard_map/all_to_all | solution.py:152
  214.1 5.8 %all-to-all-start.1 = ((bf16[16,2,1]{1,2,0:T(2,128)(2,1)}), bf16[16,2,1]{1,2,0:T(2,128)(2,1)S(1)}, u32[]{:S(2)}, u32[]{:S(2)}) async-start(bf16[16,2,1]{1,2,0:T(2,128)(2,1)} %reshape.573), calls=%async_computation.1 | async-start | bytes 16384 | tf_op jit(solution)/shard_map/all_to_all | solution.py:115
  220.4 4.1 fusion.9
  224.5 4.8 %fusion.11 = bf16[8,384,1024]{2,1,0:T(8,128)(2,1)S(1)} fusion(bf16[8,384,1024]{2,1,0:T(8,128)(2,1)} %all-to-all-done, f32[8,1024]{1,0:T(8,128)S(1)} %reshape.528, f32[384]{0:T(512)S(1)} %add_rsqrt_fusion), kind=kLoop, calls=%fused_computation.20 | loop fusion | flops 12582912 | bytes 12617216 | tf_op jit(solution)/shard_map/convert_element_type | solution.py:193
  230.1 3.1 pad_maximum_fusion
  233.2 3.5 gather_fusion.3
  236.8 5.2 %gather_fusion.2 = bf16[8,384,512]{2,1,0:T(8,128)(2,1)} fusion(bf16[16,384,512]{2,1,0:T(8,128)(2,1)} %bitcast.85, s32[1024]{0:T(1024)S(1)} %pad_clamp_fusion.3), kind=kCustom, calls=%fused_computation.clone | custom fusion | bytes 6291488 | tf_op jit(solution)/shard_map/jit(_take)/gather | solution.py:199
  242.0 5.2 %select_bitcast_fusion = (bf16[384,8,512]{2,0,1:T(8,128)(2,1)}, bf16[384,8,512]{2,0,1:T(8,128)(2,1)}) fusion(bf16[8,384,512]{2,1,0:T(8,128)(2,1)S(1)} %gather_fusion.3, pred[8]{0:T(512)(128)(4,1)S(1)} %get-tuple-element.23, bf16[8,384,512]{2,1,0:T(8,128)(2,1)} %gather_fusion.2, pred[8]{0:T(512)(128)(4,1)S(1)} %get-tuple-element.46), kind=kLoop, calls=%fused_computation.28 | loop fusion | flops 3145728 | bytes 12582928 | tf_op jit(solution)/shard_map/transpose | solution.py:200
  247.1 5.0 %copy.69 = bf16[384,8,512]{0,2,1:T(8,128)(2,1)} copy(bf16[384,8,512]{2,0,1:T(8,128)(2,1)} %get-tuple-element.51) | data formatting | bytes 6291456 | tf_op jit(solution)/shard_map/transpose | solution.py:200
  252.2 2.8 copy.64
  254.9 9.7 %fusion.46 = f32[384,1344]{0,1:T(8,128)S(1)} fusion(bf16[4096,1344]{0,1:T(8,128)(2,1)} %collective-permute-done.9, bf16[384,4096]{0,1:T(8,128)(2,1)} %bitcast.89), kind=kOutput, calls=%fused_computation.142 | convolution fusion | flops 4227858432 | bytes 16220160 | tf_op jit(solution)/shard_map/dot_general | solution.py:202
  264.6 8.7 %convolution_add_fusion = f32[384,1344]{0,1:T(8,128)S(1)} fusion(f32[384,1344]{0,1:T(8,128)S(1)} %fusion.46, bf16[4096,1344]{0,1:T(8,128)(2,1)} %constant_dynamic-update-slice_fusion, bf16[384,4096]{0,1:T(8,128)(2,1)S(1)} %bitcast.90), kind=kOutput, calls=%fused_computation.30 | convolution fusion | flops 4228374528 | bytes 18284544 | tf_op jit(solution)/shard_map/dot_general | solution.py:202
  273.5 1.2 copy-done.5
  275.6 2.1 and_reduce_fusion
  277.6 1.2 compare_and_fusion
  279.4 1.1 slice.93
  282.1 1.6 slice_add_fusion
  283.7 1.3 fusion.44
  285.1 2.7 copy.84
  287.8 2.7 copy.85
  290.6 1.7 copy.71
  292.2 1.1 slice.94
  293.3 1.1 pad_maximum_fusion.2
  294.4 2.0 copy.75
  296.4 2.2 reshape.524
  298.6 1.5 fusion.45
  300.1 1.7 negate_bitcast_fusion
  301.7 1.5 fusion.20
  303.3 10.7 %fusion.3 = (f32[8,384]{1,0:T(8,128)S(1)}, f32[8,384,2048]{2,1,0:T(8,128)}) fusion(pred[384,2048]{1,0:T(8,128)(4,1)S(1)} %copy-done.1, bf16[8,384,128]{2,1,0:T(8,128)(2,1)S(1)} %fusion.20, bf16[2048,128,1]{1,0,2:T(8,128)(2,1)S(1)} %bitcast.91), kind=kOutput, calls=%fused_computation.11 | convolution fusion | flops 1629484032 | bytes 27275264 | tf_op jit(solution)/shard_map/kgqd,skd->kgqs/dot_general | solution.py:69
  314.0 7.2 %gather_fusion = bf16[32,4,2,128,128]{4,3,2,1,0:T(8,128)(2,1)} fusion(bf16[16,4,2,128,128]{4,3,2,1,0:T(8,128)(2,1)} %param.32, s32[1024]{0:T(1024)S(1)} %pad_clamp_fusion.1), kind=kCustom, calls=%fused_computation.2 | custom fusion | bytes 16777344 | tf_op jit(solution)/shard_map/jit(_take)/gather | solution.py:111
  321.2 7.6 %broadcast_select_fusion = bf16[32,4,2,128,128]{4,3,2,1,0:T(8,128)(2,1)} fusion(bf16[32,4,2,128,128]{4,3,2,1,0:T(8,128)(2,1)} %gather_fusion, pred[32]{0:T(512)(128)(4,1)S(1)} %compare_and_fusion.4), kind=kLoop, calls=%fused_computation.24 | loop fusion | flops 4194304 | bytes 16777248 | tf_op jit(solution)/shard_map/jit(_take)/select_n | solution.py:111
  328.8 5.8 %all-to-all-start.2 = ((bf16[32,4,2,128,128]{4,3,2,1,0:T(8,128)(2,1)}), bf16[32,4,2,128,128]{4,3,2,1,0:T(8,128)(2,1)}, u32[]{:S(2)}, u32[]{:S(2)}) async-start(bf16[32,4,2,128,128]{4,3,2,1,0:T(8,128)(2,1)} %broadcast_select_fusion), calls=%async_computation.2 | async-start | bytes 16777216 | tf_op jit(solution)/shard_map/all_to_all | solution.py:114
  334.5 17.8 %fusion = (f32[8,384]{1,0:T(8,128)S(1)}, f32[8,384,3456]{2,1,0:T(8,128)}) fusion(pred[384,3456]{1,0:T(8,128)(4,1)S(1)} %compare_and_fusion, bf16[8,384,128]{2,1,0:T(8,128)(2,1)S(1)} %fusion.20, bf16[6144,256]{0,1:T(8,128)(2,1)} %all-gather.2.cloned.1.call-done, s32[]{:T(128)S(6)} %max.20), kind=kOutput, calls=%fused_computation.6 | convolution fusion | flops 2749756416 | bytes 45477892 | tf_op jit(solution)/shard_map/kgqd,skd->kgqs/dot_general | solution.py:69
  352.3 21.1 %fusion.1 = f32[8,384]{1,0:T(8,128)S(1)} fusion(f32[8,384,3456]{2,1,0:T(8,128)} %get-tuple-element.50, f32[8,384]{1,0:T(8,128)S(1)} %get-tuple-element.40, pred[384,3456]{1,0:T(8,128)(4,1)S(1)} %compare_and_fusion), kind=kLoop, calls=%fused_computation.7 | loop fusion | flops 53081088 | bytes 43819008 | tf_op jit(solution)/shard_map/reduce_sum | solution.py:77
  373.4 12.0 %fusion.7 = f32[8,384]{1,0:T(8,128)S(1)} fusion(f32[8,384,2048]{2,1,0:T(8,128)} %get-tuple-element.48, f32[8,384]{1,0:T(8,128)S(1)} %get-tuple-element.41, pred[384,2048]{1,0:T(8,128)(4,1)S(1)} %copy-done.1), kind=kLoop, calls=%fused_computation.14 | loop fusion | flops 31454208 | bytes 25976832 | tf_op jit(solution)/shard_map/reduce_sum | solution.py:77
  385.5 11.2 %fusion.12 = f32[8,384,128]{1,2,0:T(8,128)S(1)} fusion(bf16[2048,128,1]{1,0,2:T(8,128)(2,1)S(1)} %bitcast.93, f32[8,384,2048]{2,1,0:T(8,128)} %get-tuple-element.48, f32[8,384]{1,0:T(8,128)S(1)} %get-tuple-element.41, pred[384,2048]{1,0:T(8,128)(4,1)S(1)} %copy-done.1), kind=kOutput, calls=%fused_computation.21 | convolution fusion | flops 1642070016 | bytes 28061696 | tf_op jit(solution)/shard_map/kgqs,skd->kgqd/dot_general | solution.py:78
  396.7 18.4 %divide_convert_fusion = bf16[8,384,128]{1,2,0:T(8,128)(2,1)S(1)} fusion(f32[8,384,128]{1,2,0:T(8,128)S(1)} %fusion.12, f32[8,384,3456]{2,1,0:T(8,128)} %get-tuple-element.50, f32[8,384]{1,0:T(8,128)S(1)} %get-tuple-element.40, pred[384,3456]{1,0:T(8,128)(4,1)S(1)} %compare_and_fusion, bf16[6144,256]{0,1:T(8,128)(2,1)} %all-gather.2.cloned.1.call-done, ...), kind=kOutput, calls=%fused_computation.35 | convolution fusion | flops 2772959232 | bytes 47087624 | tf_op jit(solution)/shard_map/kgqs,skd->kgqd/dot_general | solution.py:78
  415.1 1.2 copy.80
  416.3 12.8 %all-to-all-done.2 = bf16[32,4,2,128,128]{4,3,2,1,0:T(8,128)(2,1)} async-done(((bf16[32,4,2,128,128]{4,3,2,1,0:T(8,128)(2,1)}), bf16[32,4,2,128,128]{4,3,2,1,0:T(8,128)(2,1)}, u32[]{:S(2)}, u32[]{:S(2)}) %all-to-all-start.2) | async-done | bytes 8388640 | tf_op jit(solution)/shard_map/all_to_all | solution.py:114
  429.0 6.5 %gather_fusion.1 = bf16[16,4,2,128,128]{4,3,2,1,0:T(8,128)(2,1)} fusion(bf16[32,4,2,128,128]{4,3,2,1,0:T(8,128)(2,1)} %all-to-all-done.2, s32[1024]{0:T(1024)S(1)} %pad_clamp_fusion), kind=kCustom, calls=%fused_computation.3 | custom fusion | bytes 8388672 | tf_op jit(solution)/shard_map/jit(_take)/gather | solution.py:123
  435.5 4.7 %broadcast_select_fusion.1 = bf16[16,4,2,128,128]{4,3,2,1,0:T(8,128)(2,1)} fusion(bf16[16,4,2,128,128]{4,3,2,1,0:T(8,128)(2,1)} %gather_fusion.1, pred[16]{0:T(512)(128)(4,1)S(1)} %compare_and_fusion.5), kind=kLoop, calls=%fused_computation.27 | loop fusion | flops 2097152 | bytes 8388624 | tf_op jit(solution)/shard_map/jit(_take)/select_n | solution.py:123
  (111 shorter events, 12.1 us)
Async XLA Ops:
  13.1 31.7 %collective-permute-start.4 = (bf16[512,1344]{0,1:T(8,128)(2,1)S(1)}, bf16[512,1344]{0,1:T(8,128)(2,1)S(1)}, u32[]{:S(2)}, u32[]{:S(2)}) collective-permute-start(bf16[512,1344]{0,1:T(8,128)(2,1)S(1)} %get-tuple-element.31), channel_id=1, source_target_pairs={{0,16},{8,24},{16,0},{24,8},{32,48},{40,56},{48,32},{56,40},{64,80... | collective-permute-start | bytes 4128776 | tf_op jit(solution)/shard_map/ppermute | solution.py:164
  15.2 33.4 %collective-permute-start = (bf16[512,1344]{0,1:T(8,128)(2,1)S(1)}, bf16[512,1344]{0,1:T(8,128)(2,1)S(1)}, u32[]{:S(2)}, u32[]{:S(2)}) collective-permute-start(bf16[512,1344]{0,1:T(8,128)(2,1)S(1)} %get-tuple-element.31), channel_id=1, source_target_pairs={{0,32},{8,40},{16,48},{24,56},{32,64},{40,72},{48,80},{56,88},{64,... | collective-permute-start | bytes 4128776 | tf_op jit(solution)/shard_map/ppermute | solution.py:164
  16.8 34.5 %collective-permute-start.1 = (bf16[512,1344]{0,1:T(8,128)(2,1)S(1)}, bf16[512,1344]{0,1:T(8,128)(2,1)S(1)}, u32[]{:S(2)}, u32[]{:S(2)}) collective-permute-start(bf16[512,1344]{0,1:T(8,128)(2,1)S(1)} %get-tuple-element.31), channel_id=1, source_target_pairs={{0,96},{8,104},{16,112},{24,120},{32,0},{40,8},{48,16},{56,24},{64... | collective-permute-start | bytes 4128776 | tf_op jit(solution)/shard_map/ppermute | solution.py:164
  44.7 50.0 %collective-permute-start.5 = (bf16[512,1344]{0,1:T(8,128)(2,1)S(1)}, bf16[512,1344]{0,1:T(8,128)(2,1)S(1)}, u32[]{:S(2)}, u32[]{:S(2)}) collective-permute-start(bf16[512,1344]{0,1:T(8,128)(2,1)S(1)} %collective-permute-done.4), channel_id=1, source_target_pairs={{0,32},{8,40},{16,48},{24,56},{32,64},{40,72},{48,80},{56,88},{64,... | collective-permute-start | bytes 4128776 | tf_op jit(solution)/shard_map/ppermute | solution.py:164
  48.6 43.9 %collective-permute-start.2 = (bf16[256,1344]{0,1:T(8,128)(2,1)S(1)}, bf16[256,1344]{0,1:T(8,128)(2,1)S(1)}, u32[]{:S(2)}, u32[]{:S(2)}) collective-permute-start(bf16[256,1344]{0,1:T(8,128)(2,1)S(1)} %slice.84), channel_id=1, source_target_pairs={{0,32},{8,40},{16,48},{24,56},{32,64},{40,72},{48,80},{56,88},{64,... | collective-permute-start | bytes 2064392 | tf_op jit(solution)/shard_map/ppermute | solution.py:164
  48.7 47.7 %collective-permute-start.6 = (bf16[512,1344]{0,1:T(8,128)(2,1)S(1)}, bf16[512,1344]{0,1:T(8,128)(2,1)S(1)}, u32[]{:S(2)}, u32[]{:S(2)}) collective-permute-start(bf16[512,1344]{0,1:T(8,128)(2,1)S(1)} %collective-permute-done.4), channel_id=1, source_target_pairs={{0,96},{8,104},{16,112},{24,120},{32,0},{40,8},{48,16},{56,24},{64... | collective-permute-start | bytes 4128776 | tf_op jit(solution)/shard_map/ppermute | solution.py:164
  51.4 42.4 %collective-permute-start.3 = (bf16[256,1344]{0,1:T(8,128)(2,1)S(1)}, bf16[256,1344]{0,1:T(8,128)(2,1)S(1)}, u32[]{:S(2)}, u32[]{:S(2)}) collective-permute-start(bf16[256,1344]{0,1:T(8,128)(2,1)S(1)} %slice.85), channel_id=1, source_target_pairs={{0,96},{8,104},{16,112},{24,120},{32,0},{40,8},{48,16},{56,24},{64... | collective-permute-start | bytes 2064392 | tf_op jit(solution)/shard_map/ppermute | solution.py:164
  94.8 21.8 %copy-start.6 = (bf16[384,1024]{1,0:T(8,128)(2,1)S(1)}, bf16[384,1024]{1,0:T(8,128)(2,1)}, u32[]{:S(2)}) copy-start(bf16[384,1024]{1,0:T(8,128)(2,1)} %param.18) | copy-start | bytes 2359300
  94.8 16.6 %collective-permute-start.7 = (bf16[256,1344]{0,1:T(8,128)(2,1)S(1)}, bf16[256,1344]{0,1:T(8,128)(2,1)S(1)}, u32[]{:S(2)}, u32[]{:S(2)}) collective-permute-start(bf16[256,1344]{0,1:T(8,128)(2,1)S(1)} %slice.86), channel_id=1, source_target_pairs={{0,32},{8,40},{16,48},{24,56},{32,64},{40,72},{48,80},{56,88},{64,... | collective-permute-start | bytes 2064392 | tf_op jit(solution)/shard_map/ppermute | solution.py:164
  96.4 16.0 %collective-permute-start.8 = (bf16[256,1344]{0,1:T(8,128)(2,1)S(1)}, bf16[256,1344]{0,1:T(8,128)(2,1)S(1)}, u32[]{:S(2)}, u32[]{:S(2)}) collective-permute-start(bf16[256,1344]{0,1:T(8,128)(2,1)S(1)} %slice.87), channel_id=1, source_target_pairs={{0,96},{8,104},{16,112},{24,120},{32,0},{40,8},{48,16},{56,24},{64... | collective-permute-start | bytes 2064392 | tf_op jit(solution)/shard_map/ppermute | solution.py:164
  113.3 141.6 %collective-permute-start.9 = (bf16[4096,1344]{0,1:T(8,128)(2,1)}, bf16[4096,1344]{0,1:T(8,128)(2,1)}, u32[]{:S(2)}, u32[]{:S(2)}) collective-permute-start(bf16[4096,1344]{0,1:T(8,128)(2,1)} %constant_dynamic-update-slice_fusion), channel_id=1, source_target_pairs={{0,8},{8,0},{16,24},{24,16},{32,40},{40,32},{48,56},{56,48},{64,72... | collective-permute-start | bytes 33030152 | tf_op jit(solution)/shard_map/ppermute | solution.py:164
  120.0 6.6 %copy-start.7 = (bf16[8192]{0:T(1024)(128)(2,1)S(1)}, bf16[8192]{0:T(1024)(128)(2,1)}, u32[]{:S(2)}) copy-start(bf16[8192]{0:T(1024)(128)(2,1)} %param.19) | copy-start | bytes 49156
  120.0 6.6 %copy-start.13 = (bf16[128]{0:T(256)(128)(2,1)S(1)}, bf16[128]{0:T(256)(128)(2,1)}, u32[]{:S(2)}) copy-start(bf16[128]{0:T(256)(128)(2,1)} %param.24) | copy-start | bytes 772
  120.0 6.6 %copy-start.15 = (s32[3]{0:T(128)S(1)}, s32[3]{0:T(128)}, u32[]{:S(2)}) copy-start(s32[3]{0:T(128)} %param.26) | copy-start | bytes 40
  120.0 6.8 %copy-start.14 = (bf16[128]{0:T(256)(128)(2,1)S(1)}, bf16[128]{0:T(256)(128)(2,1)}, u32[]{:S(2)}) copy-start(bf16[128]{0:T(256)(128)(2,1)} %param.25) | copy-start | bytes 772
  120.0 6.8 %copy-start.10 = (bf16[1024]{0:T(1024)(128)(2,1)S(1)}, bf16[1024]{0:T(1024)(128)(2,1)}, u32[]{:S(2)}) copy-start(bf16[1024]{0:T(1024)(128)(2,1)} %param.23) | copy-start | bytes 6148
  120.1 7.0 %copy-start.11 = (s32[16,1]{0,1:T(1,128)S(1)}, s32[16,1]{0,1:T(1,128)}, u32[]{:S(2)}) copy-start(s32[16,1]{0,1:T(1,128)} %param.33) | copy-start | bytes 196
  120.1 8.2 %copy-start.8 = (s32[4,4]{1,0:T(4,128)S(1)}, s32[4,4]{1,0:T(4,128)}, u32[]{:S(2)}) copy-start(s32[4,4]{1,0:T(4,128)} %param.29) | copy-start | bytes 196
  120.1 8.6 %copy-start.12 = (s32[3]{0:T(128)S(1)}, s32[3]{0:T(128)}, u32[]{:S(2)}) copy-start(s32[3]{0:T(128)} %param.27) | copy-start | bytes 40
  120.1 8.7 %copy-start.9 = (s32[4]{0:T(128)S(1)}, s32[4]{0:T(128)}, u32[]{:S(2)}) copy-start(s32[4]{0:T(128)} %param.28) | copy-start | bytes 52
  120.1 94.0 %all-to-all-start = ((bf16[8,384,1024]{2,1,0:T(8,128)(2,1)}), bf16[8,384,1024]{2,1,0:T(8,128)(2,1)}, u32[]{:S(2)}, u32[]{:S(2)}) async-start(bf16[8,384,1024]{2,1,0:T(8,128)(2,1)} %broadcast_in_dim.202), calls=%async_computation | async-start | bytes 12582912 | tf_op jit(solution)/shard_map/all_to_all | solution.py:152
  214.1 64.7 %all-to-all-start.1 = ((bf16[16,2,1]{1,2,0:T(2,128)(2,1)}), bf16[16,2,1]{1,2,0:T(2,128)(2,1)S(1)}, u32[]{:S(2)}, u32[]{:S(2)}) async-start(bf16[16,2,1]{1,2,0:T(2,128)(2,1)} %reshape.573), calls=%async_computation.1 | async-start | bytes 16384 | tf_op jit(solution)/shard_map/all_to_all | solution.py:115
  219.9 94.1 %all-gather.2.cloned.1.call-start = ((), (), s32[]{:S(2)}) async-start(), calls=%async_computation.3 | async-start | bytes 3342336 | tf_op jit(solution)/shard_map/all_gather | solution.py:220
  247.1 5.0 %copy-start = (bf16[384,8,512]{2,0,1:T(8,128)(2,1)S(1)}, bf16[384,8,512]{2,0,1:T(8,128)(2,1)}, u32[]{:S(2)}) copy-start(bf16[384,8,512]{2,0,1:T(8,128)(2,1)} %get-tuple-element.52) | copy-start | bytes 9437188
  254.9 9.7 %copy-start.4 = (bf16[384,8,512]{0,2,1:T(8,128)(2,1)S(1)}, bf16[384,8,512]{0,2,1:T(8,128)(2,1)}, u32[]{:S(2)}) copy-start(bf16[384,8,512]{0,2,1:T(8,128)(2,1)} %copy.64) | copy-start | bytes 9437188
  273.3 1.3 copy-start.5
  298.6 3.1 copy-start.2
  298.6 3.1 copy-start.3
  298.6 4.7 %copy-start.1 = (pred[384,2048]{1,0:T(8,128)(4,1)S(1)}, pred[384,2048]{1,0:T(8,128)(4,1)}, u32[]{:S(2)}) copy-start(pred[384,2048]{1,0:T(8,128)(4,1)} %and_reduce_fusion) | copy-start | bytes 2359300
  328.8 100.2 %all-to-all-start.2 = ((bf16[32,4,2,128,128]{4,3,2,1,0:T(8,128)(2,1)}), bf16[32,4,2,128,128]{4,3,2,1,0:T(8,128)(2,1)}, u32[]{:S(2)}, u32[]{:S(2)}) async-start(bf16[32,4,2,128,128]{4,3,2,1,0:T(8,128)(2,1)} %broadcast_select_fusion), calls=%async_computation.2 | async-start | bytes 16777216 | tf_op jit(solution)/shard_map/all_to_all | solution.py:114
Sparse Core Ops, SparseCore 0:
  275.6 36.2 all-gather.1

commit v4 on v2

--- a/solution.py
+++ b/solution.py
@@ -1,12 +1,17 @@
+import functools
 import math
 
 import jax
 import jax.numpy as jnp
 from jax import lax
+from jax.experimental import pallas as pl
+from jax.experimental.pallas import tpu as pltpu
 from jax.sharding import Mesh, PartitionSpec as P
 
 HD = 128
 CAP = 2
+Q_TILE = 1024
+K_TILE = 512
 MAX_REQUEST = 3072
 
 
@@ -81,6 +86,64 @@
         preferred_element_type=jnp.float32,
     )
     return (new_best, total_sum, accumulated)
+
+
+def flash_kernel(flags, grp_ref, lo_ref, hi_ref, tag_ref, key_row_ref, q_ref, k_ref, v_ref,
+                 o_ref, acc, m_sc, l_sc, *, scale):
+    qi = pl.program_id(0)
+    kj = pl.program_id(1)
+
+    @pl.when(kj == 0)
+    def _():
+        m_sc[...] = jnp.full(m_sc.shape, NEG_BIG, jnp.float32)
+        l_sc[...] = jnp.zeros(l_sc.shape, jnp.float32)
+        acc[...] = jnp.zeros(acc.shape, jnp.float32)
+
+    @pl.when(flags[qi, kj] > 0)
+    def _():
+        s = lax.dot_general(q_ref[...], k_ref[...], (((1,), (1,)), ((), ())),
+                            preferred_element_type=jnp.float32) * scale
+        tag = tag_ref[0:1, :]
+        key_row = key_row_ref[0:1, :]
+        allowed = (tag == grp_ref[...]) | ((key_row >= lo_ref[...]) & (key_row <= hi_ref[...]))
+        s = jnp.where(allowed, s, NEG_BIG)
+        m_prev = m_sc[:, 0:1]
+        m_new = jnp.maximum(m_prev, jnp.max(s, axis=1, keepdims=True))
+        p = jnp.where(allowed, jnp.exp(s - m_new), 0.0)
+        alpha = jnp.exp(m_prev - m_new)
+        l_sc[...] = jnp.broadcast_to(alpha * l_sc[:, 0:1] + jnp.sum(p, axis=1, keepdims=True), l_sc.shape)
+        m_sc[...] = jnp.broadcast_to(m_new, m_sc.shape)
+        acc[...] = acc[...] * alpha + jnp.dot(p.astype(jnp.bfloat16), v_ref[...],
+                                              preferred_element_type=jnp.float32)
+
+    @pl.when(kj == pl.num_programs(1) - 1)
+    def _():
+        o_ref[...] = (acc[...] / l_sc[:, 0:1]).astype(o_ref.dtype)
+
+
+def flash(q, k, v, grp, lo, hi, tag, key_row, flags, tq, tk, scale):
+    rows, hd = q.shape
+    keys = k.shape[0]
+    nq, nk = rows // tq, keys // tk
+    row_spec = pl.BlockSpec((tq, 1), lambda i, j, f: (i, 0))
+    key_spec = pl.BlockSpec((1, tk), lambda i, j, f: (0, j))
+    grid_spec = pltpu.PrefetchScalarGridSpec(
+        num_scalar_prefetch=1,
+        grid=(nq, nk),
+        in_specs=[row_spec, row_spec, row_spec, key_spec, key_spec,
+                  pl.BlockSpec((tq, hd), lambda i, j, f: (i, 0)),
+                  pl.BlockSpec((tk, hd), lambda i, j, f: (j, 0)),
+                  pl.BlockSpec((tk, hd), lambda i, j, f: (j, 0))],
+        out_specs=pl.BlockSpec((tq, hd), lambda i, j, f: (i, 0)),
+        scratch_shapes=[pltpu.VMEM((tq, hd), jnp.float32),
+                        pltpu.VMEM((tq, 128), jnp.float32),
+                        pltpu.VMEM((tq, 128), jnp.float32)],
+    )
+    return pl.pallas_call(
+        functools.partial(flash_kernel, scale=scale),
+        grid_spec=grid_spec,
+        out_shape=jax.ShapeDtypeStruct((rows, hd), jnp.bfloat16),
+    )(flags, grp, lo, hi, tag, key_row, q, k, v)
 
 
 def dp_index():
@@ -181,7 +244,7 @@
     local_kv = key_proj.shape[1] // HD
     group_size = local_heads // local_kv
     queries = rotary(query_proj.reshape(row_count, local_heads, HD), positions).astype(jnp.bfloat16)
-    queries = queries.reshape(row_count, local_kv, group_size, HD).transpose(1, 2, 0, 3)
+    queries = queries.reshape(row_count * local_heads, HD)
     keys_new = (
         rotary(key_proj.reshape(row_count, local_kv, HD), positions)
         .astype(jnp.bfloat16)
@@ -193,37 +256,69 @@
     prev_cache, span_all = lax.optimization_barrier((prev_cache, span_all))
     decode_cache = relayout(prev_cache, dest_device)
     score_scale = HD ** (-0.5)
-    carried = (
-        jnp.full((local_kv, group_size, row_count), NEG_BIG, jnp.float32),
-        jnp.zeros((local_kv, group_size, row_count), jnp.float32),
-        jnp.zeros((local_kv, group_size, row_count, HD), jnp.float32),
-    )
     block_size = pool_all.shape[1]
     blocks_here = pool_all.shape[0]
     kv_width = local_kv * HD
-    allowed_group = prompt_mask(prompt_table, prompt_lens, blocks_here, block_size)
-    allowed = jnp.any(group_hot[:, :, None] & allowed_group[None, :, :], axis=1)
-    keys_flat = pool_all[:, :, :kv_width].reshape(blocks_here * block_size, local_kv, HD)
-    values_flat = pool_all[:, :, kv_width:].reshape(blocks_here * block_size, local_kv, HD)
-    carried = attend(carried, queries, keys_flat, values_flat, allowed, score_scale)
     key_count = span_all.shape[0]
     window = min(key_count, MAX_REQUEST + row_count)
-    window = -(-window // row_count) * row_count
+    window = -(-window // K_TILE) * K_TILE
     window_start = jnp.maximum((me + 1) * row_count - window, 0)
     span_window = lax.dynamic_slice_in_dim(span_all, window_start, window, axis=0)
-    key_rows = window_start + jnp.arange(window, dtype=jnp.int32)
-    key_request = request_index(key_rows, ends_at)
-    span_allowed = (request_of[:, None] == key_request[None, :]) & (
-        key_rows[None, :] <= global_rows[:, None]
-    )
-    span_keys_flat = span_window[:, :kv_width].reshape(window, local_kv, HD)
-    span_values_flat = span_window[:, kv_width:].reshape(window, local_kv, HD)
-    carried = attend(
-        carried, queries, span_keys_flat, span_values_flat, span_allowed, score_scale
-    )
-    best_score, total_sum, accumulated = carried
-    output = accumulated / total_sum[..., None]
-    context = output.transpose(2, 0, 1, 3).reshape(row_count, local_heads * HD).astype(jnp.bfloat16)
+    pool_flat = pool_all.reshape(blocks_here * block_size, 2 * kv_width)
+    all_keys = jnp.concatenate([pool_flat[:, :kv_width], span_window[:, :kv_width]], axis=0)
+    all_values = jnp.concatenate([pool_flat[:, kv_width:], span_window[:, kv_width:]], axis=0)
+    blocks = jnp.arange(blocks_here, dtype=jnp.int32)
+    matching = prompt_table[:, :, None] == blocks[None, None, :]
+    slot_no = jnp.sum(
+        jnp.where(matching, jnp.arange(prompt_table.shape[1], dtype=jnp.int32)[None, :, None], 0),
+        axis=(0, 1),
+    )
+    group_no = jnp.sum(
+        jnp.where(matching, jnp.arange(prompt_table.shape[0], dtype=jnp.int32)[:, None, None], 0),
+        axis=(0, 1),
+    )
+    named = jnp.any(matching, axis=(0, 1))
+    within = slot_no[:, None] * block_size + jnp.arange(block_size, dtype=jnp.int32)[None, :]
+    block_len = jnp.take(prompt_lens, group_no)
+    pool_tag = jnp.where(named[:, None] & (within < block_len[:, None]), group_no[:, None], -1)
+    key_tag = jnp.concatenate(
+        [pool_tag.reshape(-1), jnp.full((window,), -2, jnp.int32)]
+    )
+    key_row = jnp.concatenate(
+        [
+            jnp.full((blocks_here * block_size,), -1, jnp.int32),
+            window_start + jnp.arange(window, dtype=jnp.int32),
+        ]
+    )
+    starts_at = ends_at - request_lens
+    token_group = jnp.take(request_group, request_of)
+    token_start = jnp.take(starts_at, request_of)
+    seen = (key_tag[None, :] == token_group[:, None]) | (
+        (key_row[None, :] >= token_start[:, None]) & (key_row[None, :] <= global_rows[:, None])
+    )
+    q_tokens = Q_TILE // local_heads
+    flags = jnp.any(
+        seen.reshape(row_count // q_tokens, q_tokens, -1, K_TILE), axis=(1, 3)
+    ).astype(jnp.int32)
+
+    def per_row(x):
+        return jnp.repeat(x, local_heads)[:, None]
+
+    output = flash(
+        queries,
+        all_keys,
+        all_values,
+        per_row(token_group),
+        per_row(token_start),
+        per_row(global_rows),
+        key_tag[None, :],
+        key_row[None, :],
+        flags,
+        Q_TILE,
+        K_TILE,
+        score_scale,
+    )
+    context = output.reshape(row_count, local_heads * HD)
     return (context, decode_cache)
 
 

time: 392 us -> 401 us (1.023); the launches traced: 386 us -> 404 us
  Pallas kernels: 0 us -> 68.7 us
  matrix products: 75.6 us -> 17.7 us
  other arithmetic: 64.3 us -> 41.2 us
  waiting for transfers between devices: 177 us -> 200 us
  local copies, waits for them, and re-layouts: 36.1 us -> 43.3 us
    pallas_call x0 -> x1, Pallas kernels: none -> 68.7 us  [flash(): pl.pallas_call(functools.partial(flash_kernel, scale=scale), grid_spec=gr...]
    dot_general x4 -> x0, matrix products: 58.3 us -> none  [the longest x2 29.6 us: attend(): jnp.einsum('kgqs,skd->kgqd', weights.astype(jnp.bfloat16), values_flat, p...]
    reduce_sum x3 -> x1, other arithmetic: 33.2 us -> 0.09 us  [per_device(): jnp.sum(jnp.where(matching, jnp.arange(prompt_table.shape[1], dtype=jnp.i...]
    all_gather x1, waiting for transfers between devices: 0.82 us -> 27 us  [per_device(): span_all = lax.all_gather(span_here, ('dz', 'dc'), axis=0, tiled=True)]
    all_to_all x1, waiting for transfers between devices: 10.4 us -> 0.01 us  [relayout(): lax.all_to_all(packed, ('dz', 'dc'), split_axis=0, concat_axis=0, tiled=T...]
    all_gather x1, waiting for transfers between devices: 79 us -> 85.6 us  [per_device(): weights_all = lax.all_gather(weights_here, ('dz', 'dc'), axis=0, tiled=True)]
    another operation x0 -> x4, local copies, waits for them, and re-layouts: none -> 6.21 us  [the longest x3 4.85 us: per_row(): return jnp.repeat(x, local_heads)[:, None]]
  transfers between devices with their start and end apart: 5 -> 5, of which waited for: 4 -> 3; matrix products, arithmetic and copies ran while one was open for 38% -> 16% of each run, Pallas kernels for 0% -> 17%
where the time goes in v4:
time: 401 us; the launch traced here: 404 us
  waiting for transfers between devices  200 us (50%)
  Pallas kernels  68.7 us (17%)
  local copies, waits for them, and re-layouts  43.3 us (11%)
  other arithmetic  41.2 us (10%)
  starting transfers between devices  18.7 us (5%)
  matrix products  17.7 us (4%)
  between operations  14.4 us (4%)
    all_to_all x1, waiting for transfers between devices, per_device(): lax.all_to_all(spread, 'mp', split_axis=0, concat_axis=0, tiled=True)  87.1 us
    all_gather x1, waiting for transfers between devices, per_device(): weights_all = lax.all_gather(weights_here, ('dz', 'dc'), axis=0, tiled=True)  85.6 us
    pallas_call x1, Pallas kernels, flash(): pl.pallas_call(functools.partial(flash_kernel, scale=scale), grid_spec=gr...  68.7 us
    all_gather x1, waiting for transfers between devices, per_device(): span_all = lax.all_gather(span_here, ('dz', 'dc'), axis=0, tiled=True)  27 us
    dot_general x1, matrix products, per_device(): jnp.einsum('jtf,jfc->tc', normed, weights_all.reshape(mp_size, -1, weight...  17.7 us
  transfers between devices with their start and end apart: 5, of which 3 were waited for; matrix products, arithmetic and copies ran while one was open for 16% of the time, Pallas kernels for 17%

profile of v4, /device:TPU:104, one launch (start us, length us, event | category | flops | bytes accessed | tf_op | source)
XLA Modules:
  0.0 404.0 jit_solution(3710936664971262139)
XLA Ops:
  7.2 0.8 pad_maximum_fusion.6
  8.1 0.1 reshape.305
  8.2 2.6 pad_maximum_fusion
  10.8 3.4 broadcast_in_dim.195
  14.3 6.2 %all-to-all-start = ((bf16[8,384,1024]{2,1,0:T(8,128)(2,1)}), bf16[8,384,1024]{2,1,0:T(8,128)(2,1)}, u32[]{:S(2)}, u32[]{:S(2)}) async-start(bf16[8,384,1024]{2,1,0:T(8,128)(2,1)} %broadcast_in_dim.195), calls=%async_computation | async-start | bytes 12582912 | tf_op jit(solution)/shard_map/all_to_all | solution.py:216
  20.6 0.6 convert_element_type.80
  21.2 0.2 reduce-window.16
  21.7 0.8 multiply_cosine_fusion
  22.4 87.1 %all-to-all-done = bf16[8,384,1024]{2,1,0:T(8,128)(2,1)} async-done(((bf16[8,384,1024]{2,1,0:T(8,128)(2,1)}), bf16[8,384,1024]{2,1,0:T(8,128)(2,1)}, u32[]{:S(2)}, u32[]{:S(2)}) %all-to-all-start) | async-done | bytes 6291488 | tf_op jit(solution)/shard_map/all_to_all | solution.py:216
  109.6 4.3 %fusion = f32[384]{0:T(512)S(1)} fusion(bf16[8,384,1024]{2,1,0:T(8,128)(2,1)} %all-to-all-done), kind=kLoop, calls=%fused_computation.5 | loop fusion | flops 9436800 | bytes 6292992 | tf_op jit(solution)/shard_map/reduce_sum | solution.py:229
  113.9 85.6 %all-gather.3.cloned.1.call-done = bf16[8192,1344]{1,0:T(8,128)(2,1)} async-done(((bf16[512,1344]{1,0:T(8,128)(2,1)}), bf16[8192,1344]{1,0:T(8,128)(2,1)}) %all-gather.3.cloned.1.call-update) | async-done | bytes 22020112 | tf_op jit(solution)/shard_map/all_gather | solution.py:222
  199.5 17.7 %fusion.7 = f32[384,1344]{0,1:T(8,128)S(1)} fusion(bf16[8,1024,1344]{2,1,0:T(8,128)(2,1)} %bitcast.48, bf16[8,384,1024]{2,1,0:T(8,128)(2,1)} %all-to-all-done, f32[8,1024]{1,0:T(8,128)S(1)} %reshape.311, f32[384]{0:T(512)S(1)} %add_rsqrt_fusion), kind=kOutput, calls=%fused_computation.14 | convolution fusion | flops 8468299776 | bytes 30410240 | tf_op jit(solution)/shard_map/jtf,jfc->tc/dot_general | solution.py:234
  217.3 0.1 copy.63
  217.5 0.9 fusion.12
  218.4 0.1 copy.64
  218.5 1.2 fusion.14
  219.7 0.7 pad_maximum_fusion.5
  220.4 0.9 convert_reduce_fusion
  221.4 0.7 fusion.20
  222.1 0.7 reshape.367
  222.8 5.4 %all-to-all-start.1 = ((bf16[16,2,1]{1,2,0:T(2,128)(2,1)}), bf16[16,2,1]{1,2,0:T(2,128)(2,1)S(1)}, u32[]{:S(2)}, u32[]{:S(2)}) async-start(bf16[16,2,1]{1,2,0:T(2,128)(2,1)} %reshape.367), calls=%async_computation.1 | async-start | bytes 16384 | tf_op jit(solution)/shard_map/all_to_all | solution.py:177
  228.2 0.7 select_reduce_fusion
  229.0 27.0 %all-gather.5.cloned.1.call-done = bf16[6144,256]{1,0:T(8,128)(2,1)} async-done(((bf16[384,256]{1,0:T(8,128)(2,1)}), bf16[6144,256]{1,0:T(8,128)(2,1)}) %all-gather.5.cloned.1.call-update) | async-done | bytes 3145744 | tf_op jit(solution)/shard_map/all_gather | solution.py:255
  256.1 7.1 %gather_fusion.1 = bf16[32,4,2,128,128]{4,3,2,1,0:T(8,128)(2,1)} fusion(bf16[16,4,2,128,128]{4,3,2,1,0:T(8,128)(2,1)} %param.32, s32[1024]{0:T(1024)S(1)} %pad_clamp_fusion.1), kind=kCustom, calls=%fused_computation.1 | custom fusion | bytes 16777344 | tf_op jit(solution)/shard_map/jit(_take)/gather | solution.py:173
  263.2 7.5 %broadcast_select_fusion = bf16[32,4,2,128,128]{4,3,2,1,0:T(8,128)(2,1)} fusion(bf16[32,4,2,128,128]{4,3,2,1,0:T(8,128)(2,1)} %gather_fusion.1, pred[32]{0:T(512)(128)(4,1)S(1)} %compare_and_fusion.2), kind=kLoop, calls=%fused_computation.9 | loop fusion | flops 4194304 | bytes 16777248 | tf_op jit(solution)/shard_map/jit(_take)/select_n | solution.py:173
  270.7 7.0 %all-to-all-start.2 = ((bf16[32,4,2,128,128]{4,3,2,1,0:T(8,128)(2,1)}), bf16[32,4,2,128,128]{4,3,2,1,0:T(8,128)(2,1)}, u32[]{:S(2)}, u32[]{:S(2)}) async-start(bf16[32,4,2,128,128]{4,3,2,1,0:T(8,128)(2,1)} %broadcast_select_fusion), calls=%async_computation.2 | async-start | bytes 16777216 | tf_op jit(solution)/shard_map/all_to_all | solution.py:176
  277.9 0.7 gather_fusion
  278.7 0.6 broadcast_in_dim.193.tag_ref
  279.4 0.6 broadcast_in_dim.194.key_row_ref
  280.0 0.7 fusion.29
  280.7 0.6 fusion.28
  281.3 1.9 select_select_fusion.1
  283.2 1.9 select_select_fusion
  285.1 3.7 or_reduce_fusion
  288.8 0.6 convert_element_type.72.flags
  289.4 0.1 broadcast_in_dim.190
  289.5 1.6 broadcast_in_dim_reshape.12.grp_ref
  291.2 0.1 broadcast_in_dim.191
  291.3 1.6 broadcast_in_dim_reshape.13.lo_ref
  292.9 0.1 broadcast_in_dim.192
  293.0 1.6 broadcast_in_dim_reshape.14.hi_ref
  294.9 0.1 add_reduce_fusion
  295.0 0.1 select_reduce_fusion.1
  295.2 1.6 slice_add_fusion
  296.8 0.5 copy.49
  297.3 1.3 fusion.26
  298.6 2.8 copy.62
  301.4 1.6 copy.61
  303.1 1.4 reshape.307
  304.5 1.7 slice.71
  306.2 1.4 reshape_reshape.3
  307.7 1.3 copy-done.1
  309.0 0.1 negate_bitcast_fusion
  309.1 0.4 copy-done.2
  309.5 0.5 copy-done.3
  309.9 1.4 fusion.11.q_ref
  311.3 0.8 copy-done.6
  312.1 0.6 fusion.24
  312.7 1.2 pad_maximum_fusion.1.k_ref
  313.9 1.2 pad_maximum_fusion.2.v_ref
  315.1 68.7 %shard_map.167 = bf16[3072,128]{1,0:T(8,128)(2,1)} custom-call(s32[3,11]{1,0:T(4,128)} %convert_element_type.72.flags, s32[3072,1]{1,0:T(8,128)} %broadcast_in_dim_reshape.12.grp_ref, s32[3072,1]{1,0:T(8,128)} %broadcast_in_dim_reshape.13.lo_ref, s32[3072,1]{1,0:T(8,128)} %broadcast_in_dim_reshape.14.hi_ref, s32[1,5632]{1,0:T(1,128)} %broadcast_in_dim.193.tag_ref, ...), custom_call_target="tpu_custom_call" | custom-call | tf_op jit(solution)/shard_map/pallas_call | solution.py:142
  383.9 2.1 reshape.310
  386.0 6.5 %gather_fusion.2 = bf16[16,4,2,128,128]{4,3,2,1,0:T(8,128)(2,1)} fusion(bf16[32,4,2,128,128]{4,3,2,1,0:T(8,128)(2,1)} %all-to-all-done.2, s32[1024]{0:T(1024)S(1)} %pad_clamp_fusion), kind=kCustom, calls=%fused_computation.2 | custom fusion | bytes 8388672 | tf_op jit(solution)/shard_map/jit(_take)/gather | solution.py:185
  392.5 4.7 %broadcast_select_fusion.1 = bf16[16,4,2,128,128]{4,3,2,1,0:T(8,128)(2,1)} fusion(bf16[16,4,2,128,128]{4,3,2,1,0:T(8,128)(2,1)} %gather_fusion.2, pred[16]{0:T(512)(128)(4,1)S(1)} %compare_and_fusion.3), kind=kLoop, calls=%fused_computation.13 | loop fusion | flops 2097152 | bytes 8388624 | tf_op jit(solution)/shard_map/jit(_take)/select_n | solution.py:185
  (73 shorter events, 1.3 us)
Async XLA Ops:
  7.2 3.6 copy-start.7
  7.2 192.4 %all-gather.3.cloned.1.call-start = ((), (), s32[]{:S(2)}) async-start(), calls=%async_computation.3 | async-start | bytes 24510464 | tf_op jit(solution)/shard_map/all_gather | solution.py:222
  14.3 6.3 %copy-start.8 = (bf16[8192]{0:T(1024)(128)(2,1)S(1)}, bf16[8192]{0:T(1024)(128)(2,1)}, u32[]{:S(2)}) copy-start(bf16[8192]{0:T(1024)(128)(2,1)} %param.19) | copy-start | bytes 49156
  14.3 6.3 %copy-start.13 = (bf16[128]{0:T(256)(128)(2,1)S(1)}, bf16[128]{0:T(256)(128)(2,1)}, u32[]{:S(2)}) copy-start(bf16[128]{0:T(256)(128)(2,1)} %param.24) | copy-start | bytes 772
  14.3 6.3 %copy-start.14 = (bf16[128]{0:T(256)(128)(2,1)S(1)}, bf16[128]{0:T(256)(128)(2,1)}, u32[]{:S(2)}) copy-start(bf16[128]{0:T(256)(128)(2,1)} %param.25) | copy-start | bytes 772
  14.3 6.9 %copy-start.15 = (s32[3]{0:T(128)S(1)}, s32[3]{0:T(128)}, u32[]{:S(2)}) copy-start(s32[3]{0:T(128)} %param.26) | copy-start | bytes 40
  14.3 7.2 %copy-start.9 = (s32[3]{0:T(128)S(1)}, s32[3]{0:T(128)}, u32[]{:S(2)}) copy-start(s32[3]{0:T(128)} %param.27) | copy-start | bytes 40
  14.3 7.3 %copy-start = (s32[4]{0:T(128)S(1)}, s32[4]{0:T(128)}, u32[]{:S(2)}) copy-start(s32[4]{0:T(128)} %param.28) | copy-start | bytes 52
  14.3 95.3 %all-to-all-start = ((bf16[8,384,1024]{2,1,0:T(8,128)(2,1)}), bf16[8,384,1024]{2,1,0:T(8,128)(2,1)}, u32[]{:S(2)}, u32[]{:S(2)}) async-start(bf16[8,384,1024]{2,1,0:T(8,128)(2,1)} %broadcast_in_dim.195), calls=%async_computation | async-start | bytes 12582912 | tf_op jit(solution)/shard_map/all_to_all | solution.py:216
  20.5 235.6 %all-gather.5.cloned.1.call-start = ((), (), s32[]{:S(2)}) async-start(), calls=%async_computation.4 | async-start | bytes 3342336 | tf_op jit(solution)/shard_map/all_gather | solution.py:255
  20.6 196.9 %copy-start.11 = (f32[128]{0:T(128)}, f32[128]{0:T(128)S(1)}, u32[]{:S(2)}) copy-start(f32[128]{0:T(128)S(1)} %convert_element_type.78) | copy-start | bytes 1540
  217.3 45.9 %copy-start.5 = (f32[384,1344]{0,1:T(8,128)}, f32[384,1344]{0,1:T(8,128)S(1)}, u32[]{:S(2)}) copy-start(f32[384,1344]{0,1:T(8,128)S(1)} %fusion.7) | copy-start | bytes 6193156
  222.8 47.9 %all-to-all-start.1 = ((bf16[16,2,1]{1,2,0:T(2,128)(2,1)}), bf16[16,2,1]{1,2,0:T(2,128)(2,1)S(1)}, u32[]{:S(2)}, u32[]{:S(2)}) async-start(bf16[16,2,1]{1,2,0:T(2,128)(2,1)} %reshape.367), calls=%async_computation.1 | async-start | bytes 16384 | tf_op jit(solution)/shard_map/all_to_all | solution.py:177
  270.7 7.1 %copy-start.10 = (s32[4,4]{1,0:T(4,128)S(1)}, s32[4,4]{1,0:T(4,128)}, u32[]{:S(2)}) copy-start(s32[4,4]{1,0:T(4,128)} %param.29) | copy-start | bytes 196
  270.7 115.3 %all-to-all-start.2 = ((bf16[32,4,2,128,128]{4,3,2,1,0:T(8,128)(2,1)}), bf16[32,4,2,128,128]{4,3,2,1,0:T(8,128)(2,1)}, u32[]{:S(2)}, u32[]{:S(2)}) async-start(bf16[32,4,2,128,128]{4,3,2,1,0:T(8,128)(2,1)} %broadcast_select_fusion), calls=%async_computation.2 | async-start | bytes 16777216 | tf_op jit(solution)/shard_map/all_to_all | solution.py:176
  289.5 5.1 %copy-start.12 = (bf16[1024]{0:T(1024)(128)(2,1)S(1)}, bf16[1024]{0:T(1024)(128)(2,1)}, u32[]{:S(2)}) copy-start(bf16[1024]{0:T(1024)(128)(2,1)} %param.23) | copy-start | bytes 6148
  298.6 2.8 copy-start.4
  307.6 1.4 copy-start.1
  307.6 1.9 copy-start.2
  307.6 2.3 copy-start.3
  309.9 2.2 copy-start.6
Sparse Core Ops, SparseCore 0:
  10.9 188.5 all-gather.2
  220.6 35.4 all-gather.4

commit v5 on v4

--- a/solution.py
+++ b/solution.py
@@ -150,7 +150,7 @@
     return lax.axis_index("dz") * lax.axis_size("dc") + lax.axis_index("dc")
 
 
-def relayout(prev_cache, dest_device):
+def pack_cache(prev_cache, dest_device):
     blocks_here = prev_cache.shape[0]
     devices = lax.axis_size("dz") * lax.axis_size("dc")
     slot_count = devices * CAP
@@ -170,8 +170,14 @@
     source = jnp.sum(
         jnp.where(matches, jnp.arange(blocks_here, dtype=jnp.int32)[None, :], 0), axis=1
     )
-    packed = jnp.take(prev_cache, source, axis=0)
+    packed = jnp.take(prev_cache, source, axis=0, mode="clip")
     slot_flags = filled.astype(jnp.bfloat16)
+    return packed, slot_flags
+
+
+def unpack_cache(packed, slot_flags):
+    blocks_here = packed.shape[0] // CAP
+    slot_count = packed.shape[0]
     arrived, arrived_flags = (
         lax.all_to_all(packed, ("dz", "dc"), split_axis=0, concat_axis=0, tiled=True),
         lax.all_to_all(slot_flags, ("dz", "dc"), split_axis=0, concat_axis=0, tiled=True),
@@ -182,7 +188,7 @@
         order_no[None, :] == jnp.arange(blocks_here, dtype=jnp.int32)[:, None]
     )
     chosen = jnp.sum(jnp.where(picked, jnp.arange(slot_count, dtype=jnp.int32)[None, :], 0), axis=1)
-    return jnp.take(arrived, chosen, axis=0)
+    return jnp.take(arrived, chosen, axis=0, mode="clip")
 
 
 def per_device(
@@ -214,12 +220,69 @@
     mp_size = lax.axis_size("mp")
     spread = jnp.broadcast_to(hidden[None], (mp_size,) + hidden.shape)
     pieces = lax.all_to_all(spread, "mp", split_axis=0, concat_axis=0, tiled=True)
+    local_heads = query_weight.shape[1] // HD
+    local_kv = key_weight.shape[1] // HD
+    block_size = pool_keys.shape[1]
+    blocks_here = pool_keys.shape[0] * lax.axis_size("dz") * lax.axis_size("dc")
+    key_count = row_count * lax.axis_size("dz") * lax.axis_size("dc")
+    window = min(key_count, MAX_REQUEST + row_count)
+    window = -(-window // K_TILE) * K_TILE
+    window_start = jnp.maximum((me + 1) * row_count - window, 0)
+    blocks = jnp.arange(blocks_here, dtype=jnp.int32)
+    matching = prompt_table[:, :, None] == blocks[None, None, :]
+    slot_no = jnp.sum(
+        jnp.where(matching, jnp.arange(prompt_table.shape[1], dtype=jnp.int32)[None, :, None], 0),
+        axis=(0, 1),
+    )
+    group_no = jnp.sum(
+        jnp.where(matching, jnp.arange(prompt_table.shape[0], dtype=jnp.int32)[:, None, None], 0),
+        axis=(0, 1),
+    )
+    named = jnp.any(matching, axis=(0, 1))
+    within = slot_no[:, None] * block_size + jnp.arange(block_size, dtype=jnp.int32)[None, :]
+    block_len = jnp.take(prompt_lens, group_no)
+    pool_tag = jnp.where(named[:, None] & (within < block_len[:, None]), group_no[:, None], -1)
+    key_tag = jnp.concatenate(
+        [pool_tag.reshape(-1), jnp.full((window,), -2, jnp.int32)]
+    )
+    key_row = jnp.concatenate(
+        [
+            jnp.full((blocks_here * block_size,), -1, jnp.int32),
+            window_start + jnp.arange(window, dtype=jnp.int32),
+        ]
+    )
+    starts_at = ends_at - request_lens
+    token_group = jnp.take(request_group, request_of)
+    token_start = jnp.take(starts_at, request_of)
+    seen = (key_tag[None, :] == token_group[:, None]) | (
+        (key_row[None, :] >= token_start[:, None]) & (key_row[None, :] <= global_rows[:, None])
+    )
+    q_tokens = Q_TILE // local_heads
+    flags = jnp.any(
+        seen.reshape(row_count // q_tokens, q_tokens, -1, K_TILE), axis=(1, 3)
+    ).astype(jnp.int32)
+
+
+    def per_row(x):
+        return jnp.repeat(x, local_heads)[:, None]
+
+    row_group, row_start, row_last = per_row(token_group), per_row(token_start), per_row(global_rows)
+    key_tag, key_row = key_tag[None, :], key_row[None, :]
+    packed, slot_flags = pack_cache(prev_cache, dest_device)
+    pieces, packed, slot_flags, row_group, row_start, row_last, key_tag, key_row, flags, positions = (
+        lax.optimization_barrier(
+            (pieces, packed, slot_flags, row_group, row_start, row_last, key_tag, key_row, flags,
+             positions)
+        )
+    )
     q_cols = query_weight.shape[1]
     k_cols = key_weight.shape[1]
     block_rows = query_weight.shape[0]
     pool_here = jnp.concatenate([pool_keys, pool_values], axis=2).reshape(block_rows, -1)
     weights_here = jnp.concatenate([query_weight, key_weight, value_weight, pool_here], axis=1)
     weights_all = lax.all_gather(weights_here, ("dz", "dc"), axis=0, tiled=True)
+    packed, weights_all = lax.optimization_barrier((packed, weights_all))
+    decode_cache = unpack_cache(packed, slot_flags)
     proj_cols = q_cols + 2 * k_cols
     pool_all = weights_all[:, proj_cols:].reshape(
         (-1,) + pool_keys.shape[1:2] + (2 * pool_keys.shape[2],)
@@ -240,9 +303,6 @@
     query_proj = proj[:, :q_cols] + query_bias.astype(jnp.float32)[None, :]
     key_proj = proj[:, q_cols:q_cols + k_cols] + key_bias.astype(jnp.float32)[None, :]
     value_proj = proj[:, q_cols + k_cols:proj_cols] + value_bias.astype(jnp.float32)[None, :]
-    local_heads = query_proj.shape[1] // HD
-    local_kv = key_proj.shape[1] // HD
-    group_size = local_heads // local_kv
     queries = rotary(query_proj.reshape(row_count, local_heads, HD), positions).astype(jnp.bfloat16)
     queries = queries.reshape(row_count * local_heads, HD)
     keys_new = (
@@ -253,66 +313,21 @@
     values_new = value_proj.astype(jnp.bfloat16)
     span_here = jnp.concatenate([keys_new, values_new], axis=1)
     span_all = lax.all_gather(span_here, ("dz", "dc"), axis=0, tiled=True)
-    prev_cache, span_all = lax.optimization_barrier((prev_cache, span_all))
-    decode_cache = relayout(prev_cache, dest_device)
     score_scale = HD ** (-0.5)
-    block_size = pool_all.shape[1]
-    blocks_here = pool_all.shape[0]
     kv_width = local_kv * HD
-    key_count = span_all.shape[0]
-    window = min(key_count, MAX_REQUEST + row_count)
-    window = -(-window // K_TILE) * K_TILE
-    window_start = jnp.maximum((me + 1) * row_count - window, 0)
     span_window = lax.dynamic_slice_in_dim(span_all, window_start, window, axis=0)
     pool_flat = pool_all.reshape(blocks_here * block_size, 2 * kv_width)
     all_keys = jnp.concatenate([pool_flat[:, :kv_width], span_window[:, :kv_width]], axis=0)
     all_values = jnp.concatenate([pool_flat[:, kv_width:], span_window[:, kv_width:]], axis=0)
-    blocks = jnp.arange(blocks_here, dtype=jnp.int32)
-    matching = prompt_table[:, :, None] == blocks[None, None, :]
-    slot_no = jnp.sum(
-        jnp.where(matching, jnp.arange(prompt_table.shape[1], dtype=jnp.int32)[None, :, None], 0),
-        axis=(0, 1),
-    )
-    group_no = jnp.sum(
-        jnp.where(matching, jnp.arange(prompt_table.shape[0], dtype=jnp.int32)[:, None, None], 0),
-        axis=(0, 1),
-    )
-    named = jnp.any(matching, axis=(0, 1))
-    within = slot_no[:, None] * block_size + jnp.arange(block_size, dtype=jnp.int32)[None, :]
-    block_len = jnp.take(prompt_lens, group_no)
-    pool_tag = jnp.where(named[:, None] & (within < block_len[:, None]), group_no[:, None], -1)
-    key_tag = jnp.concatenate(
-        [pool_tag.reshape(-1), jnp.full((window,), -2, jnp.int32)]
-    )
-    key_row = jnp.concatenate(
-        [
-            jnp.full((blocks_here * block_size,), -1, jnp.int32),
-            window_start + jnp.arange(window, dtype=jnp.int32),
-        ]
-    )
-    starts_at = ends_at - request_lens
-    token_group = jnp.take(request_group, request_of)
-    token_start = jnp.take(starts_at, request_of)
-    seen = (key_tag[None, :] == token_group[:, None]) | (
-        (key_row[None, :] >= token_start[:, None]) & (key_row[None, :] <= global_rows[:, None])
-    )
-    q_tokens = Q_TILE // local_heads
-    flags = jnp.any(
-        seen.reshape(row_count // q_tokens, q_tokens, -1, K_TILE), axis=(1, 3)
-    ).astype(jnp.int32)
-
-    def per_row(x):
-        return jnp.repeat(x, local_heads)[:, None]
-
     output = flash(
         queries,
         all_keys,
         all_values,
-        per_row(token_group),
-        per_row(token_start),
-        per_row(global_rows),
-        key_tag[None, :],
-        key_row[None, :],
+        row_group,
+        row_start,
+        row_last,
+        key_tag,
+        key_row,
         flags,
         Q_TILE,
         K_TILE,

time: 401 us -> 432 us (1.077)
  waiting for transfers between devices: 200 us -> 240 us
  other arithmetic: 41.2 us -> 24.6 us
  local copies, waits for them, and re-layouts: 43.3 us -> 48.1 us
    all_gather x1, waiting for transfers between devices: 27 us -> 94.3 us  [per_device(): span_all = lax.all_gather(span_here, ('dz', 'dc'), axis=0, tiled=True)]
    all_to_all x1, waiting for transfers between devices: 87.1 us -> 66.8 us  [per_device(): lax.all_to_all(spread, 'mp', split_axis=0, concat_axis=0, tiled=True)]
    select_n x5 -> x1, other arithmetic: 12.2 us -> 0.01 us  [pack_cache(): slot_rank = jnp.arange(slot_count, dtype=jnp.int32) % CAP]
    all_gather x1, waiting for transfers between devices: 85.6 us -> 78.9 us  [per_device(): weights_all = lax.all_gather(weights_here, ('dz', 'dc'), axis=0, tiled=True)]
    optimization_barrier x0 -> x3, local copies, waits for them, and re-layouts: none -> 5.02 us  [per_device(): lax.optimization_barrier((pieces, packed, slot_flags, row_group, row_star...]
  transfers between devices with their start and end apart: 5 -> 5, of which waited for: 3 -> 3; matrix products, arithmetic and copies ran while one was open for 16% -> 18% of each run, Pallas kernels for 17% -> 16%
where the time goes in v5:
time: 432 us; the launch traced here: 433 us
  waiting for transfers between devices  240 us (56%)
  Pallas kernels  71.1 us (16%)
  local copies, waits for them, and re-layouts  48.1 us (11%)
  other arithmetic  24.6 us (6%)
  matrix products  17.4 us (4%)
  starting transfers between devices  17.3 us (4%)
  between operations  14.5 us (3%)
    all_gather x1, waiting for transfers between devices, per_device(): span_all = lax.all_gather(span_here, ('dz', 'dc'), axis=0, tiled=True)  94.3 us
    all_gather x1, waiting for transfers between devices, per_device(): weights_all = lax.all_gather(weights_here, ('dz', 'dc'), axis=0, tiled=True)  78.9 us
    pallas_call x1, Pallas kernels, flash(): pl.pallas_call(functools.partial(flash_kernel, scale=scale), grid_spec=gr...  71.1 us
    all_to_all x1, waiting for transfers between devices, per_device(): lax.all_to_all(spread, 'mp', split_axis=0, concat_axis=0, tiled=True)  66.8 us
    dot_general x1, matrix products, per_device(): jnp.einsum('jtf,jfc->tc', normed, weights_all.reshape(mp_size, -1, weight...  17.4 us
  transfers between devices with their start and end apart: 5, of which 3 were waited for; matrix products, arithmetic and copies ran while one was open for 18% of the time, Pallas kernels for 16%

profile of v5, /device:TPU:104, one launch (start us, length us, event | category | flops | bytes accessed | tf_op | source)
XLA Modules:
  0.0 432.9 jit_solution(7377442365329754319)
XLA Ops:
  7.2 0.8 pad_maximum_fusion.6
  8.1 0.1 reshape.249
  8.2 2.6 pad_maximum_fusion
  10.8 3.5 broadcast_in_dim.116
  14.3 6.2 %all-to-all-start = ((bf16[8,384,1024]{2,1,0:T(8,128)(2,1)}), bf16[8,384,1024]{2,1,0:T(8,128)(2,1)}, u32[]{:S(2)}, u32[]{:S(2)}) async-start(bf16[8,384,1024]{2,1,0:T(8,128)(2,1)} %broadcast_in_dim.116), calls=%async_computation | async-start | bytes 12582912 | tf_op jit(solution)/shard_map/all_to_all | solution.py:222
  20.5 0.6 broadcast_in_dim.186.key_row_ref
  21.3 0.7 gather_fusion.1
  22.1 0.6 broadcast_in_dim.185.tag_ref
  22.8 0.2 reduce-window.16
  23.0 0.2 convert_reduce_fusion
  23.3 0.7 fusion.27
  23.9 0.7 fusion.26
  24.7 1.9 select_select_fusion
  26.6 1.8 select_select_fusion.1
  28.4 3.7 or_reduce_fusion
  32.1 0.6 convert_element_type.60.flags
  32.8 0.1 broadcast_in_dim.122
  32.9 0.7 broadcast_in_dim_reshape.11
  33.6 0.1 broadcast_in_dim.120
  33.7 0.7 broadcast_in_dim_reshape.9
  34.5 0.1 broadcast_in_dim.121
  34.6 0.7 broadcast_in_dim_reshape.10
  35.4 7.2 %gather_fusion = bf16[32,4,2,128,128]{4,3,2,1,0:T(8,128)(2,1)} fusion(bf16[16,4,2,128,128]{4,3,2,1,0:T(8,128)(2,1)} %param.32, s32[1024]{0:T(1024)S(1)} %pad_clamp_fusion.2), kind=kCustom, calls=%fused_computation | custom fusion | bytes 16777344 | tf_op jit(solution)/shard_map/jit(_take)/gather | solution.py:173
  42.8 66.8 %all-to-all-done = bf16[8,384,1024]{2,1,0:T(8,128)(2,1)} async-done(((bf16[8,384,1024]{2,1,0:T(8,128)(2,1)}), bf16[8,384,1024]{2,1,0:T(8,128)(2,1)}, u32[]{:S(2)}, u32[]{:S(2)}) %all-to-all-start) | async-done | bytes 6291488 | tf_op jit(solution)/shard_map/all_to_all | solution.py:222
  109.6 0.7 all_to_all.16
  110.3 5.4 %all-to-all-start.2 = ((bf16[16,2,1]{1,2,0:T(2,128)(2,1)}), bf16[16,2,1]{1,2,0:T(2,128)(2,1)S(1)}, u32[]{:S(2)}, u32[]{:S(2)}) async-start(bf16[16,2,1]{1,2,0:T(2,128)(2,1)} %all_to_all.16), calls=%async_computation.2 | async-start | bytes 16384 | tf_op jit(solution)/shard_map/all_to_all | solution.py:183
  115.7 4.2 fusion
  120.0 0.8 multiply_cosine_fusion
  120.8 78.9 %all-gather.3.cloned.1.call-done = bf16[8192,1344]{1,0:T(8,128)(2,1)} async-done(((bf16[512,1344]{1,0:T(8,128)(2,1)}), bf16[8192,1344]{1,0:T(8,128)(2,1)}) %all-gather.3.cloned.1.call-update) | async-done | bytes 22020112 | tf_op jit(solution)/shard_map/all_gather | solution.py:283
  199.6 17.4 %fusion.7 = f32[384,1344]{0,1:T(8,128)S(1)} fusion(bf16[8,1024,1344]{2,1,0:T(8,128)(2,1)} %bitcast.40, bf16[8,384,1024]{2,1,0:T(8,128)(2,1)} %all-to-all-done, f32[8,1024]{1,0:T(8,128)S(1)} %reshape.255, f32[384]{0:T(512)S(1)} %add_rsqrt_fusion), kind=kOutput, calls=%fused_computation.12 | convolution fusion | flops 8468299776 | bytes 30410240 | tf_op jit(solution)/shard_map/jtf,jfc->tc/dot_general | solution.py:297
  217.1 0.1 copy.60
  217.2 0.1 copy.61
  217.4 0.1 fusion.12
  217.5 0.2 fusion.14
  217.8 0.6 copy-done.5
  218.4 5.4 %all-to-all-start.1 = ((bf16[32,4,2,128,128]{4,3,2,1,0:T(8,128)(2,1)}), bf16[32,4,2,128,128]{4,3,2,1,0:T(8,128)(2,1)}, u32[]{:S(2)}, u32[]{:S(2)}) async-start(bf16[32,4,2,128,128]{4,3,2,1,0:T(8,128)(2,1)} %gather_fusion), calls=%async_computation.1 | async-start | bytes 16777216 | tf_op jit(solution)/shard_map/all_to_all | solution.py:182
  223.8 0.3 all-gather.5.cloned.1.call-start
  224.1 0.7 pad_maximum_fusion.5
  224.8 1.7 copy.52.grp_ref
  226.5 1.7 copy.53.lo_ref
  228.2 1.7 copy.54.hi_ref
  229.9 0.1 gt.25
  230.2 0.1 add_reduce_fusion
  230.3 0.1 select_reduce_fusion
  230.4 3.0 slice.39
  233.5 1.6 slice_add_fusion
  235.1 0.5 copy.47
  235.6 1.4 reshape.251
  237.0 1.0 fusion.24
  238.0 2.9 copy.58
  240.9 1.6 copy.59
  242.6 1.3 reshape_reshape.3
  244.0 1.3 copy-done.2
  245.3 0.1 negate_bitcast_fusion
  245.4 0.4 copy-done.3
  245.8 0.5 copy-done.4
  246.3 1.4 fusion.11.q_ref
  247.6 94.3 %all-gather.5.cloned.1.call-done = bf16[6144,256]{1,0:T(8,128)(2,1)} async-done(((bf16[384,256]{1,0:T(8,128)(2,1)}), bf16[6144,256]{1,0:T(8,128)(2,1)}) %all-gather.5.cloned.1.call-update) | async-done | bytes 3145744 | tf_op jit(solution)/shard_map/all_gather | solution.py:315
  341.9 2.1 fusion.22
  344.0 1.2 pad_maximum_fusion.2.v_ref
  345.2 1.2 pad_maximum_fusion.1.k_ref
  346.3 71.1 %shard_map.167 = bf16[3072,128]{1,0:T(8,128)(2,1)} custom-call(s32[3,11]{1,0:T(4,128)} %convert_element_type.60.flags, s32[3072,1]{1,0:T(8,128)} %copy.52.grp_ref, s32[3072,1]{1,0:T(8,128)} %copy.53.lo_ref, s32[3072,1]{1,0:T(8,128)} %copy.54.hi_ref, s32[1,5632]{1,0:T(1,128)} %broadcast_in_dim.185.tag_ref, s32[1,5632]{1,0:T(1,128)} %broadcast_in_dim.186.key_row_ref, ...), custom_call_target="tpu_custom_call" | custom-call | tf_op jit(solution)/shard_map/pallas_call | solution.py:142
  417.4 2.1 reshape.254
  419.6 6.5 %gather_fusion.2 = bf16[16,4,2,128,128]{4,3,2,1,0:T(8,128)(2,1)} fusion(bf16[32,4,2,128,128]{4,3,2,1,0:T(8,128)(2,1)} %all-to-all-done.1, s32[1024]{0:T(1024)S(1)} %pad_clamp_fusion), kind=kCustom, calls=%fused_computation.2 | custom fusion | bytes 8388672 | tf_op jit(solution)/shard_map/jit(_take)/gather | solution.py:191
  (75 shorter events, 1.3 us)
Async XLA Ops:
  7.2 3.6 copy-start.6
  7.2 192.5 %all-gather.3.cloned.1.call-start = ((), (), s32[]{:S(2)}) async-start(), calls=%async_computation.3 | async-start | bytes 24510464 | tf_op jit(solution)/shard_map/all_gather | solution.py:283
  14.3 6.9 %copy-start.12 = (s32[4,4]{1,0:T(4,128)S(1)}, s32[4,4]{1,0:T(4,128)}, u32[]{:S(2)}) copy-start(s32[4,4]{1,0:T(4,128)} %param.29) | copy-start | bytes 196
  14.3 7.0 %copy-start = (s32[4]{0:T(128)S(1)}, s32[4]{0:T(128)}, u32[]{:S(2)}) copy-start(s32[4]{0:T(128)} %param.28) | copy-start | bytes 52
  14.3 8.5 %copy-start.15 = (bf16[128]{0:T(256)(128)(2,1)S(1)}, bf16[128]{0:T(256)(128)(2,1)}, u32[]{:S(2)}) copy-start(bf16[128]{0:T(256)(128)(2,1)} %param.24) | copy-start | bytes 772
  14.3 8.5 %copy-start.17 = (s32[3]{0:T(128)S(1)}, s32[3]{0:T(128)}, u32[]{:S(2)}) copy-start(s32[3]{0:T(128)} %param.26) | copy-start | bytes 40
  14.3 8.7 %copy-start.16 = (bf16[128]{0:T(256)(128)(2,1)S(1)}, bf16[128]{0:T(256)(128)(2,1)}, u32[]{:S(2)}) copy-start(bf16[128]{0:T(256)(128)(2,1)} %param.25) | copy-start | bytes 772
  14.3 8.7 %copy-start.14 = (s32[16,1]{0,1:T(1,128)S(1)}, s32[16,1]{0,1:T(1,128)}, u32[]{:S(2)}) copy-start(s32[16,1]{0,1:T(1,128)} %param.33) | copy-start | bytes 196
  14.3 9.6 %copy-start.11 = (s32[3]{0:T(128)S(1)}, s32[3]{0:T(128)}, u32[]{:S(2)}) copy-start(s32[3]{0:T(128)} %param.27) | copy-start | bytes 40
  14.3 18.4 %copy-start.10 = (bf16[8192]{0:T(1024)(128)(2,1)S(1)}, bf16[8192]{0:T(1024)(128)(2,1)}, u32[]{:S(2)}) copy-start(bf16[8192]{0:T(1024)(128)(2,1)} %param.19) | copy-start | bytes 49156
  14.3 95.3 %all-to-all-start = ((bf16[8,384,1024]{2,1,0:T(8,128)(2,1)}), bf16[8,384,1024]{2,1,0:T(8,128)(2,1)}, u32[]{:S(2)}, u32[]{:S(2)}) async-start(bf16[8,384,1024]{2,1,0:T(8,128)(2,1)} %broadcast_in_dim.116), calls=%async_computation | async-start | bytes 12582912 | tf_op jit(solution)/shard_map/all_to_all | solution.py:222
  110.3 107.5 %all-to-all-start.2 = ((bf16[16,2,1]{1,2,0:T(2,128)(2,1)}), bf16[16,2,1]{1,2,0:T(2,128)(2,1)S(1)}, u32[]{:S(2)}, u32[]{:S(2)}) async-start(bf16[16,2,1]{1,2,0:T(2,128)(2,1)} %all_to_all.16), calls=%async_computation.2 | async-start | bytes 16384 | tf_op jit(solution)/shard_map/all_to_all | solution.py:183
  217.0 1.3 copy-start.5
  217.7 7.1 %copy-start.13 = (bf16[1024]{0:T(1024)(128)(2,1)S(1)}, bf16[1024]{0:T(1024)(128)(2,1)}, u32[]{:S(2)}) copy-start(bf16[1024]{0:T(1024)(128)(2,1)} %param.23) | copy-start | bytes 6148
  217.8 7.1 %copy-start.8 = (s32[3072,1]{0,1:T(1,128)S(1)}, s32[3072,1]{0,1:T(1,128)}, u32[]{:S(2)}) copy-start(s32[3072,1]{0,1:T(1,128)} %broadcast_in_dim_reshape.9) | copy-start | bytes 36868
  217.8 8.7 %copy-start.9 = (s32[3072,1]{0,1:T(1,128)S(1)}, s32[3072,1]{0,1:T(1,128)}, u32[]{:S(2)}) copy-start(s32[3072,1]{0,1:T(1,128)} %broadcast_in_dim_reshape.10) | copy-start | bytes 36868
  218.4 201.2 %all-to-all-start.1 = ((bf16[32,4,2,128,128]{4,3,2,1,0:T(8,128)(2,1)}), bf16[32,4,2,128,128]{4,3,2,1,0:T(8,128)(2,1)}, u32[]{:S(2)}, u32[]{:S(2)}) async-start(bf16[32,4,2,128,128]{4,3,2,1,0:T(8,128)(2,1)} %gather_fusion), calls=%async_computation.1 | async-start | bytes 16777216 | tf_op jit(solution)/shard_map/all_to_all | solution.py:182
  223.8 4.4 %copy-start.7 = (s32[3072,1]{0,1:T(1,128)S(1)}, s32[3072,1]{0,1:T(1,128)}, u32[]{:S(2)}) copy-start(s32[3072,1]{0,1:T(1,128)} %broadcast_in_dim_reshape.11) | copy-start | bytes 36868
  223.8 118.1 %all-gather.5.cloned.1.call-start = ((), (), s32[]{:S(2)}) async-start(), calls=%async_computation.4 | async-start | bytes 3342336 | tf_op jit(solution)/shard_map/all_gather | solution.py:315
  238.0 4.6 %copy-start.1 = (bf16[8192,64]{1,0:T(8,128)(2,1)S(1)}, bf16[8192,64]{1,0:T(8,128)(2,1)}, u32[]{:S(2)}) copy-start(bf16[8192,64]{1,0:T(8,128)(2,1)} %slice.39) | copy-start | bytes 3145732
  243.9 1.4 copy-start.2
  243.9 1.9 copy-start.3
  243.9 2.3 copy-start.4
Sparse Core Ops, SparseCore 0:
  10.9 188.6 all-gather.2
  226.3 115.5 all-gather.4

commit v6 on v5

--- a/solution.py
+++ b/solution.py
@@ -218,8 +218,7 @@
         global_rows, request_lens, request_group, prompt_lens
     )
     mp_size = lax.axis_size("mp")
-    spread = jnp.broadcast_to(hidden[None], (mp_size,) + hidden.shape)
-    pieces = lax.all_to_all(spread, "mp", split_axis=0, concat_axis=0, tiled=True)
+    full_rows = lax.all_gather(hidden, "mp", axis=1, tiled=True)
     local_heads = query_weight.shape[1] // HD
     local_kv = key_weight.shape[1] // HD
     block_size = pool_keys.shape[1]
@@ -269,9 +268,9 @@
     row_group, row_start, row_last = per_row(token_group), per_row(token_start), per_row(global_rows)
     key_tag, key_row = key_tag[None, :], key_row[None, :]
     packed, slot_flags = pack_cache(prev_cache, dest_device)
-    pieces, packed, slot_flags, row_group, row_start, row_last, key_tag, key_row, flags, positions = (
+    full_rows, packed, slot_flags, row_group, row_start, row_last, key_tag, key_row, flags, positions = (
         lax.optimization_barrier(
-            (pieces, packed, slot_flags, row_group, row_start, row_last, key_tag, key_row, flags,
+            (full_rows, packed, slot_flags, row_group, row_start, row_last, key_tag, key_row, flags,
              positions)
         )
     )
@@ -280,24 +279,32 @@
     block_rows = query_weight.shape[0]
     pool_here = jnp.concatenate([pool_keys, pool_values], axis=2).reshape(block_rows, -1)
     weights_here = jnp.concatenate([query_weight, key_weight, value_weight, pool_here], axis=1)
-    weights_all = lax.all_gather(weights_here, ("dz", "dc"), axis=0, tiled=True)
-    packed, weights_all = lax.optimization_barrier((packed, weights_all))
-    decode_cache = unpack_cache(packed, slot_flags)
+    nd = lax.axis_size("dz") * lax.axis_size("dc")
+    half_rows = block_rows // 2
+    halves = weights_here.reshape(2, half_rows, weights_here.shape[1])
+    outgoing = jnp.tile(halves, (nd // 2, 1, 1))
+    arrived_mine = lax.all_to_all(outgoing, ("dz", "dc"), split_axis=0, concat_axis=0, tiled=True)
+    arrived_other = lax.ppermute(arrived_mine, "dc", perm=[(0, 1), (1, 0)])
     proj_cols = q_cols + 2 * k_cols
-    pool_all = weights_all[:, proj_cols:].reshape(
+    first_is_mine = side == 0
+    pool_first = jnp.where(first_is_mine, arrived_mine[:, :, proj_cols:], arrived_other[:, :, proj_cols:])
+    pool_second = jnp.where(first_is_mine, arrived_other[:, :, proj_cols:], arrived_mine[:, :, proj_cols:])
+    pool_all = jnp.concatenate([pool_first, pool_second], axis=1).reshape(
         (-1,) + pool_keys.shape[1:2] + (2 * pool_keys.shape[2],)
     )
-    as_float = pieces.astype(jnp.float32)
-    inverse = lax.rsqrt(
-        jnp.mean(jnp.sum(as_float * as_float, axis=2), axis=0)[None, :, None] / pieces.shape[2]
-        + EPSILON
-    )
-    gain = norm_gain.astype(jnp.float32).reshape(mp_size, 1, -1)
-    normed = (as_float * inverse * gain).astype(jnp.bfloat16)
-    proj = jnp.einsum(
-        "jtf,jfc->tc",
-        normed,
-        weights_all.reshape(mp_size, -1, weights_all.shape[1]),
+    as_float = full_rows.astype(jnp.float32)
+    inverse = lax.rsqrt(jnp.mean(as_float * as_float, axis=1, keepdims=True) + EPSILON)
+    normed = (as_float * inverse * norm_gain.astype(jnp.float32)[None, :]).astype(jnp.bfloat16)
+    normed_halves = normed.reshape(row_count, nd, 2, half_rows)
+    normed_mine = lax.dynamic_index_in_dim(normed_halves, side, axis=2, keepdims=False)
+    normed_other = lax.dynamic_index_in_dim(normed_halves, 1 - side, axis=2, keepdims=False)
+    proj = jnp.dot(
+        normed_mine.reshape(row_count, -1),
+        arrived_mine.reshape(-1, arrived_mine.shape[2]),
+        preferred_element_type=jnp.float32,
+    ) + jnp.dot(
+        normed_other.reshape(row_count, -1),
+        arrived_other.reshape(-1, arrived_other.shape[2]),
         preferred_element_type=jnp.float32,
     )
     query_proj = proj[:, :q_cols] + query_bias.astype(jnp.float32)[None, :]
@@ -313,6 +320,8 @@
     values_new = value_proj.astype(jnp.bfloat16)
     span_here = jnp.concatenate([keys_new, values_new], axis=1)
     span_all = lax.all_gather(span_here, ("dz", "dc"), axis=0, tiled=True)
+    packed, span_all = lax.optimization_barrier((packed, span_all))
+    decode_cache = unpack_cache(packed, slot_flags)
     score_scale = HD ** (-0.5)
     kv_width = local_kv * HD
     span_window = lax.dynamic_slice_in_dim(span_all, window_start, window, axis=0)

time: 432 us -> 403 us (0.933); the launches traced: 433 us -> 397 us
  Pallas kernels: 71.1 us -> 43 us
  waiting for transfers between devices: 240 us -> 214 us
  local copies, waits for them, and re-layouts: 48.1 us -> 60.2 us
  other arithmetic: 24.6 us -> 31.2 us
    all_to_all x1, waiting for transfers between devices: 66.8 us -> 161 us  [per_device(): lax.all_to_all(outgoing, ('dz', 'dc'), split_axis=0, concat_axis=0, tiled...]
    all_gather x1, waiting for transfers between devices: 78.9 us -> 0.01 us  [per_device(): full_rows = lax.all_gather(hidden, 'mp', axis=1, tiled=True)]
    all_gather x1, waiting for transfers between devices: 94.3 us -> 29 us  [per_device(): span_all = lax.all_gather(span_here, ('dz', 'dc'), axis=0, tiled=True)]
    pallas_call x1, Pallas kernels: 71.1 us -> 43 us  [flash(): pl.pallas_call(functools.partial(flash_kernel, scale=scale), grid_spec=gr...]
    all_to_all x1, waiting for transfers between devices: 0.01 us -> 24.7 us  [unpack_cache(): lax.all_to_all(packed, ('dz', 'dc'), split_axis=0, concat_axis=0, tiled=T...]
    reshape x1 -> x2, local copies, waits for them, and re-layouts: 0.11 us -> 16.3 us  [the longest x1 10.4 us: per_device(): arrived_mine.reshape(-1, arrived_mine.shape[2])]
    another operation x0 -> x2, local copies, waits for them, and re-layouts: none -> 5.77 us  [per_device(): outgoing = jnp.tile(halves, (nd // 2, 1, 1))]
    dot_general x1 -> x2, matrix products: 17.4 us -> 14.1 us  [the longest x1 7.65 us: per_device(): jnp.dot(normed_other.reshape(row_count, -1), arrived_other.reshape(-1, ar...]
  transfers between devices with their start and end apart: 5 -> 6, of which waited for: 3 -> 3; matrix products, arithmetic and copies ran while one was open for 18% -> 18% of each run, Pallas kernels for 16% -> 11%
where the time goes in v6:
time: 403 us; the launch traced here: 397 us
  waiting for transfers between devices  214 us (53%)
  local copies, waits for them, and re-layouts  60.2 us (15%)
  Pallas kernels  43 us (11%)
  other arithmetic  31.2 us (8%)
  starting transfers between devices  19.6 us (5%)
  between operations  14.5 us (4%)
  matrix products  14.1 us (3%)
    all_to_all x1, waiting for transfers between devices, per_device(): lax.all_to_all(outgoing, ('dz', 'dc'), split_axis=0, concat_axis=0, tiled...  161 us
    pallas_call x1, Pallas kernels, flash(): pl.pallas_call(functools.partial(flash_kernel, scale=scale), grid_spec=gr...  43 us
    all_gather x1, waiting for transfers between devices, per_device(): span_all = lax.all_gather(span_here, ('dz', 'dc'), axis=0, tiled=True)  29 us
    all_to_all x1, waiting for transfers between devices, unpack_cache(): lax.all_to_all(packed, ('dz', 'dc'), split_axis=0, concat_axis=0, tiled=T...  24.7 us
    reshape x1, local copies, waits for them, and re-layouts, per_device(): arrived_mine.reshape(-1, arrived_mine.shape[2])  10.4 us
  transfers between devices with their start and end apart: 6, of which 3 were waited for; matrix products, arithmetic and copies ran while one was open for 18% of the time, Pallas kernels for 11%

profile of v6, /device:TPU:104, one launch (start us, length us, event | category | flops | bytes accessed | tf_op | source)
XLA Modules:
  0.0 397.0 jit_solution(11716474127135298368)
XLA Ops:
  7.2 0.8 pad_maximum_fusion.6
  7.9 0.1 concatenate.63
  8.1 1.5 maximum_bitcast_fusion
  9.6 0.7 copy.57
  10.2 5.1 %tile.11 = bf16[8,2,256,1344]{2,3,1,0:T(8,128)(2,1)} broadcast(bf16[2,256,1344]{1,2,0:T(8,128)(2,1)S(1)} %copy.57), dimensions={1,2,3} | broadcast | bytes 12386304 | tf_op jit(solution)/shard_map/tile | solution.py:285
  15.3 5.6 %all-to-all-start = ((bf16[16,256,1344]{1,2,0:T(8,128)(2,1)}), bf16[16,256,1344]{1,2,0:T(8,128)(2,1)}, u32[]{:S(2)}, u32[]{:S(2)}) async-start(bf16[16,256,1344]{1,2,0:T(8,128)(2,1)} %bitcast.54), calls=%async_computation | async-start | bytes 22020096 | tf_op jit(solution)/shard_map/all_to_all | solution.py:286
  21.0 1.2 copy.56
  22.3 160.6 %all-to-all-done = bf16[16,256,1344]{1,2,0:T(8,128)(2,1)} async-done(((bf16[16,256,1344]{1,2,0:T(8,128)(2,1)}), bf16[16,256,1344]{1,2,0:T(8,128)(2,1)}, u32[]{:S(2)}, u32[]{:S(2)}) %all-to-all-start) | async-done | bytes 11010080 | tf_op jit(solution)/shard_map/all_to_all | solution.py:286
  182.9 0.6 broadcast_in_dim.180.key_row_ref
  183.6 0.7 gather_fusion.1
  184.5 0.6 broadcast_in_dim.179.tag_ref
  185.1 0.2 reduce-window.16
  185.3 0.2 convert_reduce_fusion
  185.6 0.7 fusion.21
  186.3 0.7 fusion.20
  187.0 1.9 select_select_fusion
  189.0 1.9 select_select_fusion.1
  190.8 3.7 or_reduce_fusion
  194.6 0.6 convert_element_type.62.flags
  195.3 0.1 broadcast_in_dim_reshape.11
  195.4 0.1 broadcast_in_dim.112
  195.5 0.1 broadcast_in_dim_reshape.9
  195.7 0.1 broadcast_in_dim.113
  195.8 0.1 broadcast_in_dim_reshape.10
  196.0 7.1 %gather_fusion = bf16[32,4,2,128,128]{4,3,2,1,0:T(8,128)(2,1)} fusion(bf16[16,4,2,128,128]{4,3,2,1,0:T(8,128)(2,1)} %param.32, s32[1024]{0:T(1024)S(1)} %pad_clamp_fusion.2), kind=kCustom, calls=%fused_computation | custom fusion | bytes 16777344 | tf_op jit(solution)/shard_map/jit(_take)/gather | solution.py:173
  203.3 10.4 %copy.70 = bf16[16,168,8,256]{3,2,0,1:T(8,128)(2,1)} copy(bf16[16,168,8,256]{3,2,1,0:T(8,128)(2,1)} %bitcast.29) | data formatting | bytes 22020096 | tf_op jit(solution)/shard_map/reshape | solution.py:303
  213.7 4.3 %fusion = f32[384]{0:T(512)S(1)} fusion(bf16[384,8192]{0,1:T(8,128)(2,1)} %all-gather.3.cloned.1.call-done), kind=kLoop, calls=%fused_computation.5 | loop fusion | flops 9436800 | bytes 6292992 | tf_op jit(solution)/shard_map/reduce_sum | solution.py:296
  218.1 0.8 multiply_cosine_fusion
  218.9 3.7 fusion.2
  222.6 2.4 constant_dynamic-slice_fusion
  225.0 6.4 %fusion.22 = f32[384,1344]{1,0:T(8,128)} fusion(bf16[384,4096]{0,1:T(8,128)(2,1)S(1)} %bitcast.62, bf16[4096,1344]{0,1:T(8,128)(2,1)S(1)} %bitcast.59), kind=kOutput, calls=%fused_computation.99 | convolution fusion | flops 4227858432 | bytes 16220160 | tf_op jit(solution)/shard_map/dot_general | solution.py:301
  231.4 5.9 %copy.71 = bf16[16,168,8,256]{3,2,0,1:T(8,128)(2,1)S(1)} copy(bf16[16,168,8,256]{3,2,1,0:T(8,128)(2,1)} %bitcast.31) | data formatting | bytes 22020096 | tf_op jit(solution)/shard_map/reshape | solution.py:307
  237.3 7.6 %convolution_add_fusion = f32[384,1344]{1,0:T(8,128)S(1)} fusion(f32[384,1344]{1,0:T(8,128)} %fusion.22, bf16[384,4096]{0,1:T(8,128)(2,1)} %bitcast.61, bf16[4096,1344]{0,1:T(8,128)(2,1)S(1)} %bitcast.60), kind=kOutput, calls=%fused_computation.9 | convolution fusion | flops 4228374528 | bytes 18284544 | tf_op jit(solution)/shard_map/dot_general | solution.py:305
  245.0 0.1 fusion.7
  245.2 1.2 copy-done.2
  246.3 0.9 fusion.9
  247.2 0.7 pad_maximum_fusion.5
  248.0 0.7 all_to_all.16
  248.7 7.0 %all-to-all-start.2 = ((bf16[16,2,1]{1,2,0:T(2,128)(2,1)}), bf16[16,2,1]{1,2,0:T(2,128)(2,1)S(1)}, u32[]{:S(2)}, u32[]{:S(2)}) async-start(bf16[16,2,1]{1,2,0:T(2,128)(2,1)} %all_to_all.16), calls=%async_computation.2 | async-start | bytes 16384 | tf_op jit(solution)/shard_map/all_to_all | solution.py:183
  255.7 29.0 %all-gather.5.cloned.1.call-done = bf16[6144,256]{1,0:T(8,128)(2,1)} async-done(((bf16[384,256]{1,0:T(8,128)(2,1)}), bf16[6144,256]{1,0:T(8,128)(2,1)}) %all-gather.5.cloned.1.call-update) | async-done | bytes 3145744 | tf_op jit(solution)/shard_map/all_gather | solution.py:322
  284.7 6.9 %all-to-all-start.1 = ((bf16[32,4,2,128,128]{4,3,2,1,0:T(8,128)(2,1)}), bf16[32,4,2,128,128]{4,3,2,1,0:T(8,128)(2,1)}, u32[]{:S(2)}, u32[]{:S(2)}) async-start(bf16[32,4,2,128,128]{4,3,2,1,0:T(8,128)(2,1)} %gather_fusion), calls=%async_computation.1 | async-start | bytes 16777216 | tf_op jit(solution)/shard_map/all_to_all | solution.py:182
  291.6 1.7 copy.63.grp_ref
  293.3 1.6 copy.64.lo_ref
  294.9 1.7 copy.65.hi_ref
  296.9 0.1 add_reduce_fusion
  297.0 0.1 select_reduce_fusion
  297.2 1.3 broadcast_select_fusion.1
  298.5 1.1 copy.62
  299.6 1.4 reshape_reshape.3
  301.0 3.0 slice_add_fusion
  304.0 2.5 reshape.272
  306.5 0.2 fusion.27
  306.7 0.3 copy.72
  307.1 0.5 fusion.3
  307.7 0.9 copy-done.4
  308.5 1.4 fusion.5.q_ref
  309.9 0.8 copy-done.5
  310.7 0.6 fusion.18
  311.3 1.2 pad_maximum_fusion.1.v_ref
  312.6 1.2 pad_maximum_fusion.k_ref
  313.8 43.0 %shard_map.167 = bf16[3072,128]{1,0:T(8,128)(2,1)} custom-call(s32[3,11]{1,0:T(4,128)} %convert_element_type.62.flags, s32[3072,1]{1,0:T(8,128)} %copy.63.grp_ref, s32[3072,1]{1,0:T(8,128)} %copy.64.lo_ref, s32[3072,1]{1,0:T(8,128)} %copy.65.hi_ref, s32[1,5632]{1,0:T(1,128)} %broadcast_in_dim.179.tag_ref, s32[1,5632]{1,0:T(1,128)} %broadcast_in_dim.180.key_row_ref, ...), custom_call_target="tpu_custom_call" | custom-call | tf_op jit(solution)/shard_map/pallas_call | solution.py:142
  356.8 2.1 reshape.275
  358.9 24.7 %all-to-all-done.1 = bf16[32,4,2,128,128]{4,3,2,1,0:T(8,128)(2,1)} async-done(((bf16[32,4,2,128,128]{4,3,2,1,0:T(8,128)(2,1)}), bf16[32,4,2,128,128]{4,3,2,1,0:T(8,128)(2,1)}, u32[]{:S(2)}, u32[]{:S(2)}) %all-to-all-start.1) | async-done | bytes 8388640 | tf_op jit(solution)/shard_map/all_to_all | solution.py:182
  383.7 6.5 %gather_fusion.2 = bf16[16,4,2,128,128]{4,3,2,1,0:T(8,128)(2,1)} fusion(bf16[32,4,2,128,128]{4,3,2,1,0:T(8,128)(2,1)} %all-to-all-done.1, s32[1024]{0:T(1024)S(1)} %pad_clamp_fusion), kind=kCustom, calls=%fused_computation.2 | custom fusion | bytes 8388672 | tf_op jit(solution)/shard_map/jit(_take)/gather | solution.py:191
  (83 shorter events, 1.6 us)
Async XLA Ops:
  15.3 5.7 %copy-start.7 = (bf16[384,1024]{1,0:T(8,128)(2,1)S(1)}, bf16[384,1024]{1,0:T(8,128)(2,1)}, u32[]{:S(2)}) copy-start(bf16[384,1024]{1,0:T(8,128)(2,1)} %param.18) | copy-start | bytes 2359300
  15.3 168.2 %copy-start.10 = (s32[4,4]{1,0:T(4,128)S(1)}, s32[4,4]{1,0:T(4,128)}, u32[]{:S(2)}) copy-start(s32[4,4]{1,0:T(4,128)} %param.29) | copy-start | bytes 196
  15.3 167.5 %all-to-all-start = ((bf16[16,256,1344]{1,2,0:T(8,128)(2,1)}), bf16[16,256,1344]{1,2,0:T(8,128)(2,1)}, u32[]{:S(2)}, u32[]{:S(2)}) async-start(bf16[16,256,1344]{1,2,0:T(8,128)(2,1)} %bitcast.54), calls=%async_computation | async-start | bytes 22020096 | tf_op jit(solution)/shard_map/all_to_all | solution.py:286
  20.9 162.7 %copy-start = (s32[4]{0:T(128)S(1)}, s32[4]{0:T(128)}, u32[]{:S(2)}) copy-start(s32[4]{0:T(128)} %param.28) | copy-start | bytes 52
  20.9 164.2 %copy-start.13 = (bf16[128]{0:T(256)(128)(2,1)S(1)}, bf16[128]{0:T(256)(128)(2,1)}, u32[]{:S(2)}) copy-start(bf16[128]{0:T(256)(128)(2,1)} %param.24) | copy-start | bytes 772
  20.9 164.2 %copy-start.15 = (s32[3]{0:T(128)S(1)}, s32[3]{0:T(128)}, u32[]{:S(2)}) copy-start(s32[3]{0:T(128)} %param.26) | copy-start | bytes 40
  20.9 164.4 %copy-start.14 = (bf16[128]{0:T(256)(128)(2,1)S(1)}, bf16[128]{0:T(256)(128)(2,1)}, u32[]{:S(2)}) copy-start(bf16[128]{0:T(256)(128)(2,1)} %param.25) | copy-start | bytes 772
  20.9 164.4 %copy-start.12 = (s32[16,1]{0,1:T(1,128)S(1)}, s32[16,1]{0,1:T(1,128)}, u32[]{:S(2)}) copy-start(s32[16,1]{0,1:T(1,128)} %param.33) | copy-start | bytes 196
  21.0 165.3 %copy-start.9 = (s32[3]{0:T(128)S(1)}, s32[3]{0:T(128)}, u32[]{:S(2)}) copy-start(s32[3]{0:T(128)} %param.27) | copy-start | bytes 40
  21.0 174.2 %copy-start.8 = (bf16[8192]{0:T(1024)(128)(2,1)S(1)}, bf16[8192]{0:T(1024)(128)(2,1)}, u32[]{:S(2)}) copy-start(bf16[8192]{0:T(1024)(128)(2,1)} %param.19) | copy-start | bytes 49156
  21.0 192.7 %all-gather.3.cloned.1.call-start = ((), (), s32[]{:S(2)}) async-start(), calls=%async_computation.3 | async-start | bytes 7077888 | tf_op jit(solution)/shard_map/all_gather | solution.py:221
  22.2 262.5 %all-gather.5.cloned.1.call-start = ((), (), s32[]{:S(2)}) async-start(), calls=%async_computation.4 | async-start | bytes 3342336 | tf_op jit(solution)/shard_map/all_gather | solution.py:322
  182.9 48.5 %collective-permute-start = (bf16[16,256,1344]{1,2,0:T(8,128)(2,1)}, bf16[16,256,1344]{1,2,0:T(8,128)(2,1)}, u32[]{:S(2)}, u32[]{:S(2)}) collective-permute-start(bf16[16,256,1344]{1,2,0:T(8,128)(2,1)} %all-to-all-done), channel_id=1, source_target_pairs={{0,8},{8,0},{1,9},{9,1},{2,10},{10,2},{3,11},{11,3},{4,12},{12,4},... | collective-permute-start | bytes 33030152 | tf_op jit(solution)/shard_map/ppermute | solution.py:287
  213.7 5.1 %copy-start.1 = (bf16[384,8192]{0,1:T(8,128)(2,1)S(1)}, bf16[384,8192]{0,1:T(8,128)(2,1)}, u32[]{:S(2)}) copy-start(bf16[384,8192]{0,1:T(8,128)(2,1)} %all-gather.3.cloned.1.call-done) | copy-start | bytes 18874372
  218.9 6.1 %slice-start = ((s8[11010048]{0:T(1024)(128)(4,1)}), s8[4194304]{0:T(1024)(128)(4,1)S(1)}, s32[]{:S(2)}) async-start(s8[11010048]{0:T(1024)(128)(4,1)} %bitcast.57), calls=%async_computation.5 | async-start | bytes 8388608
  218.9 6.1 %slice-start.1 = ((s8[11010048]{0:T(1024)(128)(4,1)}), s8[4194304]{0:T(1024)(128)(4,1)S(1)}, s32[]{:S(2)}) async-start(s8[11010048]{0:T(1024)(128)(4,1)} %bitcast.57), calls=%async_computation.6 | async-start | bytes 8388608
  222.6 2.4 slice-start.2
  245.0 1.3 copy-start.2
  248.7 36.0 %all-to-all-start.2 = ((bf16[16,2,1]{1,2,0:T(2,128)(2,1)}), bf16[16,2,1]{1,2,0:T(2,128)(2,1)S(1)}, u32[]{:S(2)}, u32[]{:S(2)}) async-start(bf16[16,2,1]{1,2,0:T(2,128)(2,1)} %all_to_all.16), calls=%async_computation.2 | async-start | bytes 16384 | tf_op jit(solution)/shard_map/all_to_all | solution.py:183
  255.7 35.9 %copy-start.11 = (bf16[1024]{0:T(1024)(128)(2,1)S(1)}, bf16[1024]{0:T(1024)(128)(2,1)}, u32[]{:S(2)}) copy-start(bf16[1024]{0:T(1024)(128)(2,1)} %param.23) | copy-start | bytes 6148
  284.7 99.0 %all-to-all-start.1 = ((bf16[32,4,2,128,128]{4,3,2,1,0:T(8,128)(2,1)}), bf16[32,4,2,128,128]{4,3,2,1,0:T(8,128)(2,1)}, u32[]{:S(2)}, u32[]{:S(2)}) async-start(bf16[32,4,2,128,128]{4,3,2,1,0:T(8,128)(2,1)} %gather_fusion), calls=%async_computation.1 | async-start | bytes 16777216 | tf_op jit(solution)/shard_map/all_to_all | solution.py:182
  301.0 5.5 %copy-start.3 = (f32[384,1344]{1,0:T(8,128)S(1)}, f32[384,1344]{1,0:T(8,128)}, u32[]{:S(2)}) copy-start(f32[384,1344]{1,0:T(8,128)} %copy-done.2) | copy-start | bytes 6193156
  307.1 1.4 copy-start.4
  307.1 1.4 copy-start.6
  308.5 2.2 copy-start.5
Sparse Core Ops, SparseCore 0:
  24.7 132.1 all-gather.2
  248.1 36.5 all-gather.4

commit v7 on v2

--- a/solution.py
+++ b/solution.py
@@ -87,7 +87,7 @@
     return lax.axis_index("dz") * lax.axis_size("dc") + lax.axis_index("dc")
 
 
-def relayout(prev_cache, dest_device):
+def pack_cache(prev_cache, dest_device):
     blocks_here = prev_cache.shape[0]
     devices = lax.axis_size("dz") * lax.axis_size("dc")
     slot_count = devices * CAP
@@ -107,8 +107,14 @@
     source = jnp.sum(
         jnp.where(matches, jnp.arange(blocks_here, dtype=jnp.int32)[None, :], 0), axis=1
     )
-    packed = jnp.take(prev_cache, source, axis=0)
+    packed = jnp.take(prev_cache, source, axis=0, mode="clip")
     slot_flags = filled.astype(jnp.bfloat16)
+    return packed, slot_flags
+
+
+def unpack_cache(packed, slot_flags):
+    blocks_here = packed.shape[0] // CAP
+    slot_count = packed.shape[0]
     arrived, arrived_flags = (
         lax.all_to_all(packed, ("dz", "dc"), split_axis=0, concat_axis=0, tiled=True),
         lax.all_to_all(slot_flags, ("dz", "dc"), split_axis=0, concat_axis=0, tiled=True),
@@ -119,7 +125,7 @@
         order_no[None, :] == jnp.arange(blocks_here, dtype=jnp.int32)[:, None]
     )
     chosen = jnp.sum(jnp.where(picked, jnp.arange(slot_count, dtype=jnp.int32)[None, :], 0), axis=1)
-    return jnp.take(arrived, chosen, axis=0)
+    return jnp.take(arrived, chosen, axis=0, mode="clip")
 
 
 def per_device(
@@ -151,6 +157,8 @@
     mp_size = lax.axis_size("mp")
     spread = jnp.broadcast_to(hidden[None], (mp_size,) + hidden.shape)
     pieces = lax.all_to_all(spread, "mp", split_axis=0, concat_axis=0, tiled=True)
+    packed, slot_flags = pack_cache(prev_cache, dest_device)
+    pieces, packed, slot_flags = lax.optimization_barrier((pieces, packed, slot_flags))
     q_cols = query_weight.shape[1]
     k_cols = key_weight.shape[1]
     block_rows = query_weight.shape[0]
@@ -190,8 +198,8 @@
     values_new = value_proj.astype(jnp.bfloat16)
     span_here = jnp.concatenate([keys_new, values_new], axis=1)
     span_all = lax.all_gather(span_here, ("dz", "dc"), axis=0, tiled=True)
-    prev_cache, span_all = lax.optimization_barrier((prev_cache, span_all))
-    decode_cache = relayout(prev_cache, dest_device)
+    packed, slot_flags, span_all = lax.optimization_barrier((packed, slot_flags, span_all))
+    decode_cache = unpack_cache(packed, slot_flags)
     score_scale = HD ** (-0.5)
     carried = (
         jnp.full((local_kv, group_size, row_count), NEG_BIG, jnp.float32),

time: 392 us -> 418 us (1.066)
  waiting for transfers between devices: 177 us -> 215 us
  other arithmetic: 64.3 us -> 51.9 us
    all_to_all x2, waiting for transfers between devices: 10.4 us -> 48.7 us  [the longest x1 48.7 us: unpack_cache(): lax.all_to_all(packed, ('dz', 'dc'), split_axis=0, concat_axis=0, tiled=T...]
    select_n x5 -> x1, other arithmetic: 12.2 us -> 0.01 us  [pack_cache(): slot_rank = jnp.arange(slot_count, dtype=jnp.int32) % CAP]
    all_to_all x1, waiting for transfers between devices: 86.7 us -> 80.3 us  [per_device(): lax.all_to_all(spread, 'mp', split_axis=0, concat_axis=0, tiled=True)]
    all_gather x1, waiting for transfers between devices: 79 us -> 84.6 us  [per_device(): weights_all = lax.all_gather(weights_here, ('dz', 'dc'), axis=0, tiled=True)]
  transfers between devices with their start and end apart: 5 -> 5, of which waited for: 4 -> 4; matrix products, arithmetic and copies ran while one was open for 38% -> 33% of each run, Pallas kernels for 0% -> 0%
where the time goes in v7:
time: 418 us; the launch traced here: 412 us
  waiting for transfers between devices  215 us (51%)
  matrix products  75.6 us (18%)
  other arithmetic  51.9 us (12%)
  local copies, waits for them, and re-layouts  36.3 us (9%)
  starting transfers between devices  18.3 us (4%)
  between operations  14.4 us (3%)
    all_gather x1, waiting for transfers between devices, per_device(): weights_all = lax.all_gather(weights_here, ('dz', 'dc'), axis=0, tiled=True)  84.6 us
    all_to_all x1, waiting for transfers between devices, per_device(): lax.all_to_all(spread, 'mp', split_axis=0, concat_axis=0, tiled=True)  80.3 us
    all_to_all x1, waiting for transfers between devices, unpack_cache(): lax.all_to_all(packed, ('dz', 'dc'), split_axis=0, concat_axis=0, tiled=T...  48.7 us
    reduce_sum x2, other arithmetic, attend(): total_sum = total_sum * factor + jnp.sum(weights, axis=-1)  33.1 us
    dot_general x2, matrix products, attend(): jnp.einsum('kgqs,skd->kgqd', weights.astype(jnp.bfloat16), values_flat, p...  29.6 us
    dot_general x2, matrix products, attend(): jnp.einsum('kgqd,skd->kgqs', queries, keys_flat, preferred_element_type=j...  28.4 us
    dot_general x1, matrix products, per_device(): jnp.einsum('jtf,jfc->tc', normed, weights_all.reshape(mp_size, -1, weight...  17.6 us
  transfers between devices with their start and end apart: 5, of which 4 were waited for; matrix products, arithmetic and copies ran while one was open for 33% of the time, Pallas kernels for 0%

profile of v7, /device:TPU:104, one launch (start us, length us, event | category | flops | bytes accessed | tf_op | source)
XLA Modules:
  0.0 411.5 jit_solution(9092856675429090147)
XLA Ops:
  7.2 0.0 all-gather.3.cloned.1.call-start
  7.2 0.8 pad_maximum_fusion.4
  8.0 0.1 reshape.456
  8.1 2.6 pad_maximum_fusion
  10.7 0.0 all-gather.3.cloned.1.call-update
  10.7 4.6 %broadcast_in_dim.181 = bf16[8,384,1024]{2,1,0:T(8,128)(2,1)} broadcast(bf16[384,1024]{1,0:T(8,128)(2,1)} %param.16), dimensions={1,2} | broadcast | bytes 7077888 | tf_op jit(solution)/shard_map/broadcast_in_dim | solution.py:158
  15.3 6.2 %all-to-all-start = ((bf16[8,384,1024]{2,1,0:T(8,128)(2,1)}), bf16[8,384,1024]{2,1,0:T(8,128)(2,1)}, u32[]{:S(2)}, u32[]{:S(2)}) async-start(bf16[8,384,1024]{2,1,0:T(8,128)(2,1)} %broadcast_in_dim.181), calls=%async_computation | async-start | bytes 12582912 | tf_op jit(solution)/shard_map/all_to_all | solution.py:159
  21.5 0.0 all-gather.5.cloned.1.call-start
  21.6 0.2 convert_reduce_fusion.1
  21.7 0.1 fusion.39
  21.9 0.1 select_reduce_fusion.1
  22.0 0.0 copy-start.9
  22.1 7.4 %gather_fusion = bf16[32,4,2,128,128]{4,3,2,1,0:T(8,128)(2,1)} fusion(bf16[16,4,2,128,128]{4,3,2,1,0:T(8,128)(2,1)} %param.30, s32[1024]{0:T(1024)S(1)} %pad_clamp_fusion.1), kind=kCustom, calls=%fused_computation | custom fusion | bytes 16777344 | tf_op jit(solution)/shard_map/jit(_take)/gather | solution.py:110
  29.5 0.2 reduce-window.16
  29.7 0.1 convert_reduce_fusion.2
  29.8 0.1 select_reduce_fusion.5
  29.9 0.1 select_reduce_fusion.4
  30.0 0.4 multiply_cosine_fusion
  30.4 80.3 %all-to-all-done = bf16[8,384,1024]{2,1,0:T(8,128)(2,1)} async-done(((bf16[8,384,1024]{2,1,0:T(8,128)(2,1)}), bf16[8,384,1024]{2,1,0:T(8,128)(2,1)}, u32[]{:S(2)}, u32[]{:S(2)}) %all-to-all-start) | async-done | bytes 6291488 | tf_op jit(solution)/shard_map/all_to_all | solution.py:159
  110.7 4.2 %fusion.9 = f32[384]{0:T(512)S(1)} fusion(bf16[8,384,1024]{2,1,0:T(8,128)(2,1)} %all-to-all-done), kind=kLoop, calls=%fused_computation.16 | loop fusion | flops 9436800 | bytes 6292992 | tf_op jit(solution)/shard_map/reduce_sum | solution.py:174
  114.8 84.6 %all-gather.3.cloned.1.call-done = bf16[8192,1344]{1,0:T(8,128)(2,1)} async-done(((bf16[512,1344]{1,0:T(8,128)(2,1)}), bf16[8192,1344]{1,0:T(8,128)(2,1)}) %all-gather.3.cloned.1.call-update) | async-done | bytes 22020112 | tf_op jit(solution)/shard_map/all_gather | solution.py:167
  199.5 17.6 %fusion.19 = f32[384,1344]{0,1:T(8,128)S(1)} fusion(bf16[8,1024,1344]{2,1,0:T(8,128)(2,1)} %bitcast.67, bf16[8,384,1024]{2,1,0:T(8,128)(2,1)} %all-to-all-done, f32[8,1024]{1,0:T(8,128)S(1)} %reshape.465, f32[384]{0:T(512)S(1)} %add_rsqrt_fusion), kind=kOutput, calls=%fused_computation.26 | convolution fusion | flops 8468299776 | bytes 30410240 | tf_op jit(solution)/shard_map/jtf,jfc->tc/dot_general | solution.py:179
  217.1 0.1 fusion.31
  217.2 0.1 fusion.30
  217.3 0.9 pad_maximum_fusion.3
  218.2 0.0 all-gather.5.cloned.1.call-update
  218.3 0.1 select_reduce_fusion.2
  218.4 0.1 fusion.36
  218.5 0.1 convert_reduce_fusion
  218.6 0.1 broadcast_bitcast_fusion.1
  218.7 0.1 broadcast_bitcast_fusion
  218.8 0.1 fusion.34
  218.9 2.1 and_reduce_fusion
  220.9 1.2 compare_and_fusion
  222.1 0.8 copy.52
  222.9 0.8 copy.56
  223.8 1.6 slice_add_fusion
  225.4 1.3 fusion.48
  226.7 2.8 copy.67
  229.4 2.7 copy.68
  232.2 1.6 copy.53
  233.8 1.7 slice.55
  235.6 2.2 reshape.461
  237.8 1.5 fusion.49
  239.2 1.6 negate_bitcast_fusion
  240.9 1.5 fusion.27
  242.5 10.7 %fusion.3 = (f32[8,384]{1,0:T(8,128)S(1)}, f32[8,384,2048]{2,1,0:T(8,128)}) fusion(pred[384,2048]{1,0:T(8,128)(4,1)S(1)} %copy-done, bf16[8,384,128]{2,1,0:T(8,128)(2,1)S(1)} %fusion.27, bf16[2048,128,1]{1,0,2:T(8,128)(2,1)S(1)} %bitcast.64), kind=kOutput, calls=%fused_computation.9 | convolution fusion | flops 1629484032 | bytes 27275264 | tf_op jit(solution)/shard_map/kgqd,skd->kgqs/dot_general | solution.py:68
  253.1 1.3 all-gather.5.cloned.1.call-done
  254.4 0.7 all_to_all.16
  255.1 6.3 %all-to-all-start.2 = ((bf16[16,2,1]{1,2,0:T(2,128)(2,1)}), bf16[16,2,1]{1,2,0:T(2,128)(2,1)S(1)}, u32[]{:S(2)}, u32[]{:S(2)}) async-start(bf16[16,2,1]{1,2,0:T(2,128)(2,1)} %all_to_all.16), calls=%async_computation.2 | async-start | bytes 16384 | tf_op jit(solution)/shard_map/all_to_all | solution.py:120
  261.5 17.8 %fusion = (f32[8,384]{1,0:T(8,128)S(1)}, f32[8,384,3456]{2,1,0:T(8,128)}) fusion(pred[384,3456]{1,0:T(8,128)(4,1)S(1)} %compare_and_fusion, bf16[8,384,128]{2,1,0:T(8,128)(2,1)S(1)} %fusion.27, bf16[6144,256]{0,1:T(8,128)(2,1)} %all-gather.5.cloned.1.call-done, s32[]{:T(128)S(6)} %max.20), kind=kOutput, calls=%fused_computation.4 | convolution fusion | flops 2749756416 | bytes 45477892 | tf_op jit(solution)/shard_map/kgqd,skd->kgqs/dot_general | solution.py:68
  279.2 21.1 %fusion.1 = f32[8,384]{1,0:T(8,128)S(1)} fusion(f32[8,384,3456]{2,1,0:T(8,128)} %get-tuple-element.46, f32[8,384]{1,0:T(8,128)S(1)} %get-tuple-element.39, pred[384,3456]{1,0:T(8,128)(4,1)S(1)} %compare_and_fusion), kind=kLoop, calls=%fused_computation.5 | loop fusion | flops 53081088 | bytes 43819008 | tf_op jit(solution)/shard_map/reduce_sum | solution.py:76
  300.4 5.7 %all-to-all-start.1 = ((bf16[32,4,2,128,128]{4,3,2,1,0:T(8,128)(2,1)}), bf16[32,4,2,128,128]{4,3,2,1,0:T(8,128)(2,1)}, u32[]{:S(2)}, u32[]{:S(2)}) async-start(bf16[32,4,2,128,128]{4,3,2,1,0:T(8,128)(2,1)} %gather_fusion), calls=%async_computation.1 | async-start | bytes 16777216 | tf_op jit(solution)/shard_map/all_to_all | solution.py:119
  306.1 12.0 %fusion.7 = f32[8,384]{1,0:T(8,128)S(1)} fusion(f32[8,384,2048]{2,1,0:T(8,128)} %get-tuple-element.44, f32[8,384]{1,0:T(8,128)S(1)} %get-tuple-element.40, pred[384,2048]{1,0:T(8,128)(4,1)S(1)} %copy-done), kind=kLoop, calls=%fused_computation.12 | loop fusion | flops 31454208 | bytes 25976832 | tf_op jit(solution)/shard_map/reduce_sum | solution.py:76
  318.1 11.2 %fusion.12 = f32[8,384,128]{1,2,0:T(8,128)S(1)} fusion(bf16[2048,128,1]{1,0,2:T(8,128)(2,1)S(1)} %bitcast.66, f32[8,384,2048]{2,1,0:T(8,128)} %get-tuple-element.44, f32[8,384]{1,0:T(8,128)S(1)} %get-tuple-element.40, pred[384,2048]{1,0:T(8,128)(4,1)S(1)} %copy-done), kind=kOutput, calls=%fused_computation.19 | convolution fusion | flops 1642070016 | bytes 28061696 | tf_op jit(solution)/shard_map/kgqs,skd->kgqd/dot_general | solution.py:77
  329.3 18.4 %divide_convert_fusion = bf16[8,384,128]{1,2,0:T(8,128)(2,1)S(1)} fusion(f32[8,384,128]{1,2,0:T(8,128)S(1)} %fusion.12, f32[8,384,3456]{2,1,0:T(8,128)} %get-tuple-element.46, f32[8,384]{1,0:T(8,128)S(1)} %get-tuple-element.39, pred[384,3456]{1,0:T(8,128)(4,1)S(1)} %compare_and_fusion, bf16[6144,256]{0,1:T(8,128)(2,1)} %all-gather.5.cloned.1.call-done, ...), kind=kOutput, calls=%fused_computation.31 | convolution fusion | flops 2772959232 | bytes 47087624 | tf_op jit(solution)/shard_map/kgqs,skd->kgqd/dot_general | solution.py:77
  347.7 1.2 copy.61
  349.0 0.1 reshape.490
  349.0 0.1 reduce-window.17
  349.1 0.1 gt.25
  349.2 0.1 add_reduce_fusion
  349.3 0.1 select_reduce_fusion
  349.5 48.7 %all-to-all-done.1 = bf16[32,4,2,128,128]{4,3,2,1,0:T(8,128)(2,1)} async-done(((bf16[32,4,2,128,128]{4,3,2,1,0:T(8,128)(2,1)}), bf16[32,4,2,128,128]{4,3,2,1,0:T(8,128)(2,1)}, u32[]{:S(2)}, u32[]{:S(2)}) %all-to-all-start.1) | async-done | bytes 8388640 | tf_op jit(solution)/shard_map/all_to_all | solution.py:119
  398.2 6.5 %gather_fusion.1 = bf16[16,4,2,128,128]{4,3,2,1,0:T(8,128)(2,1)} fusion(bf16[32,4,2,128,128]{4,3,2,1,0:T(8,128)(2,1)} %all-to-all-done.1, s32[1024]{0:T(1024)S(1)} %pad_clamp_fusion), kind=kCustom, calls=%fused_computation.1 | custom fusion | bytes 8388672 | tf_op jit(solution)/shard_map/jit(_take)/gather | solution.py:128
  (47 shorter events, 0.3 us)
Async XLA Ops:
  7.2 192.3 %all-gather.3.cloned.1.call-start = ((), (), s32[]{:S(2)}) async-start(), calls=%async_computation.3 | async-start | bytes 24510464 | tf_op jit(solution)/shard_map/all_gather | solution.py:167
  15.3 6.2 %copy-start.8 = (s32[16,1]{0,1:T(1,128)S(1)}, s32[16,1]{0,1:T(1,128)}, u32[]{:S(2)}) copy-start(s32[16,1]{0,1:T(1,128)} %param.31) | copy-start | bytes 196
  15.3 6.5 %copy-start.4 = (bf16[8192]{0:T(1024)(128)(2,1)S(1)}, bf16[8192]{0:T(1024)(128)(2,1)}, u32[]{:S(2)}) copy-start(bf16[8192]{0:T(1024)(128)(2,1)} %param.17) | copy-start | bytes 49156
  15.3 6.6 %copy-start.10 = (bf16[128]{0:T(256)(128)(2,1)S(1)}, bf16[128]{0:T(256)(128)(2,1)}, u32[]{:S(2)}) copy-start(bf16[128]{0:T(256)(128)(2,1)} %param.22) | copy-start | bytes 772
  15.3 6.6 %copy-start.11 = (bf16[128]{0:T(256)(128)(2,1)S(1)}, bf16[128]{0:T(256)(128)(2,1)}, u32[]{:S(2)}) copy-start(bf16[128]{0:T(256)(128)(2,1)} %param.23) | copy-start | bytes 772
  15.3 95.4 %all-to-all-start = ((bf16[8,384,1024]{2,1,0:T(8,128)(2,1)}), bf16[8,384,1024]{2,1,0:T(8,128)(2,1)}, u32[]{:S(2)}, u32[]{:S(2)}) async-start(bf16[8,384,1024]{2,1,0:T(8,128)(2,1)} %broadcast_in_dim.181), calls=%async_computation | async-start | bytes 12582912 | tf_op jit(solution)/shard_map/all_to_all | solution.py:159
  21.5 232.9 %all-gather.5.cloned.1.call-start = ((), (), s32[]{:S(2)}) async-start(), calls=%async_computation.4 | async-start | bytes 3342336 | tf_op jit(solution)/shard_map/all_gather | solution.py:200
  22.0 7.4 %copy-start.12 = (s32[3]{0:T(128)S(1)}, s32[3]{0:T(128)}, u32[]{:S(2)}) copy-start(s32[3]{0:T(128)} %param.24) | copy-start | bytes 40
  22.0 7.7 %copy-start.9 = (s32[3]{0:T(128)S(1)}, s32[3]{0:T(128)}, u32[]{:S(2)}) copy-start(s32[3]{0:T(128)} %param.25) | copy-start | bytes 40
  22.0 7.8 %copy-start.6 = (s32[4]{0:T(128)S(1)}, s32[4]{0:T(128)}, u32[]{:S(2)}) copy-start(s32[4]{0:T(128)} %param.26) | copy-start | bytes 52
  199.5 18.8 %copy-start.7 = (bf16[1024]{0:T(1024)(128)(2,1)S(1)}, bf16[1024]{0:T(1024)(128)(2,1)}, u32[]{:S(2)}) copy-start(bf16[1024]{0:T(1024)(128)(2,1)} %param.21) | copy-start | bytes 6148
  199.5 18.8 %copy-start.5 = (s32[4,4]{1,0:T(4,128)S(1)}, s32[4,4]{1,0:T(4,128)}, u32[]{:S(2)}) copy-start(s32[4,4]{1,0:T(4,128)} %param.27) | copy-start | bytes 196
  217.0 1.8 copy-start.3
  237.8 3.1 copy-start.1
  237.8 3.1 copy-start.2
  237.8 4.7 %copy-start = (pred[384,2048]{1,0:T(8,128)(4,1)S(1)}, pred[384,2048]{1,0:T(8,128)(4,1)}, u32[]{:S(2)}) copy-start(pred[384,2048]{1,0:T(8,128)(4,1)} %and_reduce_fusion) | copy-start | bytes 2359300
  255.1 45.2 %all-to-all-start.2 = ((bf16[16,2,1]{1,2,0:T(2,128)(2,1)}), bf16[16,2,1]{1,2,0:T(2,128)(2,1)S(1)}, u32[]{:S(2)}, u32[]{:S(2)}) async-start(bf16[16,2,1]{1,2,0:T(2,128)(2,1)} %all_to_all.16), calls=%async_computation.2 | async-start | bytes 16384 | tf_op jit(solution)/shard_map/all_to_all | solution.py:120
  300.4 97.8 %all-to-all-start.1 = ((bf16[32,4,2,128,128]{4,3,2,1,0:T(8,128)(2,1)}), bf16[32,4,2,128,128]{4,3,2,1,0:T(8,128)(2,1)}, u32[]{:S(2)}, u32[]{:S(2)}) async-start(bf16[32,4,2,128,128]{4,3,2,1,0:T(8,128)(2,1)} %gather_fusion), calls=%async_computation.1 | async-start | bytes 16777216 | tf_op jit(solution)/shard_map/all_to_all | solution.py:119
Sparse Core Ops, SparseCore 0:
  10.8 188.5 all-gather.2
  218.4 36.0 all-gather.4

commit v8 on v7

--- a/solution.py
+++ b/solution.py
@@ -112,13 +112,14 @@
     return packed, slot_flags
 
 
-def unpack_cache(packed, slot_flags):
+def swap_flags(slot_flags):
+    return lax.all_to_all(slot_flags, ("dz", "dc"), split_axis=0, concat_axis=0, tiled=True)
+
+
+def unpack_cache(packed, arrived_flags):
     blocks_here = packed.shape[0] // CAP
     slot_count = packed.shape[0]
-    arrived, arrived_flags = (
-        lax.all_to_all(packed, ("dz", "dc"), split_axis=0, concat_axis=0, tiled=True),
-        lax.all_to_all(slot_flags, ("dz", "dc"), split_axis=0, concat_axis=0, tiled=True),
-    )
+    arrived = lax.all_to_all(packed, ("dz", "dc"), split_axis=0, concat_axis=0, tiled=True)
     arrived_live = arrived_flags > 0.5
     order_no = jnp.cumsum(arrived_live.astype(jnp.int32)) - 1
     picked = arrived_live[None, :] & (
@@ -159,6 +160,7 @@
     pieces = lax.all_to_all(spread, "mp", split_axis=0, concat_axis=0, tiled=True)
     packed, slot_flags = pack_cache(prev_cache, dest_device)
     pieces, packed, slot_flags = lax.optimization_barrier((pieces, packed, slot_flags))
+    arrived_flags = swap_flags(slot_flags)
     q_cols = query_weight.shape[1]
     k_cols = key_weight.shape[1]
     block_rows = query_weight.shape[0]
@@ -198,8 +200,8 @@
     values_new = value_proj.astype(jnp.bfloat16)
     span_here = jnp.concatenate([keys_new, values_new], axis=1)
     span_all = lax.all_gather(span_here, ("dz", "dc"), axis=0, tiled=True)
-    packed, slot_flags, span_all = lax.optimization_barrier((packed, slot_flags, span_all))
-    decode_cache = unpack_cache(packed, slot_flags)
+    packed, arrived_flags, span_all = lax.optimization_barrier((packed, arrived_flags, span_all))
+    decode_cache = unpack_cache(packed, arrived_flags)
     score_scale = HD ** (-0.5)
     carried = (
         jnp.full((local_kv, group_size, row_count), NEG_BIG, jnp.float32),

time: 418 us -> 382 us (0.914)
  waiting for transfers between devices: 215 us -> 178 us
    all_to_all x1, waiting for transfers between devices: 48.7 us -> 10.1 us  [unpack_cache(): lax.all_to_all(packed, ('dz', 'dc'), split_axis=0, concat_axis=0, tiled=T...]
  transfers between devices with their start and end apart: 5 -> 5, of which waited for: 4 -> 4; matrix products, arithmetic and copies ran while one was open for 33% -> 36% of each run, Pallas kernels for 0% -> 0%
where the time goes in v8:
time: 382 us; the launch traced here: 376 us
  waiting for transfers between devices  178 us (47%)
  matrix products  75.2 us (20%)
  other arithmetic  51.8 us (14%)
  local copies, waits for them, and re-layouts  36.4 us (10%)
  starting transfers between devices  19.5 us (5%)
  between operations  14.4 us (4%)
    all_gather x1, waiting for transfers between devices, per_device(): weights_all = lax.all_gather(weights_here, ('dz', 'dc'), axis=0, tiled=True)  84.6 us
    all_to_all x1, waiting for transfers between devices, per_device(): lax.all_to_all(spread, 'mp', split_axis=0, concat_axis=0, tiled=True)  80.3 us
    reduce_sum x2, other arithmetic, attend(): total_sum = total_sum * factor + jnp.sum(weights, axis=-1)  33.1 us
    dot_general x2, matrix products, attend(): jnp.einsum('kgqs,skd->kgqd', weights.astype(jnp.bfloat16), values_flat, p...  29.6 us
    dot_general x2, matrix products, attend(): jnp.einsum('kgqd,skd->kgqs', queries, keys_flat, preferred_element_type=j...  28.3 us
    dot_general x1, matrix products, per_device(): jnp.einsum('jtf,jfc->tc', normed, weights_all.reshape(mp_size, -1, weight...  17.4 us
    all_to_all x1, waiting for transfers between devices, unpack_cache(): lax.all_to_all(packed, ('dz', 'dc'), split_axis=0, concat_axis=0, tiled=T...  10.1 us
  transfers between devices with their start and end apart: 5, of which 4 were waited for; matrix products, arithmetic and copies ran while one was open for 36% of the time, Pallas kernels for 0%

profile of v8, /device:TPU:104, one launch (start us, length us, event | category | flops | bytes accessed | tf_op | source)
XLA Modules:
  0.0 375.7 jit_solution(5935564090043454975)
XLA Ops:
  7.2 0.0 all-gather.3.cloned.1.call-start
  7.2 0.8 pad_maximum_fusion.4
  8.0 0.1 reshape.438
  8.1 2.6 pad_maximum_fusion
  10.7 0.0 all-gather.3.cloned.1.call-update
  10.7 4.6 %broadcast_in_dim.181 = bf16[8,384,1024]{2,1,0:T(8,128)(2,1)} broadcast(bf16[384,1024]{1,0:T(8,128)(2,1)} %param.16), dimensions={1,2} | broadcast | bytes 7077888 | tf_op jit(solution)/shard_map/broadcast_in_dim | solution.py:159
  15.3 6.2 %all-to-all-start = ((bf16[8,384,1024]{2,1,0:T(8,128)(2,1)}), bf16[8,384,1024]{2,1,0:T(8,128)(2,1)}, u32[]{:S(2)}, u32[]{:S(2)}) async-start(bf16[8,384,1024]{2,1,0:T(8,128)(2,1)} %broadcast_in_dim.181), calls=%async_computation | async-start | bytes 12582912 | tf_op jit(solution)/shard_map/all_to_all | solution.py:160
  21.5 0.0 all-gather.5.cloned.1.call-start
  21.6 0.2 convert_reduce_fusion.1
  21.7 0.1 fusion.38
  21.9 0.1 select_reduce_fusion.1
  22.0 0.0 copy-start.9
  22.1 7.4 %gather_fusion = bf16[32,4,2,128,128]{4,3,2,1,0:T(8,128)(2,1)} fusion(bf16[16,4,2,128,128]{4,3,2,1,0:T(8,128)(2,1)} %param.30, s32[1024]{0:T(1024)S(1)} %pad_clamp_fusion.1), kind=kCustom, calls=%fused_computation | custom fusion | bytes 16777344 | tf_op jit(solution)/shard_map/jit(_take)/gather | solution.py:110
  29.5 0.2 reduce-window.16
  29.7 0.1 convert_reduce_fusion.2
  29.8 0.1 select_reduce_fusion.5
  29.9 0.1 select_reduce_fusion.4
  30.0 0.4 multiply_cosine_fusion
  30.4 80.3 %all-to-all-done = bf16[8,384,1024]{2,1,0:T(8,128)(2,1)} async-done(((bf16[8,384,1024]{2,1,0:T(8,128)(2,1)}), bf16[8,384,1024]{2,1,0:T(8,128)(2,1)}, u32[]{:S(2)}, u32[]{:S(2)}) %all-to-all-start) | async-done | bytes 6291488 | tf_op jit(solution)/shard_map/all_to_all | solution.py:160
  110.7 4.2 %fusion.9 = f32[384]{0:T(512)S(1)} fusion(bf16[8,384,1024]{2,1,0:T(8,128)(2,1)} %all-to-all-done), kind=kLoop, calls=%fused_computation.16 | loop fusion | flops 9436800 | bytes 6292992 | tf_op jit(solution)/shard_map/reduce_sum | solution.py:176
  114.8 84.6 %all-gather.3.cloned.1.call-done = bf16[8192,1344]{1,0:T(8,128)(2,1)} async-done(((bf16[512,1344]{1,0:T(8,128)(2,1)}), bf16[8192,1344]{1,0:T(8,128)(2,1)}) %all-gather.3.cloned.1.call-update) | async-done | bytes 22020112 | tf_op jit(solution)/shard_map/all_gather | solution.py:169
  199.5 17.4 %fusion.19 = f32[384,1344]{0,1:T(8,128)S(1)} fusion(bf16[8,1024,1344]{2,1,0:T(8,128)(2,1)} %bitcast.69, bf16[8,384,1024]{2,1,0:T(8,128)(2,1)} %all-to-all-done, f32[8,1024]{1,0:T(8,128)S(1)} %reshape.448, f32[384]{0:T(512)S(1)} %add_rsqrt_fusion), kind=kOutput, calls=%fused_computation.26 | convolution fusion | flops 8468299776 | bytes 30410240 | tf_op jit(solution)/shard_map/jtf,jfc->tc/dot_general | solution.py:181
  216.9 0.1 fusion.31
  217.0 0.1 fusion.30
  217.1 0.9 pad_maximum_fusion.3
  218.1 0.0 all-gather.5.cloned.1.call-update
  218.1 0.1 select_reduce_fusion.2
  218.2 0.1 fusion.35
  218.3 0.1 convert_reduce_fusion
  218.4 0.1 broadcast_bitcast_fusion.1
  218.5 0.1 broadcast_bitcast_fusion
  218.6 0.1 fusion.34
  218.7 2.1 and_reduce_fusion
  220.8 1.2 compare_and_fusion
  221.9 0.7 all_to_all.19
  222.6 5.7 %all-to-all-start.1 = ((bf16[16,2,1]{1,2,0:T(2,128)(2,1)}), bf16[16,2,1]{1,2,0:T(2,128)(2,1)S(1)}, u32[]{:S(2)}, u32[]{:S(2)}) async-start(bf16[16,2,1]{1,2,0:T(2,128)(2,1)} %all_to_all.19), calls=%async_computation.1 | async-start | bytes 16384 | tf_op jit(solution)/shard_map/all_to_all | solution.py:116
  228.3 3.2 all-to-all-done.1
  231.6 0.1 all_to_all.17
  231.7 0.8 copy.52
  232.5 0.8 copy.56
  233.3 1.6 slice_add_fusion
  234.9 1.3 fusion.47
  236.2 2.8 copy.67
  239.0 2.8 copy.68
  241.8 1.6 copy.53
  243.4 1.8 slice.55
  245.2 2.2 reshape.443
  247.4 1.4 fusion.48
  248.9 1.6 negate_bitcast_fusion
  250.5 1.5 fusion.27
  252.1 10.5 %fusion.3 = (f32[8,384]{1,0:T(8,128)S(1)}, f32[8,384,2048]{2,1,0:T(8,128)}) fusion(pred[384,2048]{1,0:T(8,128)(4,1)S(1)} %copy-done, bf16[8,384,128]{2,1,0:T(8,128)(2,1)S(1)} %fusion.27, bf16[2048,128,1]{1,0,2:T(8,128)(2,1)S(1)} %bitcast.66), kind=kOutput, calls=%fused_computation.9 | convolution fusion | flops 1629484032 | bytes 27275264 | tf_op jit(solution)/shard_map/kgqd,skd->kgqs/dot_general | solution.py:68
  262.6 0.1 copy.60
  262.7 0.1 reduce-window.17
  262.7 7.6 %all-to-all-start.2 = ((bf16[32,4,2,128,128]{4,3,2,1,0:T(8,128)(2,1)}), bf16[32,4,2,128,128]{4,3,2,1,0:T(8,128)(2,1)}, u32[]{:S(2)}, u32[]{:S(2)}) async-start(bf16[32,4,2,128,128]{4,3,2,1,0:T(8,128)(2,1)} %gather_fusion), calls=%async_computation.2 | async-start | bytes 16777216 | tf_op jit(solution)/shard_map/all_to_all | solution.py:122
  270.3 17.8 %fusion = (f32[8,384]{1,0:T(8,128)S(1)}, f32[8,384,3456]{2,1,0:T(8,128)}) fusion(pred[384,3456]{1,0:T(8,128)(4,1)S(1)} %compare_and_fusion, bf16[8,384,128]{2,1,0:T(8,128)(2,1)S(1)} %fusion.27, bf16[6144,256]{0,1:T(8,128)(2,1)} %all-gather.5.cloned.1.call-done, s32[]{:T(128)S(6)} %max.20), kind=kOutput, calls=%fused_computation.4 | convolution fusion | flops 2749756416 | bytes 45477892 | tf_op jit(solution)/shard_map/kgqd,skd->kgqs/dot_general | solution.py:68
  288.0 21.1 %fusion.1 = f32[8,384]{1,0:T(8,128)S(1)} fusion(f32[8,384,3456]{2,1,0:T(8,128)} %get-tuple-element.48, f32[8,384]{1,0:T(8,128)S(1)} %get-tuple-element.39, pred[384,3456]{1,0:T(8,128)(4,1)S(1)} %compare_and_fusion), kind=kLoop, calls=%fused_computation.5 | loop fusion | flops 53081088 | bytes 43819008 | tf_op jit(solution)/shard_map/reduce_sum | solution.py:76
  309.2 12.0 %fusion.7 = f32[8,384]{1,0:T(8,128)S(1)} fusion(f32[8,384,2048]{2,1,0:T(8,128)} %get-tuple-element.46, f32[8,384]{1,0:T(8,128)S(1)} %get-tuple-element.40, pred[384,2048]{1,0:T(8,128)(4,1)S(1)} %copy-done), kind=kLoop, calls=%fused_computation.12 | loop fusion | flops 31454208 | bytes 25976832 | tf_op jit(solution)/shard_map/reduce_sum | solution.py:76
  321.2 11.2 %fusion.12 = f32[8,384,128]{1,2,0:T(8,128)S(1)} fusion(bf16[2048,128,1]{1,0,2:T(8,128)(2,1)S(1)} %bitcast.68, f32[8,384,2048]{2,1,0:T(8,128)} %get-tuple-element.46, f32[8,384]{1,0:T(8,128)S(1)} %get-tuple-element.40, pred[384,2048]{1,0:T(8,128)(4,1)S(1)} %copy-done), kind=kOutput, calls=%fused_computation.19 | convolution fusion | flops 1642070016 | bytes 28061696 | tf_op jit(solution)/shard_map/kgqs,skd->kgqd/dot_general | solution.py:77
  332.4 18.4 %divide_convert_fusion = bf16[8,384,128]{1,2,0:T(8,128)(2,1)S(1)} fusion(f32[8,384,128]{1,2,0:T(8,128)S(1)} %fusion.12, f32[8,384,3456]{2,1,0:T(8,128)} %get-tuple-element.48, f32[8,384]{1,0:T(8,128)S(1)} %get-tuple-element.39, pred[384,3456]{1,0:T(8,128)(4,1)S(1)} %compare_and_fusion, bf16[6144,256]{0,1:T(8,128)(2,1)} %all-gather.5.cloned.1.call-done, ...), kind=kOutput, calls=%fused_computation.31 | convolution fusion | flops 2772959232 | bytes 47087624 | tf_op jit(solution)/shard_map/kgqs,skd->kgqd/dot_general | solution.py:77
  350.8 1.2 copy.61
  352.0 0.1 add_reduce_fusion
  352.1 0.1 select_reduce_fusion
  352.2 10.1 %all-to-all-done.2 = bf16[32,4,2,128,128]{4,3,2,1,0:T(8,128)(2,1)} async-done(((bf16[32,4,2,128,128]{4,3,2,1,0:T(8,128)(2,1)}), bf16[32,4,2,128,128]{4,3,2,1,0:T(8,128)(2,1)}, u32[]{:S(2)}, u32[]{:S(2)}) %all-to-all-start.2) | async-done | bytes 8388640 | tf_op jit(solution)/shard_map/all_to_all | solution.py:122
  362.3 6.5 %gather_fusion.1 = bf16[16,4,2,128,128]{4,3,2,1,0:T(8,128)(2,1)} fusion(bf16[32,4,2,128,128]{4,3,2,1,0:T(8,128)(2,1)} %all-to-all-done.2, s32[1024]{0:T(1024)S(1)} %pad_clamp_fusion), kind=kCustom, calls=%fused_computation.1 | custom fusion | bytes 8388672 | tf_op jit(solution)/shard_map/jit(_take)/gather | solution.py:129
  (47 shorter events, 0.2 us)
Async XLA Ops:
  7.2 192.3 %all-gather.3.cloned.1.call-start = ((), (), s32[]{:S(2)}) async-start(), calls=%async_computation.3 | async-start | bytes 24510464 | tf_op jit(solution)/shard_map/all_gather | solution.py:169
  15.3 6.2 %copy-start.8 = (s32[16,1]{0,1:T(1,128)S(1)}, s32[16,1]{0,1:T(1,128)}, u32[]{:S(2)}) copy-start(s32[16,1]{0,1:T(1,128)} %param.31) | copy-start | bytes 196
  15.3 6.5 %copy-start.4 = (bf16[8192]{0:T(1024)(128)(2,1)S(1)}, bf16[8192]{0:T(1024)(128)(2,1)}, u32[]{:S(2)}) copy-start(bf16[8192]{0:T(1024)(128)(2,1)} %param.17) | copy-start | bytes 49156
  15.3 6.6 %copy-start.10 = (bf16[128]{0:T(256)(128)(2,1)S(1)}, bf16[128]{0:T(256)(128)(2,1)}, u32[]{:S(2)}) copy-start(bf16[128]{0:T(256)(128)(2,1)} %param.22) | copy-start | bytes 772
  15.3 6.6 %copy-start.11 = (bf16[128]{0:T(256)(128)(2,1)S(1)}, bf16[128]{0:T(256)(128)(2,1)}, u32[]{:S(2)}) copy-start(bf16[128]{0:T(256)(128)(2,1)} %param.23) | copy-start | bytes 772
  15.3 95.4 %all-to-all-start = ((bf16[8,384,1024]{2,1,0:T(8,128)(2,1)}), bf16[8,384,1024]{2,1,0:T(8,128)(2,1)}, u32[]{:S(2)}, u32[]{:S(2)}) async-start(bf16[8,384,1024]{2,1,0:T(8,128)(2,1)} %broadcast_in_dim.181), calls=%async_computation | async-start | bytes 12582912 | tf_op jit(solution)/shard_map/all_to_all | solution.py:160
  21.5 241.1 %all-gather.5.cloned.1.call-start = ((), (), s32[]{:S(2)}) async-start(), calls=%async_computation.4 | async-start | bytes 3342336 | tf_op jit(solution)/shard_map/all_gather | solution.py:202
  22.0 7.4 %copy-start.12 = (s32[3]{0:T(128)S(1)}, s32[3]{0:T(128)}, u32[]{:S(2)}) copy-start(s32[3]{0:T(128)} %param.24) | copy-start | bytes 40
  22.0 7.7 %copy-start.9 = (s32[3]{0:T(128)S(1)}, s32[3]{0:T(128)}, u32[]{:S(2)}) copy-start(s32[3]{0:T(128)} %param.25) | copy-start | bytes 40
  22.0 7.8 %copy-start.6 = (s32[4]{0:T(128)S(1)}, s32[4]{0:T(128)}, u32[]{:S(2)}) copy-start(s32[4]{0:T(128)} %param.26) | copy-start | bytes 52
  199.5 18.6 %copy-start.7 = (bf16[1024]{0:T(1024)(128)(2,1)S(1)}, bf16[1024]{0:T(1024)(128)(2,1)}, u32[]{:S(2)}) copy-start(bf16[1024]{0:T(1024)(128)(2,1)} %param.21) | copy-start | bytes 6148
  199.5 18.7 %copy-start.5 = (s32[4,4]{1,0:T(4,128)S(1)}, s32[4,4]{1,0:T(4,128)}, u32[]{:S(2)}) copy-start(s32[4,4]{1,0:T(4,128)} %param.27) | copy-start | bytes 196
  216.9 1.8 copy-start.3
  222.6 8.9 %all-to-all-start.1 = ((bf16[16,2,1]{1,2,0:T(2,128)(2,1)}), bf16[16,2,1]{1,2,0:T(2,128)(2,1)S(1)}, u32[]{:S(2)}, u32[]{:S(2)}) async-start(bf16[16,2,1]{1,2,0:T(2,128)(2,1)} %all_to_all.19), calls=%async_computation.1 | async-start | bytes 16384 | tf_op jit(solution)/shard_map/all_to_all | solution.py:116
  247.4 3.1 copy-start.1
  247.4 3.1 copy-start.2
  247.4 4.6 %copy-start = (pred[384,2048]{1,0:T(8,128)(4,1)S(1)}, pred[384,2048]{1,0:T(8,128)(4,1)}, u32[]{:S(2)}) copy-start(pred[384,2048]{1,0:T(8,128)(4,1)} %and_reduce_fusion) | copy-start | bytes 2359300
  262.7 99.6 %all-to-all-start.2 = ((bf16[32,4,2,128,128]{4,3,2,1,0:T(8,128)(2,1)}), bf16[32,4,2,128,128]{4,3,2,1,0:T(8,128)(2,1)}, u32[]{:S(2)}, u32[]{:S(2)}) async-start(bf16[32,4,2,128,128]{4,3,2,1,0:T(8,128)(2,1)} %gather_fusion), calls=%async_computation.2 | async-start | bytes 16777216 | tf_op jit(solution)/shard_map/all_to_all | solution.py:122
Sparse Core Ops, SparseCore 0:
  10.8 188.5 all-gather.2
  218.2 36.0 all-gather.4

commit v9 on v8

--- a/solution.py
+++ b/solution.py
@@ -159,8 +159,8 @@
     spread = jnp.broadcast_to(hidden[None], (mp_size,) + hidden.shape)
     pieces = lax.all_to_all(spread, "mp", split_axis=0, concat_axis=0, tiled=True)
     packed, slot_flags = pack_cache(prev_cache, dest_device)
-    pieces, packed, slot_flags = lax.optimization_barrier((pieces, packed, slot_flags))
     arrived_flags = swap_flags(slot_flags)
+    pieces, packed, arrived_flags = lax.optimization_barrier((pieces, packed, arrived_flags))
     q_cols = query_weight.shape[1]
     k_cols = key_weight.shape[1]
     block_rows = query_weight.shape[0]

time: 382 us -> 373 us (0.976)
  waiting for transfers between devices: 178 us -> 166 us
  blocking collectives: 0 us -> 8.43 us
  starting transfers between devices: 19.5 us -> 13.1 us
    all_gather x1, waiting for transfers between devices: 84.6 us -> 74 us  [per_device(): weights_all = lax.all_gather(weights_here, ('dz', 'dc'), axis=0, tiled=True)]
    all_to_all x0 -> x1, blocking collectives: none -> 8.43 us  [swap_flags(): lax.all_to_all(slot_flags, ('dz', 'dc'), split_axis=0, concat_axis=0, til...]
    all_to_all x1 -> x0, starting transfers between devices: 5.69 us -> none  [swap_flags(): lax.all_to_all(slot_flags, ('dz', 'dc'), split_axis=0, concat_axis=0, til...]
  transfers between devices with their start and end apart: 5 -> 4, of which waited for: 4 -> 4; matrix products, arithmetic and copies ran while one was open for 36% -> 37% of each run, Pallas kernels for 0% -> 0%
where the time goes in v9:
time: 373 us; the launch traced here: 367 us
  waiting for transfers between devices  166 us (45%)
  matrix products  75.6 us (20%)
  other arithmetic  53.4 us (14%)
  local copies, waits for them, and re-layouts  35.8 us (10%)
  between operations  14.4 us (4%)
  starting transfers between devices  13.1 us (4%)
  blocking collectives  8.43 us (2%)
    all_to_all x1, waiting for transfers between devices, per_device(): lax.all_to_all(spread, 'mp', split_axis=0, concat_axis=0, tiled=True)  80.7 us
    all_gather x1, waiting for transfers between devices, per_device(): weights_all = lax.all_gather(weights_here, ('dz', 'dc'), axis=0, tiled=True)  74 us
    reduce_sum x2, other arithmetic, attend(): total_sum = total_sum * factor + jnp.sum(weights, axis=-1)  33.1 us
    dot_general x2, matrix products, attend(): jnp.einsum('kgqs,skd->kgqd', weights.astype(jnp.bfloat16), values_flat, p...  29.6 us
    dot_general x2, matrix products, attend(): jnp.einsum('kgqd,skd->kgqs', queries, keys_flat, preferred_element_type=j...  28.4 us
    dot_general x1, matrix products, per_device(): jnp.einsum('jtf,jfc->tc', normed, weights_all.reshape(mp_size, -1, weight...  17.6 us
    all_to_all x1, waiting for transfers between devices, unpack_cache(): lax.all_to_all(packed, ('dz', 'dc'), split_axis=0, concat_axis=0, tiled=T...  10.1 us
    all_to_all x1, blocking collectives, swap_flags(): lax.all_to_all(slot_flags, ('dz', 'dc'), split_axis=0, concat_axis=0, til...  8.43 us
  transfers between devices with their start and end apart: 4, of which 4 were waited for; matrix products, arithmetic and copies ran while one was open for 37% of the time, Pallas kernels for 0%

profile of v9, /device:TPU:104, one launch (start us, length us, event | category | flops | bytes accessed | tf_op | source)
XLA Modules:
  0.0 366.9 jit_solution(10167636889346974124)
XLA Ops:
  7.2 0.0 all-gather.3.cloned.1.call-start
  7.2 0.8 pad_maximum_fusion.4
  8.0 0.1 reshape.450
  8.1 2.6 pad_maximum_fusion
  10.7 0.0 all-gather.3.cloned.1.call-update
  10.7 0.9 convert_reduce_fusion.1
  11.7 0.7 fusion.38
  12.4 0.1 reshape.486
  12.5 8.4 %all_to_all.19 = bf16[16,2,1]{1,2,0:T(2,128)(2,1)S(1)} all-to-all(bf16[16,2,1]{1,2,0:T(2,128)(2,1)S(1)} %reshape.486), channel_id=1, replica_groups=mesh['dz'=8,'dc'=2,'mp'=8] {'dz','dc'}, dimensions={0} | all-to-all | bytes 128 | tf_op jit(solution)/shard_map/all_to_all | solution.py:116
  20.9 4.8 %broadcast_in_dim.181 = bf16[8,384,1024]{2,1,0:T(8,128)(2,1)} broadcast(bf16[384,1024]{1,0:T(8,128)(2,1)} %param.16), dimensions={1,2} | broadcast | bytes 7077888 | tf_op jit(solution)/shard_map/broadcast_in_dim | solution.py:159
  25.8 6.1 %all-to-all-start = ((bf16[8,384,1024]{2,1,0:T(8,128)(2,1)}), bf16[8,384,1024]{2,1,0:T(8,128)(2,1)}, u32[]{:S(2)}, u32[]{:S(2)}) async-start(bf16[8,384,1024]{2,1,0:T(8,128)(2,1)} %broadcast_in_dim.181), calls=%async_computation | async-start | bytes 12582912 | tf_op jit(solution)/shard_map/all_to_all | solution.py:160
  31.9 0.0 all-gather.5.cloned.1.call-start
  32.0 0.1 select_reduce_fusion.1
  32.1 0.0 copy-start.6
  32.1 7.2 %gather_fusion = bf16[32,4,2,128,128]{4,3,2,1,0:T(8,128)(2,1)} fusion(bf16[16,4,2,128,128]{4,3,2,1,0:T(8,128)(2,1)} %param.30, s32[1024]{0:T(1024)S(1)} %pad_clamp_fusion.1), kind=kCustom, calls=%fused_computation | custom fusion | bytes 16777344 | tf_op jit(solution)/shard_map/jit(_take)/gather | solution.py:110
  39.4 0.2 reduce-window.16
  39.6 0.1 convert_reduce_fusion.2
  39.7 0.1 select_reduce_fusion.5
  39.8 0.1 select_reduce_fusion.4
  39.8 0.4 multiply_cosine_fusion
  40.3 0.1 all_to_all.14
  40.4 80.7 %all-to-all-done = bf16[8,384,1024]{2,1,0:T(8,128)(2,1)} async-done(((bf16[8,384,1024]{2,1,0:T(8,128)(2,1)}), bf16[8,384,1024]{2,1,0:T(8,128)(2,1)}, u32[]{:S(2)}, u32[]{:S(2)}) %all-to-all-start) | async-done | bytes 6291488 | tf_op jit(solution)/shard_map/all_to_all | solution.py:160
  121.1 4.3 %fusion.9 = f32[384]{0:T(512)S(1)} fusion(bf16[8,384,1024]{2,1,0:T(8,128)(2,1)} %all-to-all-done), kind=kLoop, calls=%fused_computation.16 | loop fusion | flops 9436800 | bytes 6292992 | tf_op jit(solution)/shard_map/reduce_sum | solution.py:176
  125.5 74.0 %all-gather.3.cloned.1.call-done = bf16[8192,1344]{1,0:T(8,128)(2,1)} async-done(((bf16[512,1344]{1,0:T(8,128)(2,1)}), bf16[8192,1344]{1,0:T(8,128)(2,1)}) %all-gather.3.cloned.1.call-update) | async-done | bytes 22020112 | tf_op jit(solution)/shard_map/all_gather | solution.py:169
  199.5 17.6 %fusion.19 = f32[384,1344]{0,1:T(8,128)S(1)} fusion(bf16[8,1024,1344]{2,1,0:T(8,128)(2,1)} %bitcast.69, bf16[8,384,1024]{2,1,0:T(8,128)(2,1)} %all-to-all-done, f32[8,1024]{1,0:T(8,128)S(1)} %reshape.461, f32[384]{0:T(512)S(1)} %add_rsqrt_fusion), kind=kOutput, calls=%fused_computation.26 | convolution fusion | flops 8468299776 | bytes 30410240 | tf_op jit(solution)/shard_map/jtf,jfc->tc/dot_general | solution.py:181
  217.1 0.1 fusion.31
  217.2 0.1 fusion.30
  217.3 0.9 pad_maximum_fusion.3
  218.2 0.0 all-gather.5.cloned.1.call-update
  218.3 0.1 select_reduce_fusion.2
  218.4 0.1 fusion.35
  218.5 0.1 convert_reduce_fusion
  218.6 0.1 broadcast_bitcast_fusion.1
  218.7 0.1 broadcast_bitcast_fusion
  218.8 0.1 fusion.34
  218.9 2.1 and_reduce_fusion
  220.9 1.2 compare_and_fusion
  222.1 0.8 copy.53
  222.9 0.8 copy.57
  223.8 1.6 slice_add_fusion
  225.4 1.3 fusion.47
  226.7 2.8 copy.67
  229.4 2.7 copy.68
  232.2 1.6 copy.54
  233.8 1.7 slice.55
  235.6 2.2 reshape.455
  237.8 1.5 fusion.48
  239.2 1.6 negate_bitcast_fusion
  240.9 1.5 fusion.27
  242.5 10.7 %fusion.3 = (f32[8,384]{1,0:T(8,128)S(1)}, f32[8,384,2048]{2,1,0:T(8,128)}) fusion(pred[384,2048]{1,0:T(8,128)(4,1)S(1)} %copy-done, bf16[8,384,128]{2,1,0:T(8,128)(2,1)S(1)} %fusion.27, bf16[2048,128,1]{1,0,2:T(8,128)(2,1)S(1)} %bitcast.66), kind=kOutput, calls=%fused_computation.9 | convolution fusion | flops 1629484032 | bytes 27275264 | tf_op jit(solution)/shard_map/kgqd,skd->kgqs/dot_general | solution.py:68
  253.2 1.3 all-gather.5.cloned.1.call-done
  254.5 0.1 copy.60
  254.5 0.1 reduce-window.17
  254.6 6.9 %all-to-all-start.2 = ((bf16[32,4,2,128,128]{4,3,2,1,0:T(8,128)(2,1)}), bf16[32,4,2,128,128]{4,3,2,1,0:T(8,128)(2,1)}, u32[]{:S(2)}, u32[]{:S(2)}) async-start(bf16[32,4,2,128,128]{4,3,2,1,0:T(8,128)(2,1)} %gather_fusion), calls=%async_computation.2 | async-start | bytes 16777216 | tf_op jit(solution)/shard_map/all_to_all | solution.py:122
  261.5 17.8 %fusion = (f32[8,384]{1,0:T(8,128)S(1)}, f32[8,384,3456]{2,1,0:T(8,128)}) fusion(pred[384,3456]{1,0:T(8,128)(4,1)S(1)} %compare_and_fusion, bf16[8,384,128]{2,1,0:T(8,128)(2,1)S(1)} %fusion.27, bf16[6144,256]{0,1:T(8,128)(2,1)} %all-gather.5.cloned.1.call-done, s32[]{:T(128)S(6)} %max.20), kind=kOutput, calls=%fused_computation.4 | convolution fusion | flops 2749756416 | bytes 45477892 | tf_op jit(solution)/shard_map/kgqd,skd->kgqs/dot_general | solution.py:68
  279.3 21.1 %fusion.1 = f32[8,384]{1,0:T(8,128)S(1)} fusion(f32[8,384,3456]{2,1,0:T(8,128)} %get-tuple-element.48, f32[8,384]{1,0:T(8,128)S(1)} %get-tuple-element.39, pred[384,3456]{1,0:T(8,128)(4,1)S(1)} %compare_and_fusion), kind=kLoop, calls=%fused_computation.5 | loop fusion | flops 53081088 | bytes 43819008 | tf_op jit(solution)/shard_map/reduce_sum | solution.py:76
  300.4 12.0 %fusion.7 = f32[8,384]{1,0:T(8,128)S(1)} fusion(f32[8,384,2048]{2,1,0:T(8,128)} %get-tuple-element.46, f32[8,384]{1,0:T(8,128)S(1)} %get-tuple-element.40, pred[384,2048]{1,0:T(8,128)(4,1)S(1)} %copy-done), kind=kLoop, calls=%fused_computation.12 | loop fusion | flops 31454208 | bytes 25976832 | tf_op jit(solution)/shard_map/reduce_sum | solution.py:76
  312.4 11.2 %fusion.12 = f32[8,384,128]{1,2,0:T(8,128)S(1)} fusion(bf16[2048,128,1]{1,0,2:T(8,128)(2,1)S(1)} %bitcast.68, f32[8,384,2048]{2,1,0:T(8,128)} %get-tuple-element.46, f32[8,384]{1,0:T(8,128)S(1)} %get-tuple-element.40, pred[384,2048]{1,0:T(8,128)(4,1)S(1)} %copy-done), kind=kOutput, calls=%fused_computation.19 | convolution fusion | flops 1642070016 | bytes 28061696 | tf_op jit(solution)/shard_map/kgqs,skd->kgqd/dot_general | solution.py:77
  323.7 18.4 %divide_convert_fusion = bf16[8,384,128]{1,2,0:T(8,128)(2,1)S(1)} fusion(f32[8,384,128]{1,2,0:T(8,128)S(1)} %fusion.12, f32[8,384,3456]{2,1,0:T(8,128)} %get-tuple-element.48, f32[8,384]{1,0:T(8,128)S(1)} %get-tuple-element.39, pred[384,3456]{1,0:T(8,128)(4,1)S(1)} %compare_and_fusion, bf16[6144,256]{0,1:T(8,128)(2,1)} %all-gather.5.cloned.1.call-done, ...), kind=kOutput, calls=%fused_computation.31 | convolution fusion | flops 2772959232 | bytes 47087624 | tf_op jit(solution)/shard_map/kgqs,skd->kgqd/dot_general | solution.py:77
  342.1 1.2 copy.61
  343.2 0.1 add_reduce_fusion
  343.3 0.1 select_reduce_fusion
  343.5 10.1 %all-to-all-done.2 = bf16[32,4,2,128,128]{4,3,2,1,0:T(8,128)(2,1)} async-done(((bf16[32,4,2,128,128]{4,3,2,1,0:T(8,128)(2,1)}), bf16[32,4,2,128,128]{4,3,2,1,0:T(8,128)(2,1)}, u32[]{:S(2)}, u32[]{:S(2)}) %all-to-all-start.2) | async-done | bytes 8388640 | tf_op jit(solution)/shard_map/all_to_all | solution.py:122
  353.6 6.5 %gather_fusion.1 = bf16[16,4,2,128,128]{4,3,2,1,0:T(8,128)(2,1)} fusion(bf16[32,4,2,128,128]{4,3,2,1,0:T(8,128)(2,1)} %all-to-all-done.2, s32[1024]{0:T(1024)S(1)} %pad_clamp_fusion), kind=kCustom, calls=%fused_computation.1 | custom fusion | bytes 8388672 | tf_op jit(solution)/shard_map/jit(_take)/gather | solution.py:129
  (46 shorter events, 0.2 us)
Async XLA Ops:
  7.2 192.3 %all-gather.3.cloned.1.call-start = ((), (), s32[]{:S(2)}) async-start(), calls=%async_computation.3 | async-start | bytes 24510464 | tf_op jit(solution)/shard_map/all_gather | solution.py:169
  25.8 6.2 %copy-start.4 = (bf16[8192]{0:T(1024)(128)(2,1)S(1)}, bf16[8192]{0:T(1024)(128)(2,1)}, u32[]{:S(2)}) copy-start(bf16[8192]{0:T(1024)(128)(2,1)} %param.17) | copy-start | bytes 49156
  25.8 6.2 %copy-start.10 = (bf16[128]{0:T(256)(128)(2,1)S(1)}, bf16[128]{0:T(256)(128)(2,1)}, u32[]{:S(2)}) copy-start(bf16[128]{0:T(256)(128)(2,1)} %param.22) | copy-start | bytes 772
  25.8 6.2 %copy-start.11 = (bf16[128]{0:T(256)(128)(2,1)S(1)}, bf16[128]{0:T(256)(128)(2,1)}, u32[]{:S(2)}) copy-start(bf16[128]{0:T(256)(128)(2,1)} %param.23) | copy-start | bytes 772
  25.8 6.2 %copy-start.8 = (s32[16,1]{0,1:T(1,128)S(1)}, s32[16,1]{0,1:T(1,128)}, u32[]{:S(2)}) copy-start(s32[16,1]{0,1:T(1,128)} %param.31) | copy-start | bytes 196
  25.8 95.3 %all-to-all-start = ((bf16[8,384,1024]{2,1,0:T(8,128)(2,1)}), bf16[8,384,1024]{2,1,0:T(8,128)(2,1)}, u32[]{:S(2)}, u32[]{:S(2)}) async-start(bf16[8,384,1024]{2,1,0:T(8,128)(2,1)} %broadcast_in_dim.181), calls=%async_computation | async-start | bytes 12582912 | tf_op jit(solution)/shard_map/all_to_all | solution.py:160
  31.9 222.6 %all-gather.5.cloned.1.call-start = ((), (), s32[]{:S(2)}) async-start(), calls=%async_computation.4 | async-start | bytes 3342336 | tf_op jit(solution)/shard_map/all_gather | solution.py:202
  32.1 7.3 %copy-start.12 = (s32[3]{0:T(128)S(1)}, s32[3]{0:T(128)}, u32[]{:S(2)}) copy-start(s32[3]{0:T(128)} %param.24) | copy-start | bytes 40
  32.1 7.5 %copy-start.9 = (s32[3]{0:T(128)S(1)}, s32[3]{0:T(128)}, u32[]{:S(2)}) copy-start(s32[3]{0:T(128)} %param.25) | copy-start | bytes 40
  32.1 7.6 %copy-start.6 = (s32[4]{0:T(128)S(1)}, s32[4]{0:T(128)}, u32[]{:S(2)}) copy-start(s32[4]{0:T(128)} %param.26) | copy-start | bytes 52
  199.5 18.8 %copy-start.7 = (bf16[1024]{0:T(1024)(128)(2,1)S(1)}, bf16[1024]{0:T(1024)(128)(2,1)}, u32[]{:S(2)}) copy-start(bf16[1024]{0:T(1024)(128)(2,1)} %param.21) | copy-start | bytes 6148
  199.5 18.8 %copy-start.5 = (s32[4,4]{1,0:T(4,128)S(1)}, s32[4,4]{1,0:T(4,128)}, u32[]{:S(2)}) copy-start(s32[4,4]{1,0:T(4,128)} %param.27) | copy-start | bytes 196
  217.0 1.8 copy-start.3
  237.8 3.1 copy-start.1
  237.8 3.1 copy-start.2
  237.8 4.7 %copy-start = (pred[384,2048]{1,0:T(8,128)(4,1)S(1)}, pred[384,2048]{1,0:T(8,128)(4,1)}, u32[]{:S(2)}) copy-start(pred[384,2048]{1,0:T(8,128)(4,1)} %and_reduce_fusion) | copy-start | bytes 2359300
  254.6 99.0 %all-to-all-start.2 = ((bf16[32,4,2,128,128]{4,3,2,1,0:T(8,128)(2,1)}), bf16[32,4,2,128,128]{4,3,2,1,0:T(8,128)(2,1)}, u32[]{:S(2)}, u32[]{:S(2)}) async-start(bf16[32,4,2,128,128]{4,3,2,1,0:T(8,128)(2,1)} %gather_fusion), calls=%async_computation.2 | async-start | bytes 16777216 | tf_op jit(solution)/shard_map/all_to_all | solution.py:122
Sparse Core Ops, SparseCore 0:
  10.8 188.5 all-gather.2
  218.4 36.0 all-gather.4

commit v10 on v9

--- a/solution.py
+++ b/solution.py
@@ -160,7 +160,21 @@
     pieces = lax.all_to_all(spread, "mp", split_axis=0, concat_axis=0, tiled=True)
     packed, slot_flags = pack_cache(prev_cache, dest_device)
     arrived_flags = swap_flags(slot_flags)
-    pieces, packed, arrived_flags = lax.optimization_barrier((pieces, packed, arrived_flags))
+    all_blocks = pool_keys.shape[0] * lax.axis_size("dz") * lax.axis_size("dc")
+    allowed_group = prompt_mask(prompt_table, prompt_lens, all_blocks, pool_keys.shape[1])
+    allowed = jnp.any(group_hot[:, :, None] & allowed_group[None, :, :], axis=1)
+    key_count = row_count * lax.axis_size("dz") * lax.axis_size("dc")
+    window = min(key_count, MAX_REQUEST + row_count)
+    window = -(-window // row_count) * row_count
+    window_start = jnp.maximum((me + 1) * row_count - window, 0)
+    key_rows = window_start + jnp.arange(window, dtype=jnp.int32)
+    key_request = request_index(key_rows, ends_at)
+    span_allowed = (request_of[:, None] == key_request[None, :]) & (
+        key_rows[None, :] <= global_rows[:, None]
+    )
+    pieces, packed, arrived_flags, allowed, span_allowed = lax.optimization_barrier(
+        (pieces, packed, arrived_flags, allowed, span_allowed)
+    )
     q_cols = query_weight.shape[1]
     k_cols = key_weight.shape[1]
     block_rows = query_weight.shape[0]
@@ -211,21 +225,11 @@
     block_size = pool_all.shape[1]
     blocks_here = pool_all.shape[0]
     kv_width = local_kv * HD
-    allowed_group = prompt_mask(prompt_table, prompt_lens, blocks_here, block_size)
-    allowed = jnp.any(group_hot[:, :, None] & allowed_group[None, :, :], axis=1)
     keys_flat = pool_all[:, :, :kv_width].reshape(blocks_here * block_size, local_kv, HD)
     values_flat = pool_all[:, :, kv_width:].reshape(blocks_here * block_size, local_kv, HD)
     carried = attend(carried, queries, keys_flat, values_flat, allowed, score_scale)
     key_count = span_all.shape[0]
-    window = min(key_count, MAX_REQUEST + row_count)
-    window = -(-window // row_count) * row_count
-    window_start = jnp.maximum((me + 1) * row_count - window, 0)
     span_window = lax.dynamic_slice_in_dim(span_all, window_start, window, axis=0)
-    key_rows = window_start + jnp.arange(window, dtype=jnp.int32)
-    key_request = request_index(key_rows, ends_at)
-    span_allowed = (request_of[:, None] == key_request[None, :]) & (
-        key_rows[None, :] <= global_rows[:, None]
-    )
     span_keys_flat = span_window[:, :kv_width].reshape(window, local_kv, HD)
     span_values_flat = span_window[:, kv_width:].reshape(window, local_kv, HD)
     carried = attend(

time: 373 us -> 375 us (level)
    all_to_all x1, waiting for transfers between devices: 80.7 us -> 76.2 us  [per_device(): lax.all_to_all(spread, 'mp', split_axis=0, concat_axis=0, tiled=True)]
  transfers between devices with their start and end apart: 4 -> 4, of which waited for: 4 -> 4; matrix products, arithmetic and copies ran while one was open for 37% -> 38% of each run, Pallas kernels for 0% -> 0%
where the time goes in v10:
time: 375 us; the launch traced here: 368 us
  waiting for transfers between devices  163 us (43%)
  matrix products  75.7 us (20%)
  other arithmetic  55.7 us (15%)
  local copies, waits for them, and re-layouts  37.7 us (10%)
  between operations  14.4 us (4%)
  starting transfers between devices  13.1 us (3%)
  blocking collectives  8.43 us (2%)
    all_to_all x1, waiting for transfers between devices, per_device(): lax.all_to_all(spread, 'mp', split_axis=0, concat_axis=0, tiled=True)  76.2 us
    all_gather x1, waiting for transfers between devices, per_device(): weights_all = lax.all_gather(weights_here, ('dz', 'dc'), axis=0, tiled=True)  74 us
    reduce_sum x2, other arithmetic, attend(): total_sum = total_sum * factor + jnp.sum(weights, axis=-1)  33.1 us
    dot_general x2, matrix products, attend(): jnp.einsum('kgqs,skd->kgqd', weights.astype(jnp.bfloat16), values_flat, p...  29.6 us
    dot_general x2, matrix products, attend(): jnp.einsum('kgqd,skd->kgqs', queries, keys_flat, preferred_element_type=j...  28.5 us
    dot_general x1, matrix products, per_device(): jnp.einsum('jtf,jfc->tc', normed, weights_all.reshape(mp_size, -1, weight...  17.6 us
    all_to_all x1, waiting for transfers between devices, unpack_cache(): lax.all_to_all(packed, ('dz', 'dc'), split_axis=0, concat_axis=0, tiled=T...  10.1 us
    all_to_all x1, blocking collectives, swap_flags(): lax.all_to_all(slot_flags, ('dz', 'dc'), split_axis=0, concat_axis=0, til...  8.43 us
  transfers between devices with their start and end apart: 4, of which 4 were waited for; matrix products, arithmetic and copies ran while one was open for 38% of the time, Pallas kernels for 0%

profile of v10, /device:TPU:104, one launch (start us, length us, event | category | flops | bytes accessed | tf_op | source)
XLA Modules:
  0.0 368.5 jit_solution(13578361003733114710)
XLA Ops:
  7.2 0.0 all-gather.3.cloned.1.call-start
  7.2 0.8 pad_maximum_fusion.4
  8.0 0.1 reshape.399
  8.1 2.6 pad_maximum_fusion
  10.7 0.0 all-gather.3.cloned.1.call-update
  10.7 0.9 convert_reduce_fusion.1
  11.7 0.7 fusion.38
  12.4 0.1 reshape.435
  12.5 8.4 %all_to_all.19 = bf16[16,2,1]{1,2,0:T(2,128)(2,1)S(1)} all-to-all(bf16[16,2,1]{1,2,0:T(2,128)(2,1)S(1)} %reshape.435), channel_id=1, replica_groups=mesh['dz'=8,'dc'=2,'mp'=8] {'dz','dc'}, dimensions={0} | all-to-all | bytes 128 | tf_op jit(solution)/shard_map/all_to_all | solution.py:116
  20.9 4.8 %broadcast_in_dim.117 = bf16[8,384,1024]{2,1,0:T(8,128)(2,1)} broadcast(bf16[384,1024]{1,0:T(8,128)(2,1)} %param.16), dimensions={1,2} | broadcast | bytes 7077888 | tf_op jit(solution)/shard_map/broadcast_in_dim | solution.py:159
  25.8 0.0 copy-start.8
  25.8 6.1 %all-to-all-start = ((bf16[8,384,1024]{2,1,0:T(8,128)(2,1)}), bf16[8,384,1024]{2,1,0:T(8,128)(2,1)}, u32[]{:S(2)}, u32[]{:S(2)}) async-start(bf16[8,384,1024]{2,1,0:T(8,128)(2,1)} %broadcast_in_dim.117), calls=%async_computation | async-start | bytes 12582912 | tf_op jit(solution)/shard_map/all_to_all | solution.py:160
  31.9 0.0 all-gather.5.cloned.1.call-start
  32.0 0.2 reduce-window.16
  32.2 0.1 select_reduce_fusion.2
  32.3 7.2 %gather_fusion = bf16[32,4,2,128,128]{4,3,2,1,0:T(8,128)(2,1)} fusion(bf16[16,4,2,128,128]{4,3,2,1,0:T(8,128)(2,1)} %param.30, s32[1024]{0:T(1024)S(1)} %pad_clamp_fusion.1), kind=kCustom, calls=%fused_computation | custom fusion | bytes 16777344 | tf_op jit(solution)/shard_map/jit(_take)/gather | solution.py:110
  39.6 0.1 select_reduce_fusion.1
  39.7 0.1 fusion.35
  39.8 0.1 convert_reduce_fusion.2
  39.9 0.1 convert_reduce_fusion
  40.0 0.1 select_reduce_fusion.3
  40.1 0.1 select_reduce_fusion.4
  40.2 0.1 broadcast_bitcast_fusion.1
  40.3 0.1 broadcast_bitcast_fusion
  40.4 1.1 multiply_cosine_fusion
  41.4 0.1 fusion.34
  41.5 2.1 and_reduce_fusion
  43.6 1.2 compare_and_fusion
  44.8 0.1 all_to_all.14
  44.9 76.2 %all-to-all-done = bf16[8,384,1024]{2,1,0:T(8,128)(2,1)} async-done(((bf16[8,384,1024]{2,1,0:T(8,128)(2,1)}), bf16[8,384,1024]{2,1,0:T(8,128)(2,1)}, u32[]{:S(2)}, u32[]{:S(2)}) %all-to-all-start) | async-done | bytes 6291488 | tf_op jit(solution)/shard_map/all_to_all | solution.py:160
  121.1 4.3 %fusion.9 = f32[384]{0:T(512)S(1)} fusion(bf16[8,384,1024]{2,1,0:T(8,128)(2,1)} %all-to-all-done), kind=kLoop, calls=%fused_computation.16 | loop fusion | flops 9436800 | bytes 6292992 | tf_op jit(solution)/shard_map/reduce_sum | solution.py:190
  125.5 74.0 %all-gather.3.cloned.1.call-done = bf16[8192,1344]{1,0:T(8,128)(2,1)} async-done(((bf16[512,1344]{1,0:T(8,128)(2,1)}), bf16[8192,1344]{1,0:T(8,128)(2,1)}) %all-gather.3.cloned.1.call-update) | async-done | bytes 22020112 | tf_op jit(solution)/shard_map/all_gather | solution.py:183
  199.5 17.6 %fusion.19 = f32[384,1344]{0,1:T(8,128)S(1)} fusion(bf16[8,1024,1344]{2,1,0:T(8,128)(2,1)} %bitcast.69, bf16[8,384,1024]{2,1,0:T(8,128)(2,1)} %all-to-all-done, f32[8,1024]{1,0:T(8,128)S(1)} %reshape.410, f32[384]{0:T(512)S(1)} %add_rsqrt_fusion), kind=kOutput, calls=%fused_computation.26 | convolution fusion | flops 8468299776 | bytes 30410240 | tf_op jit(solution)/shard_map/jtf,jfc->tc/dot_general | solution.py:195
  217.0 0.1 fusion.31
  217.2 1.9 fusion.30
  219.1 0.7 pad_maximum_fusion.3
  219.8 0.0 all-gather.5.cloned.1.call-update
  219.9 1.7 copy.53
  221.6 1.7 copy.57
  223.4 1.6 slice_add_fusion
  225.0 1.3 fusion.47
  226.3 2.8 copy.67
  229.0 2.7 copy.68
  231.8 1.6 copy.54
  233.4 1.8 slice.55
  235.2 2.2 reshape.404
  237.4 1.5 fusion.48
  238.9 1.7 negate_bitcast_fusion
  240.6 1.5 fusion.27
  242.1 10.7 %fusion.3 = (f32[8,384]{1,0:T(8,128)S(1)}, f32[8,384,2048]{2,1,0:T(8,128)}) fusion(pred[384,2048]{1,0:T(8,128)(4,1)S(1)} %copy-done, bf16[8,384,128]{2,1,0:T(8,128)(2,1)S(1)} %fusion.27, bf16[2048,128,1]{1,0,2:T(8,128)(2,1)S(1)} %bitcast.66), kind=kOutput, calls=%fused_computation.9 | convolution fusion | flops 1629484032 | bytes 27275264 | tf_op jit(solution)/shard_map/kgqd,skd->kgqs/dot_general | solution.py:68
  252.9 3.1 all-gather.5.cloned.1.call-done
  256.0 0.1 copy.60
  256.1 0.1 reduce-window.17
  256.2 6.9 %all-to-all-start.2 = ((bf16[32,4,2,128,128]{4,3,2,1,0:T(8,128)(2,1)}), bf16[32,4,2,128,128]{4,3,2,1,0:T(8,128)(2,1)}, u32[]{:S(2)}, u32[]{:S(2)}) async-start(bf16[32,4,2,128,128]{4,3,2,1,0:T(8,128)(2,1)} %gather_fusion), calls=%async_computation.2 | async-start | bytes 16777216 | tf_op jit(solution)/shard_map/all_to_all | solution.py:122
  263.1 17.8 %fusion = (f32[8,384]{1,0:T(8,128)S(1)}, f32[8,384,3456]{2,1,0:T(8,128)}) fusion(pred[384,3456]{1,0:T(8,128)(4,1)S(1)} %compare_and_fusion, bf16[8,384,128]{2,1,0:T(8,128)(2,1)S(1)} %fusion.27, bf16[6144,256]{0,1:T(8,128)(2,1)} %all-gather.5.cloned.1.call-done, s32[]{:T(128)S(6)} %max.20), kind=kOutput, calls=%fused_computation.4 | convolution fusion | flops 2749756416 | bytes 45477892 | tf_op jit(solution)/shard_map/kgqd,skd->kgqs/dot_general | solution.py:68
  280.9 21.1 %fusion.1 = f32[8,384]{1,0:T(8,128)S(1)} fusion(f32[8,384,3456]{2,1,0:T(8,128)} %get-tuple-element.52, f32[8,384]{1,0:T(8,128)S(1)} %get-tuple-element.43, pred[384,3456]{1,0:T(8,128)(4,1)S(1)} %compare_and_fusion), kind=kLoop, calls=%fused_computation.5 | loop fusion | flops 53081088 | bytes 43819008 | tf_op jit(solution)/shard_map/reduce_sum | solution.py:76
  302.0 12.0 %fusion.7 = f32[8,384]{1,0:T(8,128)S(1)} fusion(f32[8,384,2048]{2,1,0:T(8,128)} %get-tuple-element.50, f32[8,384]{1,0:T(8,128)S(1)} %get-tuple-element.44, pred[384,2048]{1,0:T(8,128)(4,1)S(1)} %copy-done), kind=kLoop, calls=%fused_computation.12 | loop fusion | flops 31454208 | bytes 25976832 | tf_op jit(solution)/shard_map/reduce_sum | solution.py:76
  314.0 11.2 %fusion.12 = f32[8,384,128]{1,2,0:T(8,128)S(1)} fusion(bf16[2048,128,1]{1,0,2:T(8,128)(2,1)S(1)} %bitcast.68, f32[8,384,2048]{2,1,0:T(8,128)} %get-tuple-element.50, f32[8,384]{1,0:T(8,128)S(1)} %get-tuple-element.44, pred[384,2048]{1,0:T(8,128)(4,1)S(1)} %copy-done), kind=kOutput, calls=%fused_computation.19 | convolution fusion | flops 1642070016 | bytes 28061696 | tf_op jit(solution)/shard_map/kgqs,skd->kgqd/dot_general | solution.py:77
  325.2 18.4 %divide_convert_fusion = bf16[8,384,128]{1,2,0:T(8,128)(2,1)S(1)} fusion(f32[8,384,128]{1,2,0:T(8,128)S(1)} %fusion.12, f32[8,384,3456]{2,1,0:T(8,128)} %get-tuple-element.52, f32[8,384]{1,0:T(8,128)S(1)} %get-tuple-element.43, pred[384,3456]{1,0:T(8,128)(4,1)S(1)} %compare_and_fusion, bf16[6144,256]{0,1:T(8,128)(2,1)} %all-gather.5.cloned.1.call-done, ...), kind=kOutput, calls=%fused_computation.31 | convolution fusion | flops 2772959232 | bytes 47087624 | tf_op jit(solution)/shard_map/kgqs,skd->kgqd/dot_general | solution.py:77
  343.6 1.2 copy.61
  344.8 0.1 add_reduce_fusion
  344.9 0.1 select_reduce_fusion
  345.0 10.1 %all-to-all-done.2 = bf16[32,4,2,128,128]{4,3,2,1,0:T(8,128)(2,1)} async-done(((bf16[32,4,2,128,128]{4,3,2,1,0:T(8,128)(2,1)}), bf16[32,4,2,128,128]{4,3,2,1,0:T(8,128)(2,1)}, u32[]{:S(2)}, u32[]{:S(2)}) %all-to-all-start.2) | async-done | bytes 8388640 | tf_op jit(solution)/shard_map/all_to_all | solution.py:122
  355.2 6.5 %gather_fusion.1 = bf16[16,4,2,128,128]{4,3,2,1,0:T(8,128)(2,1)} fusion(bf16[32,4,2,128,128]{4,3,2,1,0:T(8,128)(2,1)} %all-to-all-done.2, s32[1024]{0:T(1024)S(1)} %pad_clamp_fusion), kind=kCustom, calls=%fused_computation.1 | custom fusion | bytes 8388672 | tf_op jit(solution)/shard_map/jit(_take)/gather | solution.py:129
  (46 shorter events, 0.2 us)
Async XLA Ops:
  7.2 192.3 %all-gather.3.cloned.1.call-start = ((), (), s32[]{:S(2)}) async-start(), calls=%async_computation.3 | async-start | bytes 24510464 | tf_op jit(solution)/shard_map/all_gather | solution.py:183
  25.8 6.2 %copy-start.12 = (s32[3]{0:T(128)S(1)}, s32[3]{0:T(128)}, u32[]{:S(2)}) copy-start(s32[3]{0:T(128)} %param.24) | copy-start | bytes 40
  25.8 6.4 %copy-start.4 = (bf16[8192]{0:T(1024)(128)(2,1)S(1)}, bf16[8192]{0:T(1024)(128)(2,1)}, u32[]{:S(2)}) copy-start(bf16[8192]{0:T(1024)(128)(2,1)} %param.17) | copy-start | bytes 49156
  25.8 6.4 %copy-start.10 = (bf16[128]{0:T(256)(128)(2,1)S(1)}, bf16[128]{0:T(256)(128)(2,1)}, u32[]{:S(2)}) copy-start(bf16[128]{0:T(256)(128)(2,1)} %param.22) | copy-start | bytes 772
  25.8 6.4 %copy-start.11 = (bf16[128]{0:T(256)(128)(2,1)S(1)}, bf16[128]{0:T(256)(128)(2,1)}, u32[]{:S(2)}) copy-start(bf16[128]{0:T(256)(128)(2,1)} %param.23) | copy-start | bytes 772
  25.8 6.4 %copy-start.8 = (s32[16,1]{0,1:T(1,128)S(1)}, s32[16,1]{0,1:T(1,128)}, u32[]{:S(2)}) copy-start(s32[16,1]{0,1:T(1,128)} %param.31) | copy-start | bytes 196
  25.8 95.3 %all-to-all-start = ((bf16[8,384,1024]{2,1,0:T(8,128)(2,1)}), bf16[8,384,1024]{2,1,0:T(8,128)(2,1)}, u32[]{:S(2)}, u32[]{:S(2)}) async-start(bf16[8,384,1024]{2,1,0:T(8,128)(2,1)} %broadcast_in_dim.117), calls=%async_computation | async-start | bytes 12582912 | tf_op jit(solution)/shard_map/all_to_all | solution.py:160
  31.9 224.1 %all-gather.5.cloned.1.call-start = ((), (), s32[]{:S(2)}) async-start(), calls=%async_computation.4 | async-start | bytes 3342336 | tf_op jit(solution)/shard_map/all_gather | solution.py:216
  32.3 7.3 %copy-start.5 = (s32[4,4]{1,0:T(4,128)S(1)}, s32[4,4]{1,0:T(4,128)}, u32[]{:S(2)}) copy-start(s32[4,4]{1,0:T(4,128)} %param.27) | copy-start | bytes 196
  32.3 7.7 %copy-start.9 = (s32[3]{0:T(128)S(1)}, s32[3]{0:T(128)}, u32[]{:S(2)}) copy-start(s32[3]{0:T(128)} %param.25) | copy-start | bytes 40
  32.3 7.8 %copy-start.6 = (s32[4]{0:T(128)S(1)}, s32[4]{0:T(128)}, u32[]{:S(2)}) copy-start(s32[4]{0:T(128)} %param.26) | copy-start | bytes 52
  199.5 20.4 %copy-start.7 = (bf16[1024]{0:T(1024)(128)(2,1)S(1)}, bf16[1024]{0:T(1024)(128)(2,1)}, u32[]{:S(2)}) copy-start(bf16[1024]{0:T(1024)(128)(2,1)} %param.21) | copy-start | bytes 6148
  217.0 4.6 %copy-start.3 = (f32[384,1344]{0,1:T(8,128)}, f32[384,1344]{0,1:T(8,128)S(1)}, u32[]{:S(2)}) copy-start(f32[384,1344]{0,1:T(8,128)S(1)} %fusion.19) | copy-start | bytes 6193156
  237.4 3.1 copy-start.1
  237.4 3.2 copy-start.2
  237.4 4.7 %copy-start = (pred[384,2048]{1,0:T(8,128)(4,1)S(1)}, pred[384,2048]{1,0:T(8,128)(4,1)}, u32[]{:S(2)}) copy-start(pred[384,2048]{1,0:T(8,128)(4,1)} %and_reduce_fusion) | copy-start | bytes 2359300
  256.2 99.0 %all-to-all-start.2 = ((bf16[32,4,2,128,128]{4,3,2,1,0:T(8,128)(2,1)}), bf16[32,4,2,128,128]{4,3,2,1,0:T(8,128)(2,1)}, u32[]{:S(2)}, u32[]{:S(2)}) async-start(bf16[32,4,2,128,128]{4,3,2,1,0:T(8,128)(2,1)} %gather_fusion), calls=%async_computation.2 | async-start | bytes 16777216 | tf_op jit(solution)/shard_map/all_to_all | solution.py:122
Sparse Core Ops, SparseCore 0:
  10.8 188.5 all-gather.2
  220.0 35.9 all-gather.4

commit v11 on v9

--- a/solution.py
+++ b/solution.py
@@ -178,6 +178,7 @@
     )
     gain = norm_gain.astype(jnp.float32).reshape(mp_size, 1, -1)
     normed = (as_float * inverse * gain).astype(jnp.bfloat16)
+    normed = lax.optimization_barrier(normed)
     proj = jnp.einsum(
         "jtf,jfc->tc",
         normed,

time: 373 us -> 373 us (level)
  waiting for transfers between devices: 166 us -> 158 us
  other arithmetic: 53.4 us -> 61.3 us
    all_gather x1, waiting for transfers between devices: 74 us -> 66.1 us  [per_device(): weights_all = lax.all_gather(weights_here, ('dz', 'dc'), axis=0, tiled=True)]
    convert_element_type x0 -> x1, other arithmetic: none -> 7.87 us  [per_device(): normed = (as_float * inverse * gain).astype(jnp.bfloat16)]
  transfers between devices with their start and end apart: 4 -> 4, of which waited for: 4 -> 4; matrix products, arithmetic and copies ran while one was open for 37% -> 39% of each run, Pallas kernels for 0% -> 0%
where the time goes in v11:
time: 373 us; the launch traced here: 367 us
  waiting for transfers between devices  158 us (42%)
  matrix products  75.5 us (20%)
  other arithmetic  61.3 us (16%)
  local copies, waits for them, and re-layouts  35.8 us (10%)
  between operations  14.4 us (4%)
  starting transfers between devices  13.1 us (4%)
  blocking collectives  8.43 us (2%)
    all_to_all x1, waiting for transfers between devices, per_device(): lax.all_to_all(spread, 'mp', split_axis=0, concat_axis=0, tiled=True)  80.7 us
    all_gather x1, waiting for transfers between devices, per_device(): weights_all = lax.all_gather(weights_here, ('dz', 'dc'), axis=0, tiled=True)  66.1 us
    reduce_sum x2, other arithmetic, attend(): total_sum = total_sum * factor + jnp.sum(weights, axis=-1)  33.1 us
    dot_general x2, matrix products, attend(): jnp.einsum('kgqs,skd->kgqd', weights.astype(jnp.bfloat16), values_flat, p...  29.6 us
    dot_general x2, matrix products, attend(): jnp.einsum('kgqd,skd->kgqs', queries, keys_flat, preferred_element_type=j...  28.4 us
    dot_general x1, matrix products, per_device(): jnp.einsum('jtf,jfc->tc', normed, weights_all.reshape(mp_size, -1, weight...  17.5 us
    all_to_all x1, waiting for transfers between devices, unpack_cache(): lax.all_to_all(packed, ('dz', 'dc'), split_axis=0, concat_axis=0, tiled=T...  10.1 us
    all_to_all x1, blocking collectives, swap_flags(): lax.all_to_all(slot_flags, ('dz', 'dc'), split_axis=0, concat_axis=0, til...  8.43 us
  transfers between devices with their start and end apart: 4, of which 4 were waited for; matrix products, arithmetic and copies ran while one was open for 39% of the time, Pallas kernels for 0%

profile of v11, /device:TPU:104, one launch (start us, length us, event | category | flops | bytes accessed | tf_op | source)
XLA Modules:
  0.0 366.8 jit_solution(14144497910533483981)
XLA Ops:
  7.2 0.0 all-gather.3.cloned.1.call-start
  7.2 0.8 pad_maximum_fusion.4
  8.0 0.1 reshape.450
  8.1 2.6 pad_maximum_fusion
  10.7 0.0 all-gather.3.cloned.1.call-update
  10.7 0.9 convert_reduce_fusion.1
  11.7 0.7 fusion.31
  12.4 0.1 reshape.486
  12.5 8.4 %all_to_all.19 = bf16[16,2,1]{1,2,0:T(2,128)(2,1)S(1)} all-to-all(bf16[16,2,1]{1,2,0:T(2,128)(2,1)S(1)} %reshape.486), channel_id=1, replica_groups=mesh['dz'=8,'dc'=2,'mp'=8] {'dz','dc'}, dimensions={0} | all-to-all | bytes 128 | tf_op jit(solution)/shard_map/all_to_all | solution.py:116
  20.9 4.8 %broadcast_in_dim.181 = bf16[8,384,1024]{2,1,0:T(8,128)(2,1)} broadcast(bf16[384,1024]{1,0:T(8,128)(2,1)} %param.16), dimensions={1,2} | broadcast | bytes 7077888 | tf_op jit(solution)/shard_map/broadcast_in_dim | solution.py:159
  25.8 6.1 %all-to-all-start = ((bf16[8,384,1024]{2,1,0:T(8,128)(2,1)}), bf16[8,384,1024]{2,1,0:T(8,128)(2,1)}, u32[]{:S(2)}, u32[]{:S(2)}) async-start(bf16[8,384,1024]{2,1,0:T(8,128)(2,1)} %broadcast_in_dim.181), calls=%async_computation | async-start | bytes 12582912 | tf_op jit(solution)/shard_map/all_to_all | solution.py:160
  31.9 0.0 all-gather.5.cloned.1.call-start
  32.0 0.1 select_reduce_fusion.1
  32.1 7.2 %gather_fusion = bf16[32,4,2,128,128]{4,3,2,1,0:T(8,128)(2,1)} fusion(bf16[16,4,2,128,128]{4,3,2,1,0:T(8,128)(2,1)} %param.30, s32[1024]{0:T(1024)S(1)} %pad_clamp_fusion.1), kind=kCustom, calls=%fused_computation | custom fusion | bytes 16777344 | tf_op jit(solution)/shard_map/jit(_take)/gather | solution.py:110
  39.4 0.2 reduce-window.16
  39.6 0.1 convert_reduce_fusion.2
  39.7 0.1 select_reduce_fusion.5
  39.8 0.1 select_reduce_fusion.4
  39.8 0.4 multiply_cosine_fusion
  40.3 0.1 all_to_all.14
  40.4 80.7 %all-to-all-done = bf16[8,384,1024]{2,1,0:T(8,128)(2,1)} async-done(((bf16[8,384,1024]{2,1,0:T(8,128)(2,1)}), bf16[8,384,1024]{2,1,0:T(8,128)(2,1)}, u32[]{:S(2)}, u32[]{:S(2)}) %all-to-all-start) | async-done | bytes 6291488 | tf_op jit(solution)/shard_map/all_to_all | solution.py:160
  121.1 4.3 %fusion.9 = f32[384]{0:T(512)S(1)} fusion(bf16[8,384,1024]{2,1,0:T(8,128)(2,1)} %all-to-all-done), kind=kLoop, calls=%fused_computation.16 | loop fusion | flops 9436800 | bytes 6292992 | tf_op jit(solution)/shard_map/reduce_sum | solution.py:176
  125.5 7.9 %fusion.11 = bf16[8,384,1024]{2,1,0:T(8,128)(2,1)} fusion(bf16[8,384,1024]{2,1,0:T(8,128)(2,1)} %all-to-all-done, f32[8,1024]{1,0:T(8,128)S(1)} %reshape.461, f32[384]{0:T(512)S(1)} %add_rsqrt_fusion), kind=kLoop, calls=%fused_computation.18 | loop fusion | flops 12582912 | bytes 12617216 | tf_op jit(solution)/shard_map/convert_element_type | solution.py:180
  133.3 66.1 %all-gather.3.cloned.1.call-done = bf16[8192,1344]{1,0:T(8,128)(2,1)} async-done(((bf16[512,1344]{1,0:T(8,128)(2,1)}), bf16[8192,1344]{1,0:T(8,128)(2,1)}) %all-gather.3.cloned.1.call-update) | async-done | bytes 22020112 | tf_op jit(solution)/shard_map/all_gather | solution.py:169
  199.5 17.5 %convolution_bitcast_fusion = f32[384,1344]{0,1:T(8,128)S(1)} fusion(bf16[8,384,1024]{2,1,0:T(8,128)(2,1)} %fusion.11, bf16[8,1024,1344]{2,1,0:T(8,128)(2,1)} %bitcast.70), kind=kOutput, calls=%fused_computation.23 | convolution fusion | flops 8455716864 | bytes 30375936 | tf_op jit(solution)/shard_map/jtf,jfc->tc/dot_general | solution.py:182
  216.9 0.1 fusion.24
  217.1 0.1 fusion.23
  217.2 0.9 pad_maximum_fusion.3
  218.1 0.0 all-gather.5.cloned.1.call-update
  218.2 0.1 select_reduce_fusion.2
  218.3 0.1 fusion.28
  218.4 0.1 convert_reduce_fusion
  218.5 0.1 broadcast_bitcast_fusion.1
  218.6 0.1 broadcast_bitcast_fusion
  218.7 0.1 fusion.27
  218.8 2.1 and_reduce_fusion
  220.8 1.2 compare_and_fusion
  222.0 0.8 copy.53
  222.8 0.8 copy.57
  223.7 1.6 slice_add_fusion
  225.3 1.3 fusion.40
  226.6 2.8 copy.67
  229.3 2.7 copy.68
  232.1 1.6 copy.54
  233.7 1.7 slice.55
  235.5 2.2 reshape.455
  237.7 1.5 fusion.41
  239.1 1.6 negate_bitcast_fusion
  240.8 1.5 fusion.20
  242.3 10.7 %fusion.3 = (f32[8,384]{1,0:T(8,128)S(1)}, f32[8,384,2048]{2,1,0:T(8,128)}) fusion(pred[384,2048]{1,0:T(8,128)(4,1)S(1)} %copy-done, bf16[8,384,128]{2,1,0:T(8,128)(2,1)S(1)} %fusion.20, bf16[2048,128,1]{1,0,2:T(8,128)(2,1)S(1)} %bitcast.67), kind=kOutput, calls=%fused_computation.9 | convolution fusion | flops 1629484032 | bytes 27275264 | tf_op jit(solution)/shard_map/kgqd,skd->kgqs/dot_general | solution.py:68
  253.0 1.3 all-gather.5.cloned.1.call-done
  254.3 0.1 copy.60
  254.4 0.1 reduce-window.17
  254.5 6.9 %all-to-all-start.2 = ((bf16[32,4,2,128,128]{4,3,2,1,0:T(8,128)(2,1)}), bf16[32,4,2,128,128]{4,3,2,1,0:T(8,128)(2,1)}, u32[]{:S(2)}, u32[]{:S(2)}) async-start(bf16[32,4,2,128,128]{4,3,2,1,0:T(8,128)(2,1)} %gather_fusion), calls=%async_computation.2 | async-start | bytes 16777216 | tf_op jit(solution)/shard_map/all_to_all | solution.py:122
  261.4 17.8 %fusion = (f32[8,384]{1,0:T(8,128)S(1)}, f32[8,384,3456]{2,1,0:T(8,128)}) fusion(pred[384,3456]{1,0:T(8,128)(4,1)S(1)} %compare_and_fusion, bf16[8,384,128]{2,1,0:T(8,128)(2,1)S(1)} %fusion.20, bf16[6144,256]{0,1:T(8,128)(2,1)} %all-gather.5.cloned.1.call-done, s32[]{:T(128)S(6)} %max.20), kind=kOutput, calls=%fused_computation.4 | convolution fusion | flops 2749756416 | bytes 45477892 | tf_op jit(solution)/shard_map/kgqd,skd->kgqs/dot_general | solution.py:68
  279.2 21.1 %fusion.1 = f32[8,384]{1,0:T(8,128)S(1)} fusion(f32[8,384,3456]{2,1,0:T(8,128)} %get-tuple-element.48, f32[8,384]{1,0:T(8,128)S(1)} %get-tuple-element.39, pred[384,3456]{1,0:T(8,128)(4,1)S(1)} %compare_and_fusion), kind=kLoop, calls=%fused_computation.5 | loop fusion | flops 53081088 | bytes 43819008 | tf_op jit(solution)/shard_map/reduce_sum | solution.py:76
  300.3 12.0 %fusion.7 = f32[8,384]{1,0:T(8,128)S(1)} fusion(f32[8,384,2048]{2,1,0:T(8,128)} %get-tuple-element.46, f32[8,384]{1,0:T(8,128)S(1)} %get-tuple-element.40, pred[384,2048]{1,0:T(8,128)(4,1)S(1)} %copy-done), kind=kLoop, calls=%fused_computation.12 | loop fusion | flops 31454208 | bytes 25976832 | tf_op jit(solution)/shard_map/reduce_sum | solution.py:76
  312.3 11.2 %fusion.12 = f32[8,384,128]{1,2,0:T(8,128)S(1)} fusion(bf16[2048,128,1]{1,0,2:T(8,128)(2,1)S(1)} %bitcast.69, f32[8,384,2048]{2,1,0:T(8,128)} %get-tuple-element.46, f32[8,384]{1,0:T(8,128)S(1)} %get-tuple-element.40, pred[384,2048]{1,0:T(8,128)(4,1)S(1)} %copy-done), kind=kOutput, calls=%fused_computation.19 | convolution fusion | flops 1642070016 | bytes 28061696 | tf_op jit(solution)/shard_map/kgqs,skd->kgqd/dot_general | solution.py:77
  323.5 18.4 %divide_convert_fusion = bf16[8,384,128]{1,2,0:T(8,128)(2,1)S(1)} fusion(f32[8,384,128]{1,2,0:T(8,128)S(1)} %fusion.12, f32[8,384,3456]{2,1,0:T(8,128)} %get-tuple-element.48, f32[8,384]{1,0:T(8,128)S(1)} %get-tuple-element.39, pred[384,3456]{1,0:T(8,128)(4,1)S(1)} %compare_and_fusion, bf16[6144,256]{0,1:T(8,128)(2,1)} %all-gather.5.cloned.1.call-done, ...), kind=kOutput, calls=%fused_computation.28 | convolution fusion | flops 2772959232 | bytes 47087624 | tf_op jit(solution)/shard_map/kgqs,skd->kgqd/dot_general | solution.py:77
  341.9 1.2 copy.61
  343.1 0.1 add_reduce_fusion
  343.2 0.1 select_reduce_fusion
  343.4 10.1 %all-to-all-done.2 = bf16[32,4,2,128,128]{4,3,2,1,0:T(8,128)(2,1)} async-done(((bf16[32,4,2,128,128]{4,3,2,1,0:T(8,128)(2,1)}), bf16[32,4,2,128,128]{4,3,2,1,0:T(8,128)(2,1)}, u32[]{:S(2)}, u32[]{:S(2)}) %all-to-all-start.2) | async-done | bytes 8388640 | tf_op jit(solution)/shard_map/all_to_all | solution.py:122
  353.5 6.5 %gather_fusion.1 = bf16[16,4,2,128,128]{4,3,2,1,0:T(8,128)(2,1)} fusion(bf16[32,4,2,128,128]{4,3,2,1,0:T(8,128)(2,1)} %all-to-all-done.2, s32[1024]{0:T(1024)S(1)} %pad_clamp_fusion), kind=kCustom, calls=%fused_computation.1 | custom fusion | bytes 8388672 | tf_op jit(solution)/shard_map/jit(_take)/gather | solution.py:129
  (47 shorter events, 0.2 us)
Async XLA Ops:
  7.2 192.3 %all-gather.3.cloned.1.call-start = ((), (), s32[]{:S(2)}) async-start(), calls=%async_computation.3 | async-start | bytes 24510464 | tf_op jit(solution)/shard_map/all_gather | solution.py:169
  25.8 6.2 %copy-start.4 = (bf16[8192]{0:T(1024)(128)(2,1)S(1)}, bf16[8192]{0:T(1024)(128)(2,1)}, u32[]{:S(2)}) copy-start(bf16[8192]{0:T(1024)(128)(2,1)} %param.17) | copy-start | bytes 49156
  25.8 6.2 %copy-start.10 = (bf16[128]{0:T(256)(128)(2,1)S(1)}, bf16[128]{0:T(256)(128)(2,1)}, u32[]{:S(2)}) copy-start(bf16[128]{0:T(256)(128)(2,1)} %param.22) | copy-start | bytes 772
  25.8 6.2 %copy-start.11 = (bf16[128]{0:T(256)(128)(2,1)S(1)}, bf16[128]{0:T(256)(128)(2,1)}, u32[]{:S(2)}) copy-start(bf16[128]{0:T(256)(128)(2,1)} %param.23) | copy-start | bytes 772
  25.8 6.2 %copy-start.8 = (s32[16,1]{0,1:T(1,128)S(1)}, s32[16,1]{0,1:T(1,128)}, u32[]{:S(2)}) copy-start(s32[16,1]{0,1:T(1,128)} %param.31) | copy-start | bytes 196
  25.8 95.3 %all-to-all-start = ((bf16[8,384,1024]{2,1,0:T(8,128)(2,1)}), bf16[8,384,1024]{2,1,0:T(8,128)(2,1)}, u32[]{:S(2)}, u32[]{:S(2)}) async-start(bf16[8,384,1024]{2,1,0:T(8,128)(2,1)} %broadcast_in_dim.181), calls=%async_computation | async-start | bytes 12582912 | tf_op jit(solution)/shard_map/all_to_all | solution.py:160
  31.9 222.5 %all-gather.5.cloned.1.call-start = ((), (), s32[]{:S(2)}) async-start(), calls=%async_computation.4 | async-start | bytes 3342336 | tf_op jit(solution)/shard_map/all_gather | solution.py:203
  32.1 7.3 %copy-start.12 = (s32[3]{0:T(128)S(1)}, s32[3]{0:T(128)}, u32[]{:S(2)}) copy-start(s32[3]{0:T(128)} %param.24) | copy-start | bytes 40
  32.1 7.5 %copy-start.9 = (s32[3]{0:T(128)S(1)}, s32[3]{0:T(128)}, u32[]{:S(2)}) copy-start(s32[3]{0:T(128)} %param.25) | copy-start | bytes 40
  32.1 7.6 %copy-start.6 = (s32[4]{0:T(128)S(1)}, s32[4]{0:T(128)}, u32[]{:S(2)}) copy-start(s32[4]{0:T(128)} %param.26) | copy-start | bytes 52
  199.5 18.7 %copy-start.7 = (bf16[1024]{0:T(1024)(128)(2,1)S(1)}, bf16[1024]{0:T(1024)(128)(2,1)}, u32[]{:S(2)}) copy-start(bf16[1024]{0:T(1024)(128)(2,1)} %param.21) | copy-start | bytes 6148
  199.5 18.7 %copy-start.5 = (s32[4,4]{1,0:T(4,128)S(1)}, s32[4,4]{1,0:T(4,128)}, u32[]{:S(2)}) copy-start(s32[4,4]{1,0:T(4,128)} %param.27) | copy-start | bytes 196
  216.9 1.8 copy-start.3
  237.7 3.1 copy-start.1
  237.7 3.1 copy-start.2
  237.7 4.7 %copy-start = (pred[384,2048]{1,0:T(8,128)(4,1)S(1)}, pred[384,2048]{1,0:T(8,128)(4,1)}, u32[]{:S(2)}) copy-start(pred[384,2048]{1,0:T(8,128)(4,1)} %and_reduce_fusion) | copy-start | bytes 2359300
  254.5 99.0 %all-to-all-start.2 = ((bf16[32,4,2,128,128]{4,3,2,1,0:T(8,128)(2,1)}), bf16[32,4,2,128,128]{4,3,2,1,0:T(8,128)(2,1)}, u32[]{:S(2)}, u32[]{:S(2)}) async-start(bf16[32,4,2,128,128]{4,3,2,1,0:T(8,128)(2,1)} %gather_fusion), calls=%async_computation.2 | async-start | bytes 16777216 | tf_op jit(solution)/shard_map/all_to_all | solution.py:122
Sparse Core Ops, SparseCore 0:
  10.8 188.5 all-gather.2
  218.3 36.0 all-gather.4

commit v12 on v9

--- a/solution.py
+++ b/solution.py
@@ -178,12 +178,8 @@
     )
     gain = norm_gain.astype(jnp.float32).reshape(mp_size, 1, -1)
     normed = (as_float * inverse * gain).astype(jnp.bfloat16)
-    proj = jnp.einsum(
-        "jtf,jfc->tc",
-        normed,
-        weights_all.reshape(mp_size, -1, weights_all.shape[1]),
-        preferred_element_type=jnp.float32,
-    )
+    normed = lax.optimization_barrier(normed.transpose(1, 0, 2).reshape(row_count, -1))
+    proj = jnp.dot(normed, weights_all, preferred_element_type=jnp.float32)
     query_proj = proj[:, :q_cols] + query_bias.astype(jnp.float32)[None, :]
     key_proj = proj[:, q_cols:q_cols + k_cols] + key_bias.astype(jnp.float32)[None, :]
     value_proj = proj[:, q_cols + k_cols:proj_cols] + value_bias.astype(jnp.float32)[None, :]

time: 373 us -> 373 us (level)
  blocking collectives: 8.43 us -> 0 us
  other arithmetic: 53.4 us -> 60.8 us
  starting transfers between devices: 13.1 us -> 18.6 us
  waiting for transfers between devices: 166 us -> 161 us
    all_to_all x1 -> x0, blocking collectives: 8.43 us -> none  [swap_flags(): lax.all_to_all(slot_flags, ('dz', 'dc'), split_axis=0, concat_axis=0, til...]
    convert_element_type x0 -> x1, other arithmetic: none -> 7.35 us  [per_device(): normed = (as_float * inverse * gain).astype(jnp.bfloat16)]
    all_gather x1, waiting for transfers between devices: 74 us -> 67.5 us  [per_device(): weights_all = lax.all_gather(weights_here, ('dz', 'dc'), axis=0, tiled=True)]
    all_to_all x0 -> x1, starting transfers between devices: none -> 5.43 us  [swap_flags(): lax.all_to_all(slot_flags, ('dz', 'dc'), split_axis=0, concat_axis=0, til...]
    unnamed x31 -> x32, local copies, waits for them, and re-layouts: 6.89 us -> 8.37 us
  transfers between devices with their start and end apart: 4 -> 5, of which waited for: 4 -> 5; matrix products, arithmetic and copies ran while one was open for 37% -> 39% of each run, Pallas kernels for 0% -> 0%
where the time goes in v12:
time: 373 us; the launch traced here: 367 us
  waiting for transfers between devices  161 us (43%)
  matrix products  75.4 us (20%)
  other arithmetic  60.8 us (16%)
  local copies, waits for them, and re-layouts  36.3 us (10%)
  starting transfers between devices  18.6 us (5%)
  between operations  14.4 us (4%)
    all_to_all x1, waiting for transfers between devices, per_device(): lax.all_to_all(spread, 'mp', split_axis=0, concat_axis=0, tiled=True)  80.6 us
    all_gather x1, waiting for transfers between devices, per_device(): weights_all = lax.all_gather(weights_here, ('dz', 'dc'), axis=0, tiled=True)  67.5 us
    reduce_sum x2, other arithmetic, attend(): total_sum = total_sum * factor + jnp.sum(weights, axis=-1)  33.1 us
    dot_general x2, matrix products, attend(): jnp.einsum('kgqs,skd->kgqd', weights.astype(jnp.bfloat16), values_flat, p...  29.6 us
    dot_general x2, matrix products, attend(): jnp.einsum('kgqd,skd->kgqs', queries, keys_flat, preferred_element_type=j...  28.4 us
    dot_general x1, matrix products, per_device(): proj = jnp.dot(normed, weights_all, preferred_element_type=jnp.float32)  17.4 us
    all_to_all x1, waiting for transfers between devices, unpack_cache(): lax.all_to_all(packed, ('dz', 'dc'), split_axis=0, concat_axis=0, tiled=T...  10.1 us
    unnamed x32, local copies, waits for them, and re-layouts  8.37 us
  transfers between devices with their start and end apart: 5, of which 5 were waited for; matrix products, arithmetic and copies ran while one was open for 39% of the time, Pallas kernels for 0%

profile of v12, /device:TPU:104, one launch (start us, length us, event | category | flops | bytes accessed | tf_op | source)
XLA Modules:
  0.0 366.7 jit_solution(15978928400612425594)
XLA Ops:
  7.2 0.0 all-gather.3.cloned.1.call-start
  7.2 0.8 pad_maximum_fusion.4
  8.0 0.1 reshape.451
  8.1 2.6 pad_maximum_fusion
  10.7 0.9 convert_reduce_fusion.1
  11.7 0.7 fusion.31
  12.4 0.7 reshape.485
  13.1 5.4 %all-to-all-start.1 = ((bf16[16,2,1]{1,2,0:T(2,128)(2,1)}), bf16[16,2,1]{1,2,0:T(2,128)(2,1)S(1)}, u32[]{:S(2)}, u32[]{:S(2)}) async-start(bf16[16,2,1]{1,2,0:T(2,128)(2,1)} %reshape.485), calls=%async_computation.1 | async-start | bytes 16384 | tf_op jit(solution)/shard_map/all_to_all | solution.py:116
  18.5 1.5 copy.48
  20.0 1.6 all-to-all-done.1
  21.7 3.2 broadcast_in_dim.181
  24.9 6.2 %all-to-all-start = ((bf16[8,384,1024]{1,2,0:T(8,128)(2,1)}), bf16[8,384,1024]{1,2,0:T(8,128)(2,1)}, u32[]{:S(2)}, u32[]{:S(2)}) async-start(bf16[8,384,1024]{1,2,0:T(8,128)(2,1)} %broadcast_in_dim.181), calls=%async_computation | async-start | bytes 12582912 | tf_op jit(solution)/shard_map/all_to_all | solution.py:160
  31.0 0.0 all-gather.5.cloned.1.call-start
  31.2 0.1 select_reduce_fusion.1
  31.3 7.3 %gather_fusion = bf16[32,4,2,128,128]{4,3,2,1,0:T(8,128)(2,1)} fusion(bf16[16,4,2,128,128]{4,3,2,1,0:T(8,128)(2,1)} %param.30, s32[1024]{0:T(1024)S(1)} %pad_clamp_fusion.1), kind=kCustom, calls=%fused_computation | custom fusion | bytes 16777344 | tf_op jit(solution)/shard_map/jit(_take)/gather | solution.py:110
  38.6 0.2 reduce-window.16
  38.8 0.1 convert_reduce_fusion.2
  38.9 0.1 select_reduce_fusion.5
  39.0 0.1 select_reduce_fusion.4
  39.1 0.4 multiply_cosine_fusion
  39.6 0.1 all_to_all.14
  39.7 80.6 %all-to-all-done = bf16[8,384,1024]{1,2,0:T(8,128)(2,1)} async-done(((bf16[8,384,1024]{1,2,0:T(8,128)(2,1)}), bf16[8,384,1024]{1,2,0:T(8,128)(2,1)}, u32[]{:S(2)}, u32[]{:S(2)}) %all-to-all-start) | async-done | bytes 6291488 | tf_op jit(solution)/shard_map/all_to_all | solution.py:160
  120.3 4.4 %fusion.9 = f32[384]{0:T(512)S(1)} fusion(bf16[8,384,1024]{1,2,0:T(8,128)(2,1)} %all-to-all-done), kind=kLoop, calls=%fused_computation.16 | loop fusion | flops 9436800 | bytes 6292992 | tf_op jit(solution)/shard_map/reduce_sum | solution.py:176
  124.7 7.3 %fusion.11 = bf16[8,384,1024]{1,2,0:T(8,128)(2,1)} fusion(bf16[8,384,1024]{1,2,0:T(8,128)(2,1)} %all-to-all-done, f32[8,1024]{1,0:T(8,128)S(1)} %reshape.461, f32[384]{0:T(512)S(1)} %add_rsqrt_fusion), kind=kLoop, calls=%fused_computation.18 | loop fusion | flops 12582912 | bytes 12617216 | tf_op jit(solution)/shard_map/convert_element_type | solution.py:180
  132.0 67.5 %all-gather.3.cloned.1.call-done = bf16[8192,1344]{1,0:T(8,128)(2,1)} async-done(((bf16[512,1344]{1,0:T(8,128)(2,1)}), bf16[8192,1344]{1,0:T(8,128)(2,1)}) %all-gather.3.cloned.1.call-update) | async-done | bytes 22020112 | tf_op jit(solution)/shard_map/all_gather | solution.py:169
  199.5 17.4 %fusion.42 = f32[384,1344]{0,1:T(8,128)S(1)} fusion(bf16[384,8192]{0,1:T(8,128)(2,1)} %bitcast.67, bf16[8192,1344]{1,0:T(8,128)(2,1)} %all-gather.3.cloned.1.call-done), kind=kOutput, calls=%fused_computation.106 | convolution fusion | flops 8455716864 | bytes 30375936 | tf_op jit(solution)/shard_map/dot_general | solution.py:182
  216.9 0.1 fusion.24
  217.0 0.1 fusion.23
  217.1 0.9 pad_maximum_fusion.3
  218.1 0.1 select_reduce_fusion.2
  218.2 0.1 fusion.28
  218.3 0.1 convert_reduce_fusion
  218.4 0.1 broadcast_bitcast_fusion.1
  218.5 0.1 broadcast_bitcast_fusion
  218.6 0.1 fusion.27
  218.7 2.1 and_reduce_fusion
  220.7 1.2 compare_and_fusion
  221.9 0.8 copy.50
  222.7 0.8 copy.54
  223.6 1.6 slice_add_fusion
  225.2 1.3 fusion.40
  226.5 2.8 copy.62
  229.2 2.7 copy.63
  232.0 1.6 copy.51
  233.6 1.7 slice.55
  235.4 2.2 reshape.455
  237.6 1.5 fusion.41
  239.0 1.6 negate_bitcast_fusion
  240.7 1.5 fusion.20
  242.3 10.7 %fusion.3 = (f32[8,384]{1,0:T(8,128)S(1)}, f32[8,384,2048]{2,1,0:T(8,128)}) fusion(pred[384,2048]{1,0:T(8,128)(4,1)S(1)} %copy-done, bf16[8,384,128]{2,1,0:T(8,128)(2,1)S(1)} %fusion.20, bf16[2048,128,1]{1,0,2:T(8,128)(2,1)S(1)} %bitcast.68), kind=kOutput, calls=%fused_computation.9 | convolution fusion | flops 1629484032 | bytes 27275264 | tf_op jit(solution)/shard_map/kgqd,skd->kgqs/dot_general | solution.py:68
  252.9 1.3 all-gather.5.cloned.1.call-done
  254.2 0.1 copy.57
  254.3 0.1 reduce-window.17
  254.4 6.9 %all-to-all-start.2 = ((bf16[32,4,2,128,128]{4,3,2,1,0:T(8,128)(2,1)}), bf16[32,4,2,128,128]{4,3,2,1,0:T(8,128)(2,1)}, u32[]{:S(2)}, u32[]{:S(2)}) async-start(bf16[32,4,2,128,128]{4,3,2,1,0:T(8,128)(2,1)} %gather_fusion), calls=%async_computation.2 | async-start | bytes 16777216 | tf_op jit(solution)/shard_map/all_to_all | solution.py:122
  261.3 17.8 %fusion = (f32[8,384]{1,0:T(8,128)S(1)}, f32[8,384,3456]{2,1,0:T(8,128)}) fusion(pred[384,3456]{1,0:T(8,128)(4,1)S(1)} %compare_and_fusion, bf16[8,384,128]{2,1,0:T(8,128)(2,1)S(1)} %fusion.20, bf16[6144,256]{0,1:T(8,128)(2,1)} %all-gather.5.cloned.1.call-done, s32[]{:T(128)S(6)} %max.20), kind=kOutput, calls=%fused_computation.4 | convolution fusion | flops 2749756416 | bytes 45477892 | tf_op jit(solution)/shard_map/kgqd,skd->kgqs/dot_general | solution.py:68
  279.1 21.1 %fusion.1 = f32[8,384]{1,0:T(8,128)S(1)} fusion(f32[8,384,3456]{2,1,0:T(8,128)} %get-tuple-element.48, f32[8,384]{1,0:T(8,128)S(1)} %get-tuple-element.39, pred[384,3456]{1,0:T(8,128)(4,1)S(1)} %compare_and_fusion), kind=kLoop, calls=%fused_computation.5 | loop fusion | flops 53081088 | bytes 43819008 | tf_op jit(solution)/shard_map/reduce_sum | solution.py:76
  300.2 12.0 %fusion.7 = f32[8,384]{1,0:T(8,128)S(1)} fusion(f32[8,384,2048]{2,1,0:T(8,128)} %get-tuple-element.46, f32[8,384]{1,0:T(8,128)S(1)} %get-tuple-element.40, pred[384,2048]{1,0:T(8,128)(4,1)S(1)} %copy-done), kind=kLoop, calls=%fused_computation.12 | loop fusion | flops 31454208 | bytes 25976832 | tf_op jit(solution)/shard_map/reduce_sum | solution.py:76
  312.2 11.2 %fusion.12 = f32[8,384,128]{1,2,0:T(8,128)S(1)} fusion(bf16[2048,128,1]{1,0,2:T(8,128)(2,1)S(1)} %bitcast.70, f32[8,384,2048]{2,1,0:T(8,128)} %get-tuple-element.46, f32[8,384]{1,0:T(8,128)S(1)} %get-tuple-element.40, pred[384,2048]{1,0:T(8,128)(4,1)S(1)} %copy-done), kind=kOutput, calls=%fused_computation.19 | convolution fusion | flops 1642070016 | bytes 28061696 | tf_op jit(solution)/shard_map/kgqs,skd->kgqd/dot_general | solution.py:77
  323.4 18.4 %divide_convert_fusion = bf16[8,384,128]{1,2,0:T(8,128)(2,1)S(1)} fusion(f32[8,384,128]{1,2,0:T(8,128)S(1)} %fusion.12, f32[8,384,3456]{2,1,0:T(8,128)} %get-tuple-element.48, f32[8,384]{1,0:T(8,128)S(1)} %get-tuple-element.39, pred[384,3456]{1,0:T(8,128)(4,1)S(1)} %compare_and_fusion, bf16[6144,256]{0,1:T(8,128)(2,1)} %all-gather.5.cloned.1.call-done, ...), kind=kOutput, calls=%fused_computation.27 | convolution fusion | flops 2772959232 | bytes 47087624 | tf_op jit(solution)/shard_map/kgqs,skd->kgqd/dot_general | solution.py:77
  341.9 1.2 copy.58
  343.0 0.1 add_reduce_fusion
  343.1 0.1 select_reduce_fusion
  343.3 10.1 %all-to-all-done.2 = bf16[32,4,2,128,128]{4,3,2,1,0:T(8,128)(2,1)} async-done(((bf16[32,4,2,128,128]{4,3,2,1,0:T(8,128)(2,1)}), bf16[32,4,2,128,128]{4,3,2,1,0:T(8,128)(2,1)}, u32[]{:S(2)}, u32[]{:S(2)}) %all-to-all-start.2) | async-done | bytes 8388640 | tf_op jit(solution)/shard_map/all_to_all | solution.py:122
  353.4 6.5 %gather_fusion.1 = bf16[16,4,2,128,128]{4,3,2,1,0:T(8,128)(2,1)} fusion(bf16[32,4,2,128,128]{4,3,2,1,0:T(8,128)(2,1)} %all-to-all-done.2, s32[1024]{0:T(1024)S(1)} %pad_clamp_fusion), kind=kCustom, calls=%fused_computation.1 | custom fusion | bytes 8388672 | tf_op jit(solution)/shard_map/jit(_take)/gather | solution.py:129
  (49 shorter events, 0.3 us)
Async XLA Ops:
  7.2 192.3 %all-gather.3.cloned.1.call-start = ((), (), s32[]{:S(2)}) async-start(), calls=%async_computation.3 | async-start | bytes 24510464 | tf_op jit(solution)/shard_map/all_gather | solution.py:169
  13.1 8.6 %all-to-all-start.1 = ((bf16[16,2,1]{1,2,0:T(2,128)(2,1)}), bf16[16,2,1]{1,2,0:T(2,128)(2,1)S(1)}, u32[]{:S(2)}, u32[]{:S(2)}) async-start(bf16[16,2,1]{1,2,0:T(2,128)(2,1)} %reshape.485), calls=%async_computation.1 | async-start | bytes 16384 | tf_op jit(solution)/shard_map/all_to_all | solution.py:116
  24.9 6.2 %copy-start.4 = (bf16[8192]{0:T(1024)(128)(2,1)S(1)}, bf16[8192]{0:T(1024)(128)(2,1)}, u32[]{:S(2)}) copy-start(bf16[8192]{0:T(1024)(128)(2,1)} %param.17) | copy-start | bytes 49156
  24.9 6.3 %copy-start.10 = (bf16[128]{0:T(256)(128)(2,1)S(1)}, bf16[128]{0:T(256)(128)(2,1)}, u32[]{:S(2)}) copy-start(bf16[128]{0:T(256)(128)(2,1)} %param.22) | copy-start | bytes 772
  24.9 6.3 %copy-start.11 = (bf16[128]{0:T(256)(128)(2,1)S(1)}, bf16[128]{0:T(256)(128)(2,1)}, u32[]{:S(2)}) copy-start(bf16[128]{0:T(256)(128)(2,1)} %param.23) | copy-start | bytes 772
  24.9 6.3 %copy-start.8 = (s32[16,1]{0,1:T(1,128)S(1)}, s32[16,1]{0,1:T(1,128)}, u32[]{:S(2)}) copy-start(s32[16,1]{0,1:T(1,128)} %param.31) | copy-start | bytes 196
  24.9 95.4 %all-to-all-start = ((bf16[8,384,1024]{1,2,0:T(8,128)(2,1)}), bf16[8,384,1024]{1,2,0:T(8,128)(2,1)}, u32[]{:S(2)}, u32[]{:S(2)}) async-start(bf16[8,384,1024]{1,2,0:T(8,128)(2,1)} %broadcast_in_dim.181), calls=%async_computation | async-start | bytes 12582912 | tf_op jit(solution)/shard_map/all_to_all | solution.py:160
  31.0 223.2 %all-gather.5.cloned.1.call-start = ((), (), s32[]{:S(2)}) async-start(), calls=%async_computation.4 | async-start | bytes 3342336 | tf_op jit(solution)/shard_map/all_gather | solution.py:198
  31.3 7.3 %copy-start.12 = (s32[3]{0:T(128)S(1)}, s32[3]{0:T(128)}, u32[]{:S(2)}) copy-start(s32[3]{0:T(128)} %param.24) | copy-start | bytes 40
  31.3 7.6 %copy-start.9 = (s32[3]{0:T(128)S(1)}, s32[3]{0:T(128)}, u32[]{:S(2)}) copy-start(s32[3]{0:T(128)} %param.25) | copy-start | bytes 40
  31.3 7.7 %copy-start.6 = (s32[4]{0:T(128)S(1)}, s32[4]{0:T(128)}, u32[]{:S(2)}) copy-start(s32[4]{0:T(128)} %param.26) | copy-start | bytes 52
  132.0 86.1 %copy-start.7 = (bf16[1024]{0:T(1024)(128)(2,1)S(1)}, bf16[1024]{0:T(1024)(128)(2,1)}, u32[]{:S(2)}) copy-start(bf16[1024]{0:T(1024)(128)(2,1)} %param.21) | copy-start | bytes 6148
  132.0 86.1 %copy-start.5 = (s32[4,4]{1,0:T(4,128)S(1)}, s32[4,4]{1,0:T(4,128)}, u32[]{:S(2)}) copy-start(s32[4,4]{1,0:T(4,128)} %param.27) | copy-start | bytes 196
  216.8 1.8 copy-start.3
  237.6 3.1 copy-start.1
  237.6 3.1 copy-start.2
  237.6 4.7 %copy-start = (pred[384,2048]{1,0:T(8,128)(4,1)S(1)}, pred[384,2048]{1,0:T(8,128)(4,1)}, u32[]{:S(2)}) copy-start(pred[384,2048]{1,0:T(8,128)(4,1)} %and_reduce_fusion) | copy-start | bytes 2359300
  254.4 99.0 %all-to-all-start.2 = ((bf16[32,4,2,128,128]{4,3,2,1,0:T(8,128)(2,1)}), bf16[32,4,2,128,128]{4,3,2,1,0:T(8,128)(2,1)}, u32[]{:S(2)}, u32[]{:S(2)}) async-start(bf16[32,4,2,128,128]{4,3,2,1,0:T(8,128)(2,1)} %gather_fusion), calls=%async_computation.2 | async-start | bytes 16777216 | tf_op jit(solution)/shard_map/all_to_all | solution.py:122
Sparse Core Ops, SparseCore 0:
  10.8 188.5 all-gather.2
  218.2 36.0 all-gather.4
